TPU v7x, 256 devices: a whole 4x4x8 slice. The times are simulated.
256 devices in a mesh: ctx: 32 (over x, z_lo, y), head: 8 (over z_hi, core).
Axes of the slice: x: 4, y: 4, z: 8 (z_hi: 4, z_lo: 2; z = z_hi * 2 + z_lo), core: 2. Of those that a mesh axis runs over, the one named last changes fastest.
Arguments:
- tokens: bfloat16 [8192, 4096], P('ctx', 'head'), may hold values from -6 to 6
- cotangent: bfloat16 [8192, 4096], P('ctx', 'head'), may hold values from -0.1796875 to 0.1796875
- expert_ids: int32 [8192, 2], P('ctx'), may hold values from 0 to 31, all different within a row; in each aligned block of 256 rows (0 to 255, 256 to 511, ...) at most 24 rows name the same one
- w_router: bfloat16 [4096, 32], P('head'), may hold values from -0.09375 to 0.09375
- w_gate: bfloat16 [32, 1408, 4096], P('ctx', None, 'head'), may hold values from -0.09375 to 0.09375
- w_up: bfloat16 [32, 1408, 4096], P('ctx', None, 'head'), may hold values from -0.09375 to 0.09375
- w_down: bfloat16 [32, 1408, 4096], P('ctx', None, 'head'), may hold values from -0.15625 to 0.15625
Outputs:
- mixed: bfloat16 [8192, 4096], P('ctx', 'head')
- grad_tokens: bfloat16 [8192, 4096], P('ctx', 'head')
- grad_router: float32 [4096, 32], P('head')
- grad_gate: bfloat16 [32, 1408, 4096], P('ctx', None, 'head')
- grad_up: bfloat16 [32, 1408, 4096], P('ctx', None, 'head')
- grad_down: bfloat16 [32, 1408, 4096], P('ctx', None, 'head')
Inputs may be any that keep to these rules, and one draw needn't show every extreme that they name: `expert_ids`: each row names 2 different experts. Within the rows of one device (aligned blocks of 256 rows) no expert is named by more than 24 rows, a bound that some block reaches.
All inputs are finite; a program needn't handle non-finite values.
Results may differ from a plain program's by a relative error of at most 0.023.
Values may be sent and summed in bfloat16 or wider, within the bound.
No kernel may reach another device: no remote copies, remote signals or barrier semaphores. Data moves between devices by JAX's collectives and lax.ppermute only.
A program may use at most 64 MiB of HBM per device.

v0:
```python
import jax
import jax.numpy as jnp
from jax import lax
from jax.sharding import PartitionSpec as P


def contract_rows(left, right):
    return lax.dot_general(
        left, right, (((0,), (0,)), ((), ())), preferred_element_type=jnp.float32
    )


def contract_last(left, right):
    return lax.dot_general(
        left, right, (((1,), (1,)), ((), ())), preferred_element_type=jnp.float32
    )


def activations(gate_pre, up_pre, back_proj, prob_rows):
    sigma = jax.nn.sigmoid(gate_pre)
    active = gate_pre * sigma
    hidden = (active * up_pre).astype(jnp.bfloat16)
    hidden_grad = prob_rows[:, None] * back_proj
    gate_grad = (hidden_grad * up_pre * sigma * (1.0 + gate_pre * (1.0 - sigma))).astype(
        jnp.bfloat16
    )
    up_grad = (hidden_grad * active).astype(jnp.bfloat16)
    return (hidden, gate_grad, up_grad)


def local(tokens, cotangent, expert_ids, w_router, w_gate, w_up, w_down):
    ctx_count = lax.axis_size("ctx")
    tok_rows = tokens.shape[0]
    shard_width = tokens.shape[1]
    pick_count = expert_ids.shape[1]
    experts = w_router.shape[1]
    capacity = 3 * tok_rows * pick_count // (2 * experts)
    partial_logits = jnp.dot(tokens, w_router, preferred_element_type=jnp.float32)
    onehot = (expert_ids[:, :, None] == jnp.arange(experts, dtype=jnp.int32)[None, None, :]).astype(
        jnp.float32
    )
    chosen = lax.psum(jnp.sum(partial_logits[:, None, :] * onehot, axis=2), "head")
    prob_pairs = jnp.stack(
        [jax.nn.sigmoid(chosen[:, 0] - chosen[:, 1]), jax.nn.sigmoid(chosen[:, 1] - chosen[:, 0])],
        axis=1,
    )
    flat_ids = expert_ids.reshape(-1)
    id_hits = (flat_ids[:, None] == jnp.arange(experts, dtype=jnp.int32)[None, :]).astype(jnp.int32)
    places = jnp.sum((jnp.cumsum(id_hits, axis=0) - 1) * id_hits, axis=1)
    slot_index = flat_ids * capacity + places
    slot_table = (
        jnp.zeros((experts * capacity,), jnp.int32)
        .at[slot_index]
        .set(jnp.arange(tok_rows * pick_count, dtype=jnp.int32) + 1)
    )
    occupied = slot_table > 0
    source = jnp.maximum(slot_table - 1, 0)
    row_index = source // pick_count
    prob_send = jnp.where(occupied, prob_pairs.reshape(-1)[source], jnp.float32(0.0)).reshape(
        experts, capacity
    )

    def pack_rows(values):
        picked = jnp.where(occupied[:, None], values[row_index], jnp.zeros((), values.dtype))
        return picked.reshape(experts, capacity, values.shape[1])

    recv_x, recv_g, recv_p = (
        lax.all_to_all(pack_rows(tokens), "ctx", split_axis=0, concat_axis=0, tiled=True),
        lax.all_to_all(pack_rows(cotangent), "ctx", split_axis=0, concat_axis=0, tiled=True),
        lax.all_to_all(
            prob_send.astype(jnp.bfloat16), "ctx", split_axis=0, concat_axis=0, tiled=True
        ).astype(prob_send.dtype),
    )
    slot_count = recv_x.shape[0] * recv_x.shape[1]
    x_rows = recv_x.reshape(slot_count, shard_width)
    cot_rows = recv_g.reshape(slot_count, shard_width)
    prob_rows = recv_p.reshape(slot_count)
    gate_w = w_gate[0]
    up_w = w_up[0]
    down_w = w_down[0]
    gate_part = contract_last(x_rows, gate_w)
    up_part = contract_last(x_rows, up_w)
    back_part = contract_last(cot_rows, down_w)
    gate_pre, up_pre, back_proj = (
        lax.psum(gate_part.astype(jnp.bfloat16), "head").astype(jnp.float32),
        lax.psum(up_part.astype(jnp.bfloat16), "head").astype(jnp.float32),
        lax.psum(back_part.astype(jnp.bfloat16), "head").astype(jnp.float32),
    )
    hidden, gate_grad, up_grad = activations(gate_pre, up_pre, back_proj, prob_rows)
    out_rows = jnp.dot(hidden, down_w, preferred_element_type=jnp.float32).astype(jnp.bfloat16)
    dx_rows = (
        jnp.dot(gate_grad, gate_w, preferred_element_type=jnp.float32)
        + jnp.dot(up_grad, up_w, preferred_element_type=jnp.float32)
    ).astype(jnp.bfloat16)
    hidden_kept = lax.optimization_barrier(hidden)
    scaled = (prob_rows[:, None] * hidden_kept.astype(jnp.float32)).astype(jnp.bfloat16)
    grad_down = contract_rows(scaled, cot_rows).astype(jnp.bfloat16)[None]
    grad_gate = contract_rows(gate_grad, x_rows).astype(jnp.bfloat16)[None]
    grad_up = contract_rows(up_grad, x_rows).astype(jnp.bfloat16)[None]
    back_out, back_dx = (
        lax.all_to_all(
            out_rows.reshape(ctx_count, capacity, shard_width),
            "ctx",
            split_axis=0,
            concat_axis=0,
            tiled=True,
        ),
        lax.all_to_all(
            dx_rows.reshape(ctx_count, capacity, shard_width),
            "ctx",
            split_axis=0,
            concat_axis=0,
            tiled=True,
        ),
    )
    out_pairs = back_out.reshape(experts * capacity, shard_width)[slot_index].reshape(
        tok_rows, pick_count, shard_width
    )
    dx_pairs = back_dx.reshape(experts * capacity, shard_width)[slot_index].reshape(
        tok_rows, pick_count, shard_width
    )
    mixed = jnp.sum(prob_pairs[:, :, None] * out_pairs.astype(jnp.float32), axis=1).astype(
        jnp.bfloat16
    )
    score_part = jnp.sum(
        cotangent.astype(jnp.float32)[:, None, :] * out_pairs.astype(jnp.float32), axis=2
    )
    score_grad = lax.psum(score_part, "head")
    logit_lead = prob_pairs[:, 0] * prob_pairs[:, 1] * (score_grad[:, 0] - score_grad[:, 1])
    logit_grad = jnp.stack([logit_lead, -logit_lead], axis=1)
    dense_grad = jnp.sum(logit_grad[:, :, None] * onehot, axis=1)
    router_term = jnp.dot(
        dense_grad, w_router.astype(jnp.float32).T, precision=lax.Precision.HIGHEST
    )
    grad_tokens = (
        dx_pairs[:, 0].astype(jnp.float32) + dx_pairs[:, 1].astype(jnp.float32) + router_term
    ).astype(jnp.bfloat16)
    router_part = jnp.dot(tokens.astype(jnp.float32).T, dense_grad, precision=lax.Precision.HIGHEST)
    grad_router = lax.psum(router_part, "ctx")
    return (mixed, grad_tokens, grad_router, grad_gate, grad_up, grad_down)


def solution(mesh):
    placed = (
        P("ctx", "head"),
        P("ctx", "head"),
        P("ctx", None),
        P("head", None),
        P("ctx", None, "head"),
        P("ctx", None, "head"),
        P("ctx", None, "head"),
    )
    return jax.shard_map(
        local,
        mesh=mesh,
        in_specs=placed,
        out_specs=(
            P("ctx", "head"),
            P("ctx", "head"),
            P("head", None),
            P("ctx", None, "head"),
            P("ctx", None, "head"),
            P("ctx", None, "head"),
        ),
        check_vma=False,
    )
```

profile of v0, /device:TPU:64, one launch (start us, length us, event | category | flops | bytes accessed | tf_op | source)
XLA Modules:
  0.0 605.1 jit_solution(14181950294091375107)
XLA Ops:
  7.2 0.0 copy-start
  7.2 0.9 copy.53
  8.1 0.1 eq.45
  8.3 0.1 eq.41
  8.4 0.7 broadcast_multiply_fusion
  9.1 1.2 reduce-window.6
  10.3 0.2 slice_reduce_fusion
  10.6 0.1 copy.52
  10.7 0.1 mul.105
  10.9 0.1 fusion.28
  11.0 2.4 scatter_custom_fusion
  13.5 1.1 fusion.37
  14.6 0.7 select_reduce_fusion.1
  15.3 15.2 %psum.42 = f32[256,2]{0,1:T(2,128)S(1)} all-reduce(f32[256,2]{0,1:T(2,128)S(1)} %select_reduce_fusion.1), channel_id=1, replica_groups=mesh['ctx'=32,'head'=8] {'head'}, use_global_device_ids=true, to_apply=%region_1.0 | all-reduce | flops 512 | bytes 4096 | tf_op jit(solution)/shard_map/psum | solution.py:42
  30.6 0.1 copy.51
  30.7 0.1 reshape.144
  30.9 5.0 gather_fusion.2
  35.9 0.6 select_convert_fusion
  36.5 0.1 broadcast_in_dim.50
  36.6 2.7 gather_fusion
  39.3 2.7 gather_fusion.3
  42.0 1.1 broadcast_select_fusion
  43.1 20.9 %all_to_all.26 = bf16[32,24,512]{2,1,0:T(8,128)(2,1)S(1)} all-to-all(bf16[32,24,512]{2,1,0:T(8,128)(2,1)S(1)} %get-tuple-element.21), channel_id=1, replica_groups=mesh['ctx'=32,'head'=8] {'ctx'}, dimensions={0} | all-to-all | bytes 1572864 | tf_op jit(solution)/shard_map/all_to_all | solution.py:68
  64.0 4.4 all-to-all-start.3
  68.4 0.0 all-reduce.6.cloned.1.call-start
  68.4 2.8 convolution_convert_fusion.1
  71.2 2.8 convolution_convert_fusion.2
  74.0 6.5 %all-to-all-done.3 = bf16[32,24,512]{2,1,0:T(8,128)(2,1)S(1)} async-done(((bf16[32,24,512]{2,1,0:T(8,128)(2,1)}), bf16[32,24,512]{2,1,0:T(8,128)(2,1)S(1)}, u32[]{:S(2)}, u32[]{:S(2)}) %all-to-all-start.3) | async-done | bytes 786464 | tf_op jit(solution)/shard_map/all_to_all | solution.py:69
  80.6 4.4 convolution_convert_fusion
  85.0 0.0 all-reduce.6.cloned.1.call-update
  85.0 0.7 copy-done.16
  85.7 0.1 convert_element_type.137
  85.8 12.5 %all_to_all.27 = bf16[32,1,24]{2,1,0:T(2,128)(2,1)S(1)} all-to-all(bf16[32,1,24]{2,1,0:T(2,128)(2,1)S(1)} %convert_element_type.137), channel_id=1, replica_groups=mesh['ctx'=32,'head'=8] {'ctx'}, dimensions={0} | all-to-all | bytes 3072 | tf_op jit(solution)/shard_map/all_to_all | solution.py:70
  98.3 0.1 convert_reduce_fusion
  98.3 0.1 reshape.150
  98.4 137.6 %all-reduce.6.cloned.1.call-done = (bf16[768,1408]{1,0:T(8,128)(2,1)}, bf16[768,1408]{1,0:T(8,128)(2,1)}, bf16[768,1408]{1,0:T(8,128)(2,1)}) async-done(((bf16[768,1408]{1,0:T(8,128)(2,1)}, bf16[768,1408]{1,0:T(8,128)(2,1)}, bf16[768,1408]{1,0:T(8,128)(2,1)}), (bf16[768,1408]{1,0:T(8,128)(2,1)}, bf16[768,1408]{1,0:T(8,128)(2,1)}, bf16[768,1408]{1,0:T(8,128)(2,1)})) %all-reduce.6.cloned.1.call-update) | async-done | bytes 6488080 | tf_op jit(solution)/shard_map/psum | solution.py:86
  236.0 6.0 fusion.3
  242.1 1.4 fusion.15
  243.5 0.7 copy-done.6
  244.1 0.3 copy-done.18
  244.5 2.3 add_convert_fusion
  246.7 8.4 %all-to-all-start.4 = ((bf16[32,24,512]{2,1,0:T(8,128)(2,1)}), bf16[32,24,512]{2,1,0:T(8,128)(2,1)S(1)}, u32[]{:S(2)}, u32[]{:S(2)}) async-start(bf16[32,24,512]{2,1,0:T(8,128)(2,1)} %bitcast.12), calls=%async_computation.4 | async-start | bytes 1572864 | tf_op jit(solution)/shard_map/all_to_all | solution.py:108
  255.2 4.3 fusion.21
  259.5 8.7 %all-to-all-done.4 = bf16[32,24,512]{2,1,0:T(8,128)(2,1)S(1)} async-done(((bf16[32,24,512]{2,1,0:T(8,128)(2,1)}), bf16[32,24,512]{2,1,0:T(8,128)(2,1)S(1)}, u32[]{:S(2)}, u32[]{:S(2)}) %all-to-all-start.4) | async-done | bytes 786464 | tf_op jit(solution)/shard_map/all_to_all | solution.py:108
  268.1 4.8 all-to-all-start.1
  273.0 0.0 all-reduce.4.cloned.1.call-start
  273.0 0.9 convert_element_type.128
  273.9 0.7 pad_clamp_fusion.1
  274.6 4.3 fusion.8
  279.0 2.4 fusion.9
  281.4 2.5 fusion.10
  283.9 2.6 gather_fusion.4
  286.5 1.2 reshape.148
  287.8 1.7 fusion.36
  289.5 2.6 gather_fusion.1
  292.1 1.8 reshape.149
  293.9 3.8 multiply_reduce_fusion
  297.7 0.1 copy.60
  297.8 15.7 %psum.46 = f32[256,2]{0,1:T(2,128)S(1)} all-reduce(f32[256,2]{0,1:T(2,128)S(1)} %copy.60), channel_id=1, replica_groups=mesh['ctx'=32,'head'=8] {'head'}, use_global_device_ids=true, to_apply=%region_11.12 | all-reduce | flops 512 | bytes 4096 | tf_op jit(solution)/shard_map/psum | solution.py:128
  313.5 0.9 convolution_bitcast_fusion
  314.4 0.0 all-reduce.4.cloned.1.call-update
  314.4 2.2 fusion.26
  316.6 280.1 %all-reduce.4.cloned.1.call-done = f32[512,32]{0,1:T(8,128)} async-done(((f32[512,32]{0,1:T(8,128)}), f32[512,32]{0,1:T(8,128)}) %all-reduce.4.cloned.1.call-update) | async-done | bytes 65552 | tf_op jit(solution)/shard_map/psum | solution.py:139
  596.8 1.5 copy.71
  (47 shorter events, 0.2 us)
Async XLA Ops:
  7.2 61.2 %copy-start = (bf16[1,1408,512]{2,1,0:T(8,128)(2,1)S(1)}, bf16[1,1408,512]{2,1,0:T(8,128)(2,1)}, u32[]{:S(2)}) copy-start(bf16[1,1408,512]{2,1,0:T(8,128)(2,1)} %param.12) | copy-start | bytes 4325380
  7.2 29.4 %copy-start.1 = (bf16[256,512]{1,0:T(8,128)(2,1)S(1)}, bf16[256,512]{1,0:T(8,128)(2,1)}, u32[]{:S(2)}) copy-start(bf16[256,512]{1,0:T(8,128)(2,1)} %param.7) | copy-start | bytes 786436
  11.0 19.9 %copy-start.15 = (s32[512,1]{0,1:T(1,128)}, s32[512,1]{0,1:T(1,128)S(1)}, u32[]{:S(2)}) copy-start(s32[512,1]{0,1:T(1,128)S(1)} %compare_select_fusion) | copy-start | bytes 6148
  30.7 5.9 copy-start.7
  36.6 2.7 copy-start.2
  64.0 7.2 %copy-start.9 = (bf16[32,24,512]{2,1,0:T(8,128)(2,1)}, bf16[32,24,512]{2,1,0:T(8,128)(2,1)S(1)}, u32[]{:S(2)}) copy-start(bf16[32,24,512]{2,1,0:T(8,128)(2,1)S(1)} %all_to_all.26) | copy-start | bytes 2359300
  64.0 16.6 %all-to-all-start.3 = ((bf16[32,24,512]{2,1,0:T(8,128)(2,1)}), bf16[32,24,512]{2,1,0:T(8,128)(2,1)S(1)}, u32[]{:S(2)}, u32[]{:S(2)}) async-start(bf16[32,24,512]{2,1,0:T(8,128)(2,1)} %get-tuple-element.20), calls=%async_computation.3 | async-start | bytes 1572864 | tf_op jit(solution)/shard_map/all_to_all | solution.py:69
  68.4 167.7 %all-reduce.6.cloned.1.call-start = ((), (), s32[]{:S(2)}) async-start(), calls=%async_computation.6 | async-start | bytes 12976128 | tf_op jit(solution)/shard_map/psum | solution.py:86
  68.4 2.8 copy-start.17
  80.6 4.4 copy-start.11
  85.0 0.7 copy-start.16
  242.1 1.4 copy-start.4
  242.1 2.1 copy-start.6
  242.1 2.4 copy-start.18
  246.7 21.4 %all-to-all-start.4 = ((bf16[32,24,512]{2,1,0:T(8,128)(2,1)}), bf16[32,24,512]{2,1,0:T(8,128)(2,1)S(1)}, u32[]{:S(2)}, u32[]{:S(2)}) async-start(bf16[32,24,512]{2,1,0:T(8,128)(2,1)} %bitcast.12), calls=%async_computation.4 | async-start | bytes 1572864 | tf_op jit(solution)/shard_map/all_to_all | solution.py:108
  268.1 21.3 %all-to-all-start.1 = ((bf16[32,24,512]{2,1,0:T(8,128)(2,1)}), bf16[32,24,512]{2,1,0:T(8,128)(2,1)S(1)}, u32[]{:S(2)}, u32[]{:S(2)}) async-start(bf16[32,24,512]{2,1,0:T(8,128)(2,1)} %bitcast.81), calls=%async_computation.1 | async-start | bytes 1572864 | tf_op jit(solution)/shard_map/all_to_all | solution.py:101
  273.0 323.8 %all-reduce.4.cloned.1.call-start = ((), (), s32[]{:S(2)}) async-start(), calls=%async_computation.5 | async-start | bytes 131072 | tf_op jit(solution)/shard_map/psum | solution.py:139
  274.6 4.4 copy-start.5
  274.6 4.4 copy-start.10
  278.9 2.4 copy-start.3
  278.9 2.4 copy-start.12
  292.1 21.4 %copy-start.14 = (s32[256,2]{0,1:T(2,128)S(1)}, s32[256,2]{0,1:T(2,128)}, u32[]{:S(2)}) copy-start(s32[256,2]{0,1:T(2,128)} %param.9) | copy-start | bytes 6148
  292.1 22.3 %copy-start.8 = (bf16[256,1,512]{2,1,0:T(2,128)(2,1)S(1)}, bf16[256,1,512]{2,1,0:T(2,128)(2,1)}, u32[]{:S(2)}) copy-start(bf16[256,1,512]{2,1,0:T(2,128)(2,1)} %get-tuple-element.18) | copy-start | bytes 786436
  292.1 22.3 %copy-start.13 = (bf16[512,32]{0,1:T(8,128)(2,1)S(1)}, bf16[512,32]{0,1:T(8,128)(2,1)}, u32[]{:S(2)}) copy-start(bf16[512,32]{0,1:T(8,128)(2,1)} %param.10) | copy-start | bytes 98308
Sparse Core Ops, SparseCore 0:
  85.1 150.8 all-reduce.5
  314.5 282.1 all-reduce.3
where the time goes:
time: 606 us; the launch traced here: 605 us
  waiting for transfers between devices  433 us (71%)
  blocking collectives  64.3 us (11%)
  matrix products  31.5 us (5%)
  local copies, waits for them, and re-layouts  28.3 us (5%)
  starting transfers between devices  17.7 us (3%)
  other arithmetic  15.9 us (3%)
  between operations  14.4 us (2%)
    psum x1, waiting for transfers between devices, local(): grad_router = lax.psum(router_part, 'ctx')  280 us
    psum x1, waiting for transfers between devices, local(): lax.psum(up_part.astype(jnp.bfloat16), 'head').astype(jnp.float32)  138 us
    all_to_all x1, blocking collectives, local(): lax.all_to_all(pack_rows(tokens), 'ctx', split_axis=0, concat_axis=0, til...  20.9 us
    psum x1, blocking collectives, local(): score_grad = lax.psum(score_part, 'head')  15.7 us
    psum x1, blocking collectives, local(): lax.psum(jnp.sum(partial_logits[:, None, :] * onehot, axis=2), 'head')  15.2 us
    all_to_all x1, blocking collectives, local(): lax.all_to_all(prob_send.astype(jnp.bfloat16), 'ctx', split_axis=0, conca...  12.5 us
  transfers between devices with their start and end apart: 5, of which 4 were waited for; matrix products, arithmetic and copies ran while one was open for 5% of the time, Pallas kernels for 0%

commit v1 on v0

--- a/solution.py
+++ b/solution.py
@@ -28,6 +28,22 @@
     return (hidden, gate_grad, up_grad)
 
 
+def head_sum(part):
+    count = lax.axis_size("head")
+    spread = jnp.broadcast_to(part[None], (count,) + part.shape)
+    gathered = lax.all_to_all(spread, "head", split_axis=0, concat_axis=0, tiled=True)
+    return jnp.sum(gathered, axis=0)
+
+
+def ctx_sum(part):
+    count = lax.axis_size("ctx")
+    rows = part.shape[0]
+    pieces = part.reshape(count, rows // count, part.shape[1])
+    mine = jnp.sum(lax.all_to_all(pieces, "ctx", split_axis=0, concat_axis=0, tiled=True), axis=0)
+    spread = jnp.broadcast_to(mine[None], pieces.shape)
+    return lax.all_to_all(spread, "ctx", split_axis=0, concat_axis=0, tiled=True).reshape(part.shape)
+
+
 def local(tokens, cotangent, expert_ids, w_router, w_gate, w_up, w_down):
     ctx_count = lax.axis_size("ctx")
     tok_rows = tokens.shape[0]
@@ -39,7 +55,7 @@
     onehot = (expert_ids[:, :, None] == jnp.arange(experts, dtype=jnp.int32)[None, None, :]).astype(
         jnp.float32
     )
-    chosen = lax.psum(jnp.sum(partial_logits[:, None, :] * onehot, axis=2), "head")
+    chosen = head_sum(jnp.sum(partial_logits[:, None, :] * onehot, axis=2))
     prob_pairs = jnp.stack(
         [jax.nn.sigmoid(chosen[:, 0] - chosen[:, 1]), jax.nn.sigmoid(chosen[:, 1] - chosen[:, 0])],
         axis=1,
@@ -125,7 +141,7 @@
     score_part = jnp.sum(
         cotangent.astype(jnp.float32)[:, None, :] * out_pairs.astype(jnp.float32), axis=2
     )
-    score_grad = lax.psum(score_part, "head")
+    score_grad = head_sum(score_part)
     logit_lead = prob_pairs[:, 0] * prob_pairs[:, 1] * (score_grad[:, 0] - score_grad[:, 1])
     logit_grad = jnp.stack([logit_lead, -logit_lead], axis=1)
     dense_grad = jnp.sum(logit_grad[:, :, None] * onehot, axis=1)
@@ -136,7 +152,7 @@
         dx_pairs[:, 0].astype(jnp.float32) + dx_pairs[:, 1].astype(jnp.float32) + router_term
     ).astype(jnp.bfloat16)
     router_part = jnp.dot(tokens.astype(jnp.float32).T, dense_grad, precision=lax.Precision.HIGHEST)
-    grad_router = lax.psum(router_part, "ctx")
+    grad_router = ctx_sum(router_part)
     return (mixed, grad_tokens, grad_router, grad_gate, grad_up, grad_down)
 
 

time: 606 us -> 344 us (0.57)
  waiting for transfers between devices: 433 us -> 165 us
  blocking collectives: 64.3 us -> 33.8 us
  starting transfers between devices: 17.7 us -> 46.6 us
    psum x1 -> x0, waiting for transfers between devices: 280 us -> none  [local(): grad_router = lax.psum(router_part, 'ctx')]
    psum x2 -> x0, blocking collectives: 30.9 us -> none  [the longest x1 15.7 us: local(): score_grad = lax.psum(score_part, 'head')]
    all_to_all x0 -> x4, starting transfers between devices: none -> 28.3 us  [the longest x2 16.1 us: head_sum(): lax.all_to_all(spread, 'head', split_axis=0, concat_axis=0, tiled=True)]
    all_to_all x0 -> x4, waiting for transfers between devices: none -> 15.1 us  [the longest x1 7.74 us: ctx_sum(): lax.all_to_all(pieces, 'ctx', split_axis=0, concat_axis=0, tiled=True)]
    all_to_all x1, waiting for transfers between devices: 8.67 us -> 0.01 us  [local(): lax.all_to_all(dx_rows.reshape(ctx_count, capacity, shard_width), 'ctx',...]
    all_to_all x1, waiting for transfers between devices: 0.01 us -> 7 us  [local(): lax.all_to_all(out_rows.reshape(ctx_count, capacity, shard_width), 'ctx',...]
  transfers between devices with their start and end apart: 5 -> 8, of which waited for: 4 -> 5; matrix products, arithmetic and copies ran while one was open for 5% -> 15% of each run, Pallas kernels for 0% -> 0%
where the time goes in v1:
time: 344 us; the launch traced here: 342 us
  waiting for transfers between devices  165 us (48%)
  starting transfers between devices  46.6 us (14%)
  blocking collectives  33.8 us (10%)
  local copies, waits for them, and re-layouts  31.4 us (9%)
  matrix products  31.4 us (9%)
  other arithmetic  19.1 us (6%)
  between operations  14.5 us (4%)
    psum x1, waiting for transfers between devices, local(): lax.psum(up_part.astype(jnp.bfloat16), 'head').astype(jnp.float32)  137 us
    all_to_all x1, blocking collectives, local(): lax.all_to_all(pack_rows(tokens), 'ctx', split_axis=0, concat_axis=0, til...  21.4 us
    all_to_all x2, starting transfers between devices, head_sum(): lax.all_to_all(spread, 'head', split_axis=0, concat_axis=0, tiled=True)  16.1 us
    all_to_all x1, blocking collectives, local(): lax.all_to_all(prob_send.astype(jnp.bfloat16), 'ctx', split_axis=0, conca...  12.5 us
    dot_general x3, matrix products, contract_rows(): lax.dot_general(left, right, (((0,), (0,)), ((), ())), preferred_element_...  10.9 us
    dot_general x3, matrix products, contract_last(): lax.dot_general(left, right, (((1,), (1,)), ((), ())), preferred_element_...  9.78 us
    all_to_all x1, starting transfers between devices, local(): lax.all_to_all(out_rows.reshape(ctx_count, capacity, shard_width), 'ctx',...  8.66 us
    all_to_all x1, starting transfers between devices, ctx_sum(): lax.all_to_all(pieces, 'ctx', split_axis=0, concat_axis=0, tiled=True)  8.28 us
  transfers between devices with their start and end apart: 8, of which 5 were waited for; matrix products, arithmetic and copies ran while one was open for 15% of the time, Pallas kernels for 0%

profile of v1, /device:TPU:64, one launch (start us, length us, event | category | flops | bytes accessed | tf_op | source)
XLA Modules:
  0.0 341.5 jit_solution(5666756664481809394)
XLA Ops:
  7.2 1.2 fusion.37
  8.5 0.7 select_reduce_fusion.1
  9.2 0.6 broadcast_in_dim.38
  9.8 8.1 %all-to-all-start = ((f32[8,256,2]{1,2,0:T(2,128)}), f32[8,256,2]{1,2,0:T(2,128)S(1)}, u32[]{:S(2)}, u32[]{:S(2)}) async-start(f32[8,256,2]{1,2,0:T(2,128)} %broadcast_in_dim.38), calls=%async_computation | async-start | bytes 32768 | tf_op jit(solution)/shard_map/all_to_all | solution.py:34
  17.9 0.8 copy.56
  18.7 0.1 eq.45
  19.0 0.7 broadcast_multiply_fusion
  19.7 1.2 reduce-window.6
  20.9 0.2 slice_reduce_fusion
  21.1 0.1 copy.55
  21.3 0.1 mul.105
  21.6 2.4 scatter_custom_fusion
  24.0 0.6 pad_clamp_fusion
  24.6 0.6 copy-done.12
  25.2 2.7 gather_fusion
  27.9 2.8 gather_fusion.3
  30.8 0.6 reduce_sum.75
  31.4 0.8 add_divide_fusion.1
  32.2 0.5 copy-done.20
  32.7 0.8 copy.54
  33.5 1.0 reshape.154
  34.5 5.1 %gather_fusion.2 = bf16[768]{0:T(1024)(128)(2,1)S(1)} fusion(bf16[512]{0:T(512)(128)(2,1)S(1)} %reshape.154, s32[1024]{0:T(1024)} %get-tuple-element.50), kind=kCustom, calls=%fused_computation.2 | custom fusion | bytes 6144 | tf_op jit(solution)/shard_map/gather | solution.py:75
  39.7 0.6 select_convert_fusion
  40.2 0.8 broadcast_in_dim.39
  41.0 1.1 broadcast_select_fusion
  42.1 21.4 %all_to_all.46 = bf16[32,24,512]{2,1,0:T(8,128)(2,1)S(1)} all-to-all(bf16[32,24,512]{2,1,0:T(8,128)(2,1)S(1)} %get-tuple-element.45), channel_id=1, replica_groups=mesh['ctx'=32,'head'=8] {'ctx'}, dimensions={0} | all-to-all | bytes 1572864 | tf_op jit(solution)/shard_map/all_to_all | solution.py:84
  63.5 4.8 %all-to-all-start.4 = ((bf16[32,24,512]{2,1,0:T(8,128)(2,1)}), bf16[32,24,512]{2,1,0:T(8,128)(2,1)S(1)}, u32[]{:S(2)}, u32[]{:S(2)}) async-start(bf16[32,24,512]{2,1,0:T(8,128)(2,1)} %get-tuple-element.44), calls=%async_computation.4 | async-start | bytes 1572864 | tf_op jit(solution)/shard_map/all_to_all | solution.py:85
  68.4 4.2 %convolution_convert_fusion.1 = bf16[768,1408]{1,0:T(8,128)(2,1)} fusion(bf16[768,512]{1,0:T(8,128)(2,1)S(1)} %bitcast.79, bf16[1,1408,512]{2,1,0:T(8,128)(2,1)} %param.12), kind=kOutput, calls=%fused_computation.23 | convolution fusion | flops 1108377600 | bytes 4390912 | tf_op jit(solution)/shard_map/dot_general | solution.py:14
  72.6 2.8 convolution_convert_fusion.2
  75.4 6.1 %all-to-all-done.4 = bf16[32,24,512]{2,1,0:T(8,128)(2,1)S(1)} async-done(((bf16[32,24,512]{2,1,0:T(8,128)(2,1)}), bf16[32,24,512]{2,1,0:T(8,128)(2,1)S(1)}, u32[]{:S(2)}, u32[]{:S(2)}) %all-to-all-start.4) | async-done | bytes 786464 | tf_op jit(solution)/shard_map/all_to_all | solution.py:85
  81.4 2.8 convolution_convert_fusion
  84.3 12.5 %all_to_all.47 = bf16[32,1,24]{2,1,0:T(2,128)(2,1)S(1)} all-to-all(bf16[32,1,24]{2,1,0:T(2,128)(2,1)S(1)} %convert_element_type.137), channel_id=1, replica_groups=mesh['ctx'=32,'head'=8] {'ctx'}, dimensions={0} | all-to-all | bytes 3072 | tf_op jit(solution)/shard_map/all_to_all | solution.py:86
  97.0 136.5 %all-reduce.3.cloned.1.call-done = (bf16[768,1408]{1,0:T(8,128)(2,1)}, bf16[768,1408]{1,0:T(8,128)(2,1)}, bf16[768,1408]{1,0:T(8,128)(2,1)}) async-done(((bf16[768,1408]{1,0:T(8,128)(2,1)}, bf16[768,1408]{1,0:T(8,128)(2,1)}, bf16[768,1408]{1,0:T(8,128)(2,1)}), (bf16[768,1408]{1,0:T(8,128)(2,1)}, bf16[768,1408]{1,0:T(8,128)(2,1)}, bf16[768,1408]{1,0:T(8,128)(2,1)})) %all-reduce.3.cloned.1.call-update) | async-done | bytes 6488080 | tf_op jit(solution)/shard_map/psum | solution.py:102
  233.5 6.4 %fusion.3 = (bf16[768,1408]{1,0:T(8,128)(2,1)}, bf16[768,1408]{1,0:T(8,128)(2,1)}, bf16[768,1408]{1,0:T(8,128)(2,1)S(1)}) fusion(bf16[768,1408]{1,0:T(8,128)(2,1)} %get-tuple-element.32, bf16[768,1408]{1,0:T(8,128)(2,1)} %get-tuple-element.33, bf16[768,1408]{1,0:T(8,128)(2,1)} %get-tuple-element.34, f32[768]{0:T(1024)S(1)} %reshape.162), kind=kLoop, calls=%fused_computation.14 | loop fusion | flops 20545536 | bytes 12979200 | tf_op jit(solution)/shard_map/convert_element_type | solution.py:24
  239.9 2.3 fusion.21
  242.1 8.7 %all-to-all-start.2 = ((bf16[32,24,512]{2,1,0:T(8,128)(2,1)}), bf16[32,24,512]{2,1,0:T(8,128)(2,1)S(1)}, u32[]{:S(2)}, u32[]{:S(2)}) async-start(bf16[32,24,512]{2,1,0:T(8,128)(2,1)} %bitcast.8), calls=%async_computation.2 | async-start | bytes 1572864 | tf_op jit(solution)/shard_map/all_to_all | solution.py:117
  250.8 3.5 %fusion.15 = f32[768,512]{1,0:T(8,128)S(1)} fusion(bf16[768,1408]{1,0:T(8,128)(2,1)} %get-tuple-element.40, bf16[1,1408,512]{2,1,0:T(8,128)(2,1)} %param.12), kind=kOutput, calls=%fused_computation.36 | convolution fusion | flops 1107296256 | bytes 5177344 | tf_op jit(solution)/shard_map/dot_general | solution.py:109
  254.4 2.3 add_convert_fusion
  256.7 7.0 %all-to-all-done.2 = bf16[32,24,512]{2,1,0:T(8,128)(2,1)S(1)} async-done(((bf16[32,24,512]{2,1,0:T(8,128)(2,1)}), bf16[32,24,512]{2,1,0:T(8,128)(2,1)S(1)}, u32[]{:S(2)}, u32[]{:S(2)}) %all-to-all-start.2) | async-done | bytes 786464 | tf_op jit(solution)/shard_map/all_to_all | solution.py:117
  263.7 4.8 %all-to-all-start.5 = ((bf16[32,24,512]{2,1,0:T(8,128)(2,1)}), bf16[32,24,512]{2,1,0:T(8,128)(2,1)S(1)}, u32[]{:S(2)}, u32[]{:S(2)}) async-start(bf16[32,24,512]{2,1,0:T(8,128)(2,1)} %bitcast.85), calls=%async_computation.5 | async-start | bytes 1572864 | tf_op jit(solution)/shard_map/all_to_all | solution.py:124
  268.5 0.8 convert_element_type.128
  269.4 4.3 %fusion.8 = bf16[1,1408,512]{2,1,0:T(8,128)(2,1)} fusion(bf16[768,1408]{1,0:T(8,128)(2,1)} %get-tuple-element.39, bf16[768,512]{1,0:T(8,128)(2,1)} %bitcast.81), kind=kOutput, calls=%fused_computation.28 | convolution fusion | flops 1108017152 | bytes 4390912 | tf_op jit(solution)/shard_map/dot_general | solution.py:8
  273.7 2.5 fusion.10
  276.2 2.6 gather_fusion.1
  278.9 2.7 reshape.161
  281.6 4.0 %multiply_reduce_fusion = (f32[256,2]{1,0:T(8,128)S(1)}, bf16[256,512]{1,0:T(8,128)(2,1)}) fusion(f32[256,2,512]{2,1,0:T(2,128)} %reshape.161, f32[256,512]{1,0:T(8,128)} %convert_element_type.128, f32[256,2]{1,0:T(8,128)S(1)} %copy-done.6), kind=kLoop, calls=%fused_computation.46 | loop fusion | flops 916992 | bytes 1839104 | tf_op jit(solution)/shard_map/reduce_sum | solution.py:141
  285.7 0.6 broadcast_in_dim.75
  286.3 8.0 %all-to-all-start.6 = ((f32[8,256,2]{1,2,0:T(2,128)}), f32[8,256,2]{1,2,0:T(2,128)S(1)}, u32[]{:S(2)}, u32[]{:S(2)}) async-start(f32[8,256,2]{1,2,0:T(2,128)} %broadcast_in_dim.75), calls=%async_computation.6 | async-start | bytes 32768 | tf_op jit(solution)/shard_map/all_to_all | solution.py:34
  294.3 4.0 %fusion.9 = bf16[1,1408,512]{2,1,0:T(8,128)(2,1)} fusion(bf16[768,1408]{1,0:T(8,128)(2,1)} %get-tuple-element.40, bf16[768,512]{1,0:T(8,128)(2,1)S(1)} %bitcast.82), kind=kOutput, calls=%fused_computation.29 | convolution fusion | flops 1108017152 | bytes 4390912 | tf_op jit(solution)/shard_map/dot_general | solution.py:8
  298.3 2.0 gather_fusion.4
  300.3 0.2 reshape.158
  300.6 0.2 convolution_bitcast_fusion
  301.0 0.8 reshape.224
  301.8 8.3 %all-to-all-start.7 = ((f32[32,1,512]{2,1,0:T(1,128)}), f32[32,1,512]{2,1,0:T(1,128)S(1)}, u32[]{:S(2)}, u32[]{:S(2)}) async-start(f32[32,1,512]{2,1,0:T(1,128)} %reshape.224), calls=%async_computation.7 | async-start | bytes 131072 | tf_op jit(solution)/shard_map/all_to_all | solution.py:42
  310.1 0.7 fusion.36
  310.8 7.7 %all-to-all-done.7 = f32[32,1,512]{2,1,0:T(1,128)S(1)} async-done(((f32[32,1,512]{2,1,0:T(1,128)}), f32[32,1,512]{2,1,0:T(1,128)S(1)}, u32[]{:S(2)}, u32[]{:S(2)}) %all-to-all-start.7) | async-done | bytes 65568 | tf_op jit(solution)/shard_map/all_to_all | solution.py:42
  318.6 0.5 broadcast.167
  319.1 0.7 reduce.10
  320.0 0.8 reshape.226
  320.8 3.9 %all-to-all-start.8 = ((f32[32,1,512]{2,1,0:T(1,128)}), f32[32,1,512]{2,1,0:T(1,128)S(1)}, u32[]{:S(2)}, u32[]{:S(2)}) async-start(f32[32,1,512]{2,1,0:T(1,128)} %reshape.226), calls=%async_computation.8 | async-start | bytes 131072 | tf_op jit(solution)/shard_map/all_to_all | solution.py:44
  324.7 1.1 fusion.26
  325.8 7.3 %all-to-all-done.8 = f32[32,1,512]{2,1,0:T(1,128)S(1)} async-done(((f32[32,1,512]{2,1,0:T(1,128)}), f32[32,1,512]{2,1,0:T(1,128)S(1)}, u32[]{:S(2)}, u32[]{:S(2)}) %all-to-all-start.8) | async-done | bytes 65568 | tf_op jit(solution)/shard_map/all_to_all | solution.py:44
  333.1 0.7 reduce.11
  334.0 0.7 copy.65
  (78 shorter events, 1.3 us)
Async XLA Ops:
  7.2 74.3 %copy-start = (bf16[1,1408,512]{2,1,0:T(8,128)(2,1)S(1)}, bf16[1,1408,512]{2,1,0:T(8,128)(2,1)}, u32[]{:S(2)}) copy-start(bf16[1,1408,512]{2,1,0:T(8,128)(2,1)} %param.13) | copy-start | bytes 4325380
  7.2 18.1 %copy-start.1 = (bf16[256,512]{1,0:T(8,128)(2,1)S(1)}, bf16[256,512]{1,0:T(8,128)(2,1)}, u32[]{:S(2)}) copy-start(bf16[256,512]{1,0:T(8,128)(2,1)} %param.7) | copy-start | bytes 786436
  9.8 21.0 %all-to-all-start = ((f32[8,256,2]{1,2,0:T(2,128)}), f32[8,256,2]{1,2,0:T(2,128)S(1)}, u32[]{:S(2)}, u32[]{:S(2)}) async-start(f32[8,256,2]{1,2,0:T(2,128)} %broadcast_in_dim.38), calls=%async_computation | async-start | bytes 32768 | tf_op jit(solution)/shard_map/all_to_all | solution.py:34
  21.5 3.1 copy-start.22
  24.0 0.6 copy-start.13
  24.6 0.6 copy-start.12
  25.2 2.7 copy-start.2
  31.4 8.3 %copy-start.14 = (s32[768]{0:T(1024)S(1)}, s32[768]{0:T(1024)}, u32[]{:S(2)}) copy-start(s32[768]{0:T(1024)} %copy-done.13) | copy-start | bytes 9220
  32.1 0.5 copy-start.20
  32.1 0.5 copy-start.18
  63.5 9.1 %copy-start.7 = (bf16[32,24,512]{2,1,0:T(8,128)(2,1)}, bf16[32,24,512]{2,1,0:T(8,128)(2,1)S(1)}, u32[]{:S(2)}) copy-start(bf16[32,24,512]{2,1,0:T(8,128)(2,1)S(1)} %all_to_all.46) | copy-start | bytes 2359300
  63.5 18.0 %all-to-all-start.4 = ((bf16[32,24,512]{2,1,0:T(8,128)(2,1)}), bf16[32,24,512]{2,1,0:T(8,128)(2,1)S(1)}, u32[]{:S(2)}, u32[]{:S(2)}) async-start(bf16[32,24,512]{2,1,0:T(8,128)(2,1)} %get-tuple-element.44), calls=%async_computation.4 | async-start | bytes 1572864 | tf_op jit(solution)/shard_map/all_to_all | solution.py:85
  68.3 165.2 %all-reduce.3.cloned.1.call-start = ((), (), s32[]{:S(2)}) async-start(), calls=%async_computation.9 | async-start | bytes 12976128 | tf_op jit(solution)/shard_map/psum | solution.py:102
  68.3 4.3 %copy-start.24 = (bf16[1,1408,512]{2,1,0:T(8,128)(2,1)S(1)}, bf16[1,1408,512]{2,1,0:T(8,128)(2,1)}, u32[]{:S(2)}) copy-start(bf16[1,1408,512]{2,1,0:T(8,128)(2,1)} %param.11) | copy-start | bytes 4325380
  81.4 2.8 copy-start.9
  239.8 2.3 copy-start.3
  242.1 21.5 %all-to-all-start.2 = ((bf16[32,24,512]{2,1,0:T(8,128)(2,1)}), bf16[32,24,512]{2,1,0:T(8,128)(2,1)S(1)}, u32[]{:S(2)}, u32[]{:S(2)}) async-start(bf16[32,24,512]{2,1,0:T(8,128)(2,1)} %bitcast.8), calls=%async_computation.2 | async-start | bytes 1572864 | tf_op jit(solution)/shard_map/all_to_all | solution.py:117
  250.8 3.6 %copy-start.5 = (bf16[768,1408]{1,0:T(8,128)(2,1)S(1)}, bf16[768,1408]{1,0:T(8,128)(2,1)}, u32[]{:S(2)}) copy-start(bf16[768,1408]{1,0:T(8,128)(2,1)} %get-tuple-element.39) | copy-start | bytes 6488068
  250.8 3.6 %copy-start.25 = (bf16[1,1408,512]{2,1,0:T(8,128)(2,1)S(1)}, bf16[1,1408,512]{2,1,0:T(8,128)(2,1)}, u32[]{:S(2)}) copy-start(bf16[1,1408,512]{2,1,0:T(8,128)(2,1)} %param.11) | copy-start | bytes 4325380
  256.7 12.7 %copy-start.23 = (s32[512,1]{0,1:T(1,128)S(1)}, s32[512,1]{0,1:T(1,128)}, u32[]{:S(2)}) copy-start(s32[512,1]{0,1:T(1,128)} %copy-done.22) | copy-start | bytes 6148
  263.7 22.0 %all-to-all-start.5 = ((bf16[32,24,512]{2,1,0:T(8,128)(2,1)}), bf16[32,24,512]{2,1,0:T(8,128)(2,1)S(1)}, u32[]{:S(2)}, u32[]{:S(2)}) async-start(bf16[32,24,512]{2,1,0:T(8,128)(2,1)} %bitcast.85), calls=%async_computation.5 | async-start | bytes 1572864 | tf_op jit(solution)/shard_map/all_to_all | solution.py:124
  269.3 6.9 %copy-start.16 = (s32[1024]{0:T(1024)}, s32[1024]{0:T(1024)S(1)}, u32[]{:S(2)}) copy-start(s32[1024]{0:T(1024)S(1)} %pad_clamp_fusion.1) | copy-start | bytes 12292
  269.3 4.4 %copy-start.4 = (bf16[768,1408]{1,0:T(8,128)(2,1)S(1)}, bf16[768,1408]{1,0:T(8,128)(2,1)}, u32[]{:S(2)}) copy-start(bf16[768,1408]{1,0:T(8,128)(2,1)} %copy-done.3) | copy-start | bytes 6488068
  269.4 4.4 %copy-start.10 = (bf16[32,24,512]{2,1,0:T(8,128)(2,1)S(1)}, bf16[32,24,512]{2,1,0:T(8,128)(2,1)}, u32[]{:S(2)}) copy-start(bf16[32,24,512]{2,1,0:T(8,128)(2,1)} %copy-done.9) | copy-start | bytes 2359300
  276.2 5.4 %copy-start.6 = (f32[256,2]{1,0:T(8,128)S(1)}, f32[256,2]{1,0:T(8,128)}, u32[]{:S(2)}) copy-start(f32[256,2]{1,0:T(8,128)} %copy.54) | copy-start | bytes 6148
  278.9 15.4 %copy-start.8 = (bf16[32,24,512]{2,1,0:T(8,128)(2,1)S(1)}, bf16[32,24,512]{2,1,0:T(8,128)(2,1)}, u32[]{:S(2)}) copy-start(bf16[32,24,512]{2,1,0:T(8,128)(2,1)} %copy-done.7) | copy-start | bytes 2359300
  286.3 14.2 %all-to-all-start.6 = ((f32[8,256,2]{1,2,0:T(2,128)}), f32[8,256,2]{1,2,0:T(2,128)S(1)}, u32[]{:S(2)}, u32[]{:S(2)}) async-start(f32[8,256,2]{1,2,0:T(2,128)} %broadcast_in_dim.75), calls=%async_computation.6 | async-start | bytes 32768 | tf_op jit(solution)/shard_map/all_to_all | solution.py:34
  294.3 4.0 %copy-start.17 = (s32[1024]{0:T(1024)S(1)}, s32[1024]{0:T(1024)}, u32[]{:S(2)}) copy-start(s32[1024]{0:T(1024)} %copy-done.16) | copy-start | bytes 12292
  298.3 2.2 copy-start.19
  298.3 2.2 copy-start.21
  298.3 2.3 copy-start.15
  300.9 23.8 %copy-start.11 = (bf16[512,32]{0,1:T(8,128)(2,1)S(1)}, bf16[512,32]{0,1:T(8,128)(2,1)}, u32[]{:S(2)}) copy-start(bf16[512,32]{0,1:T(8,128)(2,1)} %param.10) | copy-start | bytes 98308
  301.8 16.8 %all-to-all-start.7 = ((f32[32,1,512]{2,1,0:T(1,128)}), f32[32,1,512]{2,1,0:T(1,128)S(1)}, u32[]{:S(2)}, u32[]{:S(2)}) async-start(f32[32,1,512]{2,1,0:T(1,128)} %reshape.224), calls=%async_computation.7 | async-start | bytes 131072 | tf_op jit(solution)/shard_map/all_to_all | solution.py:42
  320.8 12.3 %all-to-all-start.8 = ((f32[32,1,512]{2,1,0:T(1,128)}), f32[32,1,512]{2,1,0:T(1,128)S(1)}, u32[]{:S(2)}, u32[]{:S(2)}) async-start(f32[32,1,512]{2,1,0:T(1,128)} %reshape.226), calls=%async_computation.8 | async-start | bytes 131072 | tf_op jit(solution)/shard_map/all_to_all | solution.py:44
Sparse Core Ops, SparseCore 0:
  84.4 149.0 all-reduce.2

commit v2 on v1

--- a/solution.py
+++ b/solution.py
@@ -16,16 +16,21 @@
     )
 
 
-def activations(gate_pre, up_pre, back_proj, prob_rows):
+def forward_act(gate_pre, up_pre):
     sigma = jax.nn.sigmoid(gate_pre)
     active = gate_pre * sigma
-    hidden = (active * up_pre).astype(jnp.bfloat16)
+    return (active * up_pre).astype(jnp.bfloat16)
+
+
+def backward_act(gate_pre, up_pre, back_proj, prob_rows):
+    sigma = jax.nn.sigmoid(gate_pre)
+    active = gate_pre * sigma
     hidden_grad = prob_rows[:, None] * back_proj
     gate_grad = (hidden_grad * up_pre * sigma * (1.0 + gate_pre * (1.0 - sigma))).astype(
         jnp.bfloat16
     )
     up_grad = (hidden_grad * active).astype(jnp.bfloat16)
-    return (hidden, gate_grad, up_grad)
+    return (gate_grad, up_grad)
 
 
 def head_sum(part):
@@ -80,30 +85,34 @@
         picked = jnp.where(occupied[:, None], values[row_index], jnp.zeros((), values.dtype))
         return picked.reshape(experts, capacity, values.shape[1])
 
-    recv_x, recv_g, recv_p = (
-        lax.all_to_all(pack_rows(tokens), "ctx", split_axis=0, concat_axis=0, tiled=True),
-        lax.all_to_all(pack_rows(cotangent), "ctx", split_axis=0, concat_axis=0, tiled=True),
-        lax.all_to_all(
-            prob_send.astype(jnp.bfloat16), "ctx", split_axis=0, concat_axis=0, tiled=True
-        ).astype(prob_send.dtype),
+    pad = jnp.zeros((experts, capacity, 128), jnp.bfloat16)
+    cot_pack = jnp.concatenate(
+        [pack_rows(cotangent), pad.at[:, :, 0].set(prob_send.astype(jnp.bfloat16))], axis=2
     )
+    recv_x = lax.all_to_all(pack_rows(tokens), "ctx", split_axis=0, concat_axis=0, tiled=True)
+    recv_g = lax.all_to_all(cot_pack, "ctx", split_axis=0, concat_axis=0, tiled=True)
     slot_count = recv_x.shape[0] * recv_x.shape[1]
     x_rows = recv_x.reshape(slot_count, shard_width)
-    cot_rows = recv_g.reshape(slot_count, shard_width)
-    prob_rows = recv_p.reshape(slot_count)
+    cot_rows = recv_g[:, :, :shard_width].reshape(slot_count, shard_width)
+    prob_rows = recv_g[:, :, shard_width].reshape(slot_count).astype(jnp.float32)
     gate_w = w_gate[0]
     up_w = w_up[0]
     down_w = w_down[0]
-    gate_part = contract_last(x_rows, gate_w)
-    up_part = contract_last(x_rows, up_w)
-    back_part = contract_last(cot_rows, down_w)
-    gate_pre, up_pre, back_proj = (
-        lax.psum(gate_part.astype(jnp.bfloat16), "head").astype(jnp.float32),
-        lax.psum(up_part.astype(jnp.bfloat16), "head").astype(jnp.float32),
-        lax.psum(back_part.astype(jnp.bfloat16), "head").astype(jnp.float32),
+    gate_part = contract_last(x_rows, gate_w).astype(jnp.bfloat16)
+    up_part = contract_last(x_rows, up_w).astype(jnp.bfloat16)
+    gate_sum, up_sum = lax.psum((gate_part, up_part), "head")
+    back_part = contract_last(cot_rows, down_w).astype(jnp.bfloat16)
+    back_part, gate_sum, up_sum = lax.optimization_barrier((back_part, gate_sum, up_sum))
+    back_sum = lax.psum(back_part, "head")
+    hidden = forward_act(gate_sum.astype(jnp.float32), up_sum.astype(jnp.float32))
+    out_rows = jnp.dot(hidden, down_w, preferred_element_type=jnp.float32).astype(jnp.bfloat16)
+    gate_late, up_late, back_sum = lax.optimization_barrier((gate_sum, up_sum, back_sum))
+    gate_grad, up_grad = backward_act(
+        gate_late.astype(jnp.float32),
+        up_late.astype(jnp.float32),
+        back_sum.astype(jnp.float32),
+        prob_rows,
     )
-    hidden, gate_grad, up_grad = activations(gate_pre, up_pre, back_proj, prob_rows)
-    out_rows = jnp.dot(hidden, down_w, preferred_element_type=jnp.float32).astype(jnp.bfloat16)
     dx_rows = (
         jnp.dot(gate_grad, gate_w, preferred_element_type=jnp.float32)
         + jnp.dot(up_grad, up_w, preferred_element_type=jnp.float32)

time: 344 us -> 341 us (level)
  blocking collectives: 33.8 us -> 61.8 us
  waiting for transfers between devices: 165 us -> 144 us
  starting transfers between devices: 46.6 us -> 32.3 us
  other arithmetic: 19.1 us -> 22.8 us
  matrix products: 31.4 us -> 27.9 us
    all_to_all x1 -> x2, blocking collectives: 12.5 us -> 40.5 us  [the longest x1 27.5 us: local(): lax.all_to_all(cot_pack, 'ctx', split_axis=0, concat_axis=0, tiled=True)]
    psum x1 -> x2, waiting for transfers between devices: 137 us -> 124 us  [the longest x1 87.6 us: local(): gate_sum, up_sum = lax.psum((gate_part, up_part), 'head')]
    all_to_all x2 -> x1, starting transfers between devices: 16.1 us -> 8.11 us  [head_sum(): lax.all_to_all(spread, 'head', split_axis=0, concat_axis=0, tiled=True)]
    all_to_all x1, waiting for transfers between devices: 7.33 us -> 0.01 us  [ctx_sum(): lax.all_to_all(spread, 'ctx', split_axis=0, concat_axis=0, tiled=True)]
    all_to_all x1 -> x0, waiting for transfers between devices: 6.06 us -> none  [local(): lax.all_to_all(pack_rows(cotangent), 'ctx', split_axis=0, concat_axis=0,...]
    all_to_all x1 -> x0, starting transfers between devices: 4.83 us -> none  [local(): lax.all_to_all(pack_rows(cotangent), 'ctx', split_axis=0, concat_axis=0,...]
    all_to_all x1, waiting for transfers between devices: 7 us -> 11.5 us  [local(): lax.all_to_all(out_rows.reshape(ctx_count, capacity, shard_width), 'ctx',...]
    unnamed x58 -> x56, local copies, waits for them, and re-layouts: 4.59 us -> 7.69 us
  transfers between devices with their start and end apart: 8 -> 7, of which waited for: 5 -> 5; matrix products, arithmetic and copies ran while one was open for 15% -> 14% of each run, Pallas kernels for 0% -> 0%
where the time goes in v2:
time: 341 us; the launch traced here: 337 us
  waiting for transfers between devices  144 us (42%)
  blocking collectives  61.8 us (18%)
  local copies, waits for them, and re-layouts  33.2 us (10%)
  starting transfers between devices  32.3 us (9%)
  matrix products  27.9 us (8%)
  other arithmetic  22.8 us (7%)
  between operations  14.5 us (4%)
    psum x1, waiting for transfers between devices, local(): gate_sum, up_sum = lax.psum((gate_part, up_part), 'head')  87.6 us
    psum x1, waiting for transfers between devices, local(): back_sum = lax.psum(back_part, 'head')  36.1 us
    all_to_all x1, blocking collectives, local(): lax.all_to_all(cot_pack, 'ctx', split_axis=0, concat_axis=0, tiled=True)  27.5 us
    all_to_all x1, blocking collectives, local(): lax.all_to_all(pack_rows(tokens), 'ctx', split_axis=0, concat_axis=0, til...  21.4 us
    all_to_all x1, blocking collectives, head_sum(): lax.all_to_all(spread, 'head', split_axis=0, concat_axis=0, tiled=True)  13 us
    all_to_all x1, waiting for transfers between devices, local(): lax.all_to_all(out_rows.reshape(ctx_count, capacity, shard_width), 'ctx',...  11.5 us
    dot_general x3, matrix products, contract_rows(): lax.dot_general(left, right, (((0,), (0,)), ((), ())), preferred_element_...  11 us
    dot_general x3, matrix products, contract_last(): lax.dot_general(left, right, (((1,), (1,)), ((), ())), preferred_element_...  8.42 us
  transfers between devices with their start and end apart: 7, of which 5 were waited for; matrix products, arithmetic and copies ran while one was open for 14% of the time, Pallas kernels for 0%

profile of v2, /device:TPU:64, one launch (start us, length us, event | category | flops | bytes accessed | tf_op | source)
XLA Modules:
  0.0 336.5 jit_solution(622979481300973113)
XLA Ops:
  7.2 1.2 fusion.44
  8.5 0.7 select_reduce_fusion.1
  9.2 0.6 broadcast_in_dim.38
  9.8 8.1 %all-to-all-start = ((f32[8,256,2]{1,2,0:T(2,128)}), f32[8,256,2]{1,2,0:T(2,128)S(1)}, u32[]{:S(2)}, u32[]{:S(2)}) async-start(f32[8,256,2]{1,2,0:T(2,128)} %broadcast_in_dim.38), calls=%async_computation | async-start | bytes 32768 | tf_op jit(solution)/shard_map/all_to_all | solution.py:39
  17.9 0.8 copy.69
  19.0 0.7 broadcast_multiply_fusion
  19.7 1.2 reduce-window.6
  21.6 2.4 scatter_custom_fusion
  24.0 0.6 pad_clamp_fusion.1
  24.6 0.6 copy-done.14
  25.2 2.7 gather_fusion.2
  27.9 2.8 gather_fusion
  30.8 0.6 reduce_sum.75
  31.4 0.8 add_divide_fusion.1
  32.2 0.8 copy.67
  33.0 1.0 reshape.178
  34.0 6.8 %gather_fusion.1 = bf16[768]{0:T(1024)(128)(2,1)} fusion(bf16[512]{0:T(512)(128)(2,1)S(1)} %reshape.178, s32[1024]{0:T(1024)} %get-tuple-element.78), kind=kCustom, calls=%fused_computation.1 | custom fusion | bytes 6144 | tf_op jit(solution)/shard_map/gather | solution.py:80
  40.8 1.3 select_convert_fusion
  42.1 0.8 broadcast_in_dim.39
  42.9 1.1 broadcast_select_fusion
  44.0 21.4 %all_to_all.40 = bf16[32,24,512]{2,1,0:T(8,128)(2,1)S(1)} all-to-all(bf16[32,24,512]{2,1,0:T(8,128)(2,1)S(1)} %get-tuple-element.72), channel_id=1, replica_groups=mesh['ctx'=32,'head'=8] {'ctx'}, dimensions={0} | all-to-all | bytes 1572864 | tf_op jit(solution)/shard_map/all_to_all | solution.py:92
  65.3 2.8 convolution_convert_fusion
  68.2 2.8 convolution_convert_fusion.1
  71.0 0.7 copy-done.18
  71.6 0.3 convert_element_type.143
  72.2 27.5 %all_to_all.41 = bf16[32,24,640]{2,1,0:T(8,128)(2,1)S(1)} all-to-all(bf16[32,24,640]{2,1,0:T(8,128)(2,1)S(1)} %fusion.33), channel_id=1, replica_groups=mesh['ctx'=32,'head'=8] {'ctx'}, dimensions={0} | all-to-all | bytes 1966080 | tf_op jit(solution)/shard_map/all_to_all | solution.py:93
  99.6 0.9 copy-done.3
  100.7 0.9 copy-done.12
  101.5 2.8 convolution_convert_fusion.2
  104.3 87.6 %all-reduce.7.cloned.1.call-done = (bf16[768,1408]{1,0:T(8,128)(2,1)}, bf16[768,1408]{1,0:T(8,128)(2,1)}) async-done(((bf16[768,1408]{1,0:T(8,128)(2,1)}, bf16[768,1408]{1,0:T(8,128)(2,1)}), (bf16[768,1408]{1,0:T(8,128)(2,1)}, bf16[768,1408]{1,0:T(8,128)(2,1)})) %all-reduce.7.cloned.1.call-update) | async-done | bytes 4325392 | tf_op jit(solution)/shard_map/psum | solution.py:103
  191.9 3.6 %fusion.12 = bf16[768,1408]{1,0:T(8,128)(2,1)S(1)} fusion(bf16[768,1408]{1,0:T(8,128)(2,1)} %get-tuple-element.28, bf16[768,1408]{1,0:T(8,128)(2,1)} %get-tuple-element.29), kind=kLoop, calls=%fused_computation.25 | loop fusion | flops 8650752 | bytes 6488064 | tf_op jit(solution)/shard_map/convert_element_type | solution.py:22
  195.5 2.3 fusion.27
  197.8 7.5 %all-to-all-start.3 = ((bf16[32,24,512]{2,1,0:T(8,128)(2,1)}), bf16[32,24,512]{2,1,0:T(8,128)(2,1)S(1)}, u32[]{:S(2)}, u32[]{:S(2)}) async-start(bf16[32,24,512]{2,1,0:T(8,128)(2,1)} %bitcast.10), calls=%async_computation.3 | async-start | bytes 1572864 | tf_op jit(solution)/shard_map/all_to_all | solution.py:126
  205.5 0.5 all-reduce.5.cloned.1.call-update
  206.0 0.8 convert_element_type.134
  206.9 11.5 %all-to-all-done.3 = bf16[32,24,512]{2,1,0:T(8,128)(2,1)S(1)} async-done(((bf16[32,24,512]{2,1,0:T(8,128)(2,1)}), bf16[32,24,512]{2,1,0:T(8,128)(2,1)S(1)}, u32[]{:S(2)}, u32[]{:S(2)}) %all-to-all-start.3) | async-done | bytes 786464 | tf_op jit(solution)/shard_map/all_to_all | solution.py:126
  218.3 2.0 gather_fusion.3
  220.3 0.7 reshape.188
  221.0 3.9 %multiply_reduce_fusion = (f32[256,2]{1,0:T(8,128)S(1)}, bf16[256,512]{1,0:T(8,128)(2,1)}) fusion(f32[256,2,512]{2,1,0:T(2,128)S(1)} %reshape.188, f32[256,512]{1,0:T(8,128)} %convert_element_type.134, f32[256,2]{1,0:T(8,128)S(1)} %copy-done.9), kind=kLoop, calls=%fused_computation.52 | loop fusion | flops 916992 | bytes 1839104 | tf_op jit(solution)/shard_map/reduce_sum | solution.py:150
  224.9 13.0 %all_to_all.42 = f32[8,256,2]{1,2,0:T(2,128)S(1)} all-to-all(f32[8,256,2]{1,2,0:T(2,128)S(1)} %broadcast_in_dim.78), channel_id=1, replica_groups=mesh['ctx'=32,'head'=8] {'head'}, dimensions={0} | all-to-all | bytes 32768 | tf_op jit(solution)/shard_map/all_to_all | solution.py:39
  238.4 0.8 reshape.245
  239.2 5.3 %all-to-all-start.6 = ((f32[32,1,512]{2,1,0:T(1,128)}), f32[32,1,512]{2,1,0:T(1,128)S(1)}, u32[]{:S(2)}, u32[]{:S(2)}) async-start(f32[32,1,512]{2,1,0:T(1,128)} %reshape.245), calls=%async_computation.6 | async-start | bytes 131072 | tf_op jit(solution)/shard_map/all_to_all | solution.py:47
  244.5 1.1 convert_reduce_fusion
  245.7 7.6 %all-to-all-done.6 = f32[32,1,512]{2,1,0:T(1,128)S(1)} async-done(((f32[32,1,512]{2,1,0:T(1,128)}), f32[32,1,512]{2,1,0:T(1,128)S(1)}, u32[]{:S(2)}, u32[]{:S(2)}) %all-to-all-start.6) | async-done | bytes 65568 | tf_op jit(solution)/shard_map/all_to_all | solution.py:47
  253.3 0.5 broadcast.196
  253.8 0.8 reduce.10
  254.8 0.8 reshape.247
  255.6 3.9 %all-to-all-start.7 = ((f32[32,1,512]{2,1,0:T(1,128)}), f32[32,1,512]{2,1,0:T(1,128)S(1)}, u32[]{:S(2)}, u32[]{:S(2)}) async-start(f32[32,1,512]{2,1,0:T(1,128)} %reshape.247), calls=%async_computation.7 | async-start | bytes 131072 | tf_op jit(solution)/shard_map/all_to_all | solution.py:49
  259.5 36.1 %all-reduce.5.cloned.1.call-done = bf16[768,1408]{1,0:T(8,128)(2,1)} async-done(((bf16[768,1408]{1,0:T(8,128)(2,1)}), bf16[768,1408]{1,0:T(8,128)(2,1)}) %all-reduce.5.cloned.1.call-update) | async-done | bytes 2162704 | tf_op jit(solution)/shard_map/psum | solution.py:106
  295.5 4.6 %fusion.9 = (bf16[768,1408]{1,0:T(8,128)(2,1)S(1)}, bf16[768,1408]{1,0:T(8,128)(2,1)S(1)}) fusion(bf16[768,1408]{1,0:T(8,128)(2,1)} %get-tuple-element.29, bf16[768,1408]{1,0:T(8,128)(2,1)} %get-tuple-element.28, bf16[768,1408]{1,0:T(8,128)(2,1)} %all-reduce.5.cloned.1.call-done, f32[768]{0:T(1024)S(1)} %reshape.189), kind=kLoop, calls=%fused_computation.20 | loop fusion | flops 18382848 | bytes 10816512 | tf_op jit(solution)/shard_map/convert_element_type | solution.py:29
  300.2 1.4 fusion.18
  301.6 0.6 copy-done.7
  302.2 0.4 copy-done.24
  302.6 2.3 add_convert_fusion
  304.9 7.3 %all-to-all-start.4 = ((bf16[32,24,512]{2,1,0:T(8,128)(2,1)}), bf16[32,24,512]{2,1,0:T(8,128)(2,1)S(1)}, u32[]{:S(2)}, u32[]{:S(2)}) async-start(bf16[32,24,512]{2,1,0:T(8,128)(2,1)} %bitcast.12), calls=%async_computation.4 | async-start | bytes 1572864 | tf_op jit(solution)/shard_map/all_to_all | solution.py:133
  312.3 4.4 %fusion.15 = bf16[1,1408,512]{2,1,0:T(8,128)(2,1)} fusion(bf16[768,512]{1,0:T(8,128)(2,1)} %bitcast.84, bf16[768,1408]{1,0:T(8,128)(2,1)} %copy-done.8, f32[768]{0:T(1024)S(1)} %reshape.189), kind=kOutput, calls=%fused_computation.34 | convolution fusion | flops 1111261184 | bytes 4393984 | tf_op jit(solution)/shard_map/dot_general | solution.py:8
  316.6 0.8 reduce.11
  317.6 0.7 copy.78
  318.3 4.2 %fusion.13 = bf16[1,1408,512]{2,1,0:T(8,128)(2,1)} fusion(bf16[768,1408]{1,0:T(8,128)(2,1)} %copy-done.7, bf16[768,512]{1,0:T(8,128)(2,1)S(1)} %bitcast.81), kind=kOutput, calls=%fused_computation.32 | convolution fusion | flops 1108017152 | bytes 4390912 | tf_op jit(solution)/shard_map/dot_general | solution.py:8
  322.5 2.4 fusion.14
  324.9 0.7 all-to-all-done.4
  325.6 2.0 gather_fusion.4
  327.8 0.7 fusion.43
  328.5 1.1 fusion.32
  (79 shorter events, 2.6 us)
Async XLA Ops:
  7.2 94.4 %copy-start = (bf16[1,1408,512]{2,1,0:T(8,128)(2,1)S(1)}, bf16[1,1408,512]{2,1,0:T(8,128)(2,1)}, u32[]{:S(2)}) copy-start(bf16[1,1408,512]{2,1,0:T(8,128)(2,1)} %param.15) | copy-start | bytes 4325380
  7.2 18.1 %copy-start.1 = (bf16[256,512]{1,0:T(8,128)(2,1)S(1)}, bf16[256,512]{1,0:T(8,128)(2,1)}, u32[]{:S(2)}) copy-start(bf16[256,512]{1,0:T(8,128)(2,1)} %param.9) | copy-start | bytes 786436
  9.8 21.0 %all-to-all-start = ((f32[8,256,2]{1,2,0:T(2,128)}), f32[8,256,2]{1,2,0:T(2,128)S(1)}, u32[]{:S(2)}, u32[]{:S(2)}) async-start(f32[8,256,2]{1,2,0:T(2,128)} %broadcast_in_dim.38), calls=%async_computation | async-start | bytes 32768 | tf_op jit(solution)/shard_map/all_to_all | solution.py:39
  17.9 174.0 %all-reduce.7.cloned.1.call-start = ((), (), s32[]{:S(2)}) async-start(), calls=%async_computation.9 | async-start | bytes 8650752 | tf_op jit(solution)/shard_map/psum | solution.py:103
  21.5 3.1 copy-start.19
  24.0 0.6 copy-start.15
  24.6 0.6 copy-start.14
  25.2 2.7 copy-start.2
  31.4 9.5 %copy-start.16 = (s32[768]{0:T(1024)S(1)}, s32[768]{0:T(1024)}, u32[]{:S(2)}) copy-start(s32[768]{0:T(1024)} %copy-done.15) | copy-start | bytes 9220
  42.9 22.4 %copy-start.21 = (bf16[1,1408,512]{2,1,0:T(8,128)(2,1)S(1)}, bf16[1,1408,512]{2,1,0:T(8,128)(2,1)}, u32[]{:S(2)}) copy-start(bf16[1,1408,512]{2,1,0:T(8,128)(2,1)} %param.14) | copy-start | bytes 4325380
  65.3 2.8 copy-start.10
  65.3 2.8 copy-start.23
  71.0 0.7 copy-start.18
  71.0 1.1 copy-start.4
  99.6 0.9 copy-start.3
  100.7 0.9 copy-start.12
  195.5 2.3 copy-start.8
  197.7 9.1 %copy-start.20 = (s32[512,1]{0,1:T(1,128)S(1)}, s32[512,1]{0,1:T(1,128)}, u32[]{:S(2)}) copy-start(s32[512,1]{0,1:T(1,128)} %copy-done.19) | copy-start | bytes 6148
  197.8 20.6 %all-to-all-start.3 = ((bf16[32,24,512]{2,1,0:T(8,128)(2,1)}), bf16[32,24,512]{2,1,0:T(8,128)(2,1)S(1)}, u32[]{:S(2)}, u32[]{:S(2)}) async-start(bf16[32,24,512]{2,1,0:T(8,128)(2,1)} %bitcast.10), calls=%async_computation.3 | async-start | bytes 1572864 | tf_op jit(solution)/shard_map/all_to_all | solution.py:126
  205.3 90.3 %all-reduce.5.cloned.1.call-start = ((), (), s32[]{:S(2)}) async-start(), calls=%async_computation.8 | async-start | bytes 4325376 | tf_op jit(solution)/shard_map/psum | solution.py:106
  218.3 2.6 copy-start.9
  220.3 17.7 %copy-start.17 = (s32[256,2]{0,1:T(2,128)S(1)}, s32[256,2]{0,1:T(2,128)}, u32[]{:S(2)}) copy-start(s32[256,2]{0,1:T(2,128)} %param.11) | copy-start | bytes 6148
  239.2 14.1 %all-to-all-start.6 = ((f32[32,1,512]{2,1,0:T(1,128)}), f32[32,1,512]{2,1,0:T(1,128)S(1)}, u32[]{:S(2)}, u32[]{:S(2)}) async-start(f32[32,1,512]{2,1,0:T(1,128)} %reshape.245), calls=%async_computation.6 | async-start | bytes 131072 | tf_op jit(solution)/shard_map/all_to_all | solution.py:47
  255.6 49.3 %all-to-all-start.7 = ((f32[32,1,512]{2,1,0:T(1,128)}), f32[32,1,512]{2,1,0:T(1,128)S(1)}, u32[]{:S(2)}, u32[]{:S(2)}) async-start(f32[32,1,512]{2,1,0:T(1,128)} %reshape.247), calls=%async_computation.7 | async-start | bytes 131072 | tf_op jit(solution)/shard_map/all_to_all | solution.py:49
  259.5 40.7 %copy-start.22 = (bf16[1,1408,512]{2,1,0:T(8,128)(2,1)S(1)}, bf16[1,1408,512]{2,1,0:T(8,128)(2,1)}, u32[]{:S(2)}) copy-start(bf16[1,1408,512]{2,1,0:T(8,128)(2,1)} %param.14) | copy-start | bytes 4325380
  300.1 1.4 copy-start.5
  300.2 2.0 copy-start.7
  300.2 2.4 copy-start.24
  304.9 20.7 %all-to-all-start.4 = ((bf16[32,24,512]{2,1,0:T(8,128)(2,1)}), bf16[32,24,512]{2,1,0:T(8,128)(2,1)S(1)}, u32[]{:S(2)}, u32[]{:S(2)}) async-start(bf16[32,24,512]{2,1,0:T(8,128)(2,1)} %bitcast.12), calls=%async_computation.4 | async-start | bytes 1572864 | tf_op jit(solution)/shard_map/all_to_all | solution.py:133
  312.3 6.0 %copy-start.11 = (bf16[32,24,512]{2,1,0:T(8,128)(2,1)S(1)}, bf16[32,24,512]{2,1,0:T(8,128)(2,1)}, u32[]{:S(2)}) copy-start(bf16[32,24,512]{2,1,0:T(8,128)(2,1)} %copy-done.10) | copy-start | bytes 2359300
  318.3 4.2 %copy-start.6 = (bf16[768,1408]{1,0:T(8,128)(2,1)S(1)}, bf16[768,1408]{1,0:T(8,128)(2,1)}, u32[]{:S(2)}) copy-start(bf16[768,1408]{1,0:T(8,128)(2,1)} %copy-done.5) | copy-start | bytes 6488068
  327.6 1.0 copy-start.13
Sparse Core Ops, SparseCore 0:
  71.1 120.7 all-reduce.6
  208.7 86.7 all-reduce.4

commit v3 on v2

--- a/solution.py
+++ b/solution.py
@@ -85,34 +85,32 @@
         picked = jnp.where(occupied[:, None], values[row_index], jnp.zeros((), values.dtype))
         return picked.reshape(experts, capacity, values.shape[1])
 
-    pad = jnp.zeros((experts, capacity, 128), jnp.bfloat16)
-    cot_pack = jnp.concatenate(
-        [pack_rows(cotangent), pad.at[:, :, 0].set(prob_send.astype(jnp.bfloat16))], axis=2
+    both = lax.all_to_all(
+        jnp.concatenate([pack_rows(tokens), pack_rows(cotangent)], axis=2),
+        "ctx",
+        split_axis=0,
+        concat_axis=0,
+        tiled=True,
     )
-    recv_x = lax.all_to_all(pack_rows(tokens), "ctx", split_axis=0, concat_axis=0, tiled=True)
-    recv_g = lax.all_to_all(cot_pack, "ctx", split_axis=0, concat_axis=0, tiled=True)
-    slot_count = recv_x.shape[0] * recv_x.shape[1]
-    x_rows = recv_x.reshape(slot_count, shard_width)
-    cot_rows = recv_g[:, :, :shard_width].reshape(slot_count, shard_width)
-    prob_rows = recv_g[:, :, shard_width].reshape(slot_count).astype(jnp.float32)
+    recv_p = lax.all_to_all(
+        prob_send.astype(jnp.bfloat16), "ctx", split_axis=0, concat_axis=0, tiled=True
+    )
+    slot_count = both.shape[0] * both.shape[1]
+    x_rows = both[:, :, :shard_width].reshape(slot_count, shard_width)
+    cot_rows = both[:, :, shard_width:].reshape(slot_count, shard_width)
+    prob_rows = recv_p.reshape(slot_count).astype(jnp.float32)
     gate_w = w_gate[0]
     up_w = w_up[0]
     down_w = w_down[0]
     gate_part = contract_last(x_rows, gate_w).astype(jnp.bfloat16)
     up_part = contract_last(x_rows, up_w).astype(jnp.bfloat16)
-    gate_sum, up_sum = lax.psum((gate_part, up_part), "head")
     back_part = contract_last(cot_rows, down_w).astype(jnp.bfloat16)
-    back_part, gate_sum, up_sum = lax.optimization_barrier((back_part, gate_sum, up_sum))
-    back_sum = lax.psum(back_part, "head")
-    hidden = forward_act(gate_sum.astype(jnp.float32), up_sum.astype(jnp.float32))
+    gate_sum, up_sum, back_sum = lax.psum((gate_part, up_part, back_part), "head")
+    gate_pre = gate_sum.astype(jnp.float32)
+    up_pre = up_sum.astype(jnp.float32)
+    hidden = forward_act(gate_pre, up_pre)
+    gate_grad, up_grad = backward_act(gate_pre, up_pre, back_sum.astype(jnp.float32), prob_rows)
     out_rows = jnp.dot(hidden, down_w, preferred_element_type=jnp.float32).astype(jnp.bfloat16)
-    gate_late, up_late, back_sum = lax.optimization_barrier((gate_sum, up_sum, back_sum))
-    gate_grad, up_grad = backward_act(
-        gate_late.astype(jnp.float32),
-        up_late.astype(jnp.float32),
-        back_sum.astype(jnp.float32),
-        prob_rows,
-    )
     dx_rows = (
         jnp.dot(gate_grad, gate_w, preferred_element_type=jnp.float32)
         + jnp.dot(up_grad, up_w, preferred_element_type=jnp.float32)
@@ -122,28 +120,18 @@
     grad_down = contract_rows(scaled, cot_rows).astype(jnp.bfloat16)[None]
     grad_gate = contract_rows(gate_grad, x_rows).astype(jnp.bfloat16)[None]
     grad_up = contract_rows(up_grad, x_rows).astype(jnp.bfloat16)[None]
-    back_out, back_dx = (
-        lax.all_to_all(
-            out_rows.reshape(ctx_count, capacity, shard_width),
-            "ctx",
-            split_axis=0,
-            concat_axis=0,
-            tiled=True,
-        ),
-        lax.all_to_all(
-            dx_rows.reshape(ctx_count, capacity, shard_width),
-            "ctx",
-            split_axis=0,
-            concat_axis=0,
-            tiled=True,
-        ),
+    back_both = lax.all_to_all(
+        jnp.concatenate([out_rows, dx_rows], axis=1).reshape(ctx_count, capacity, 2 * shard_width),
+        "ctx",
+        split_axis=0,
+        concat_axis=0,
+        tiled=True,
     )
-    out_pairs = back_out.reshape(experts * capacity, shard_width)[slot_index].reshape(
-        tok_rows, pick_count, shard_width
+    both_pairs = back_both.reshape(experts * capacity, 2 * shard_width)[slot_index].reshape(
+        tok_rows, pick_count, 2 * shard_width
     )
-    dx_pairs = back_dx.reshape(experts * capacity, shard_width)[slot_index].reshape(
-        tok_rows, pick_count, shard_width
-    )
+    out_pairs = both_pairs[:, :, :shard_width]
+    dx_pairs = both_pairs[:, :, shard_width:]
     mixed = jnp.sum(prob_pairs[:, :, None] * out_pairs.astype(jnp.float32), axis=1).astype(
         jnp.bfloat16
     )

time: 341 us -> 340 us (level)
  waiting for transfers between devices: 144 us -> 167 us
  blocking collectives: 61.8 us -> 42.8 us
  other arithmetic: 22.8 us -> 17.4 us
    all_to_all x3 -> x2, blocking collectives: 61.8 us -> 42.8 us  [the longest x1 30.6 us: local(): lax.all_to_all(jnp.concatenate([pack_rows(tokens), pack_rows(cotangent)],...]
    psum x2 -> x1, waiting for transfers between devices: 124 us -> 138 us  [local(): lax.psum((gate_part, up_part, back_part), 'head')]
    all_to_all x1 -> x2, starting transfers between devices: 8.11 us -> 18.1 us  [head_sum(): lax.all_to_all(spread, 'head', split_axis=0, concat_axis=0, tiled=True)]
    all_to_all x1, waiting for transfers between devices: 0.01 us -> 6.29 us  [ctx_sum(): lax.all_to_all(spread, 'ctx', split_axis=0, concat_axis=0, tiled=True)]
    all_to_all x2 -> x1, starting transfers between devices: 14.8 us -> 8.61 us  [local(): lax.all_to_all(jnp.concatenate([out_rows, dx_rows], axis=1).reshape(ctx_c...]
    convert_element_type x2 -> x1, other arithmetic: 4.69 us -> 0.05 us  [local(): prob_rows = recv_p.reshape(slot_count).astype(jnp.float32)]
    unnamed x56 -> x52, local copies, waits for them, and re-layouts: 7.69 us -> 5.18 us
    all_to_all x2 -> x1, waiting for transfers between devices: 12.1 us -> 14.4 us  [local(): lax.all_to_all(jnp.concatenate([out_rows, dx_rows], axis=1).reshape(ctx_c...]
  transfers between devices with their start and end apart: 7 -> 6, of which waited for: 5 -> 5; matrix products, arithmetic and copies ran while one was open for 14% -> 8% of each run, Pallas kernels for 0% -> 0%
where the time goes in v3:
time: 340 us; the launch traced here: 337 us
  waiting for transfers between devices  167 us (49%)
  blocking collectives  42.8 us (13%)
  starting transfers between devices  35 us (10%)
  local copies, waits for them, and re-layouts  33.1 us (10%)
  matrix products  27.7 us (8%)
  other arithmetic  17.4 us (5%)
  between operations  14.5 us (4%)
    psum x1, waiting for transfers between devices, local(): lax.psum((gate_part, up_part, back_part), 'head')  138 us
    all_to_all x1, blocking collectives, local(): lax.all_to_all(jnp.concatenate([pack_rows(tokens), pack_rows(cotangent)],...  30.6 us
    all_to_all x2, starting transfers between devices, head_sum(): lax.all_to_all(spread, 'head', split_axis=0, concat_axis=0, tiled=True)  18.1 us
    all_to_all x1, waiting for transfers between devices, local(): lax.all_to_all(jnp.concatenate([out_rows, dx_rows], axis=1).reshape(ctx_c...  14.4 us
    all_to_all x1, blocking collectives, local(): lax.all_to_all(prob_send.astype(jnp.bfloat16), 'ctx', split_axis=0, conca...  12.2 us
    dot_general x3, matrix products, contract_rows(): lax.dot_general(left, right, (((0,), (0,)), ((), ())), preferred_element_...  11.1 us
    all_to_all x1, starting transfers between devices, local(): lax.all_to_all(jnp.concatenate([out_rows, dx_rows], axis=1).reshape(ctx_c...  8.61 us
    dot_general x3, matrix products, contract_last(): lax.dot_general(left, right, (((1,), (1,)), ((), ())), preferred_element_...  8.43 us
  transfers between devices with their start and end apart: 6, of which 5 were waited for; matrix products, arithmetic and copies ran while one was open for 8% of the time, Pallas kernels for 0%

profile of v3, /device:TPU:64, one launch (start us, length us, event | category | flops | bytes accessed | tf_op | source)
XLA Modules:
  0.0 337.0 jit_solution(727289403727142691)
XLA Ops:
  7.2 1.2 fusion.40
  8.5 0.7 select_reduce_fusion.1
  9.2 0.6 broadcast_in_dim.38
  9.8 8.1 %all-to-all-start = ((f32[8,256,2]{1,2,0:T(2,128)}), f32[8,256,2]{1,2,0:T(2,128)S(1)}, u32[]{:S(2)}, u32[]{:S(2)}) async-start(f32[8,256,2]{1,2,0:T(2,128)} %broadcast_in_dim.38), calls=%async_computation | async-start | bytes 32768 | tf_op jit(solution)/shard_map/all_to_all | solution.py:39
  17.9 0.8 copy.61
  18.7 0.1 eq.45
  18.9 0.1 eq.41
  19.0 0.7 broadcast_multiply_fusion
  19.7 1.2 reduce-window.6
  20.9 0.2 slice_reduce_fusion
  21.1 0.1 copy.60
  21.3 0.1 mul.102
  21.6 2.4 scatter_custom_fusion
  24.0 0.6 pad_clamp_fusion.1
  24.6 0.6 copy-done.13
  25.2 2.7 gather_fusion
  27.9 2.8 gather_fusion.1
  30.8 0.6 reduce_sum.75
  31.4 0.8 add_divide_fusion.1
  32.2 0.8 copy.59
  33.0 1.0 reshape.134
  34.0 6.8 %gather_fusion.2 = bf16[768]{0:T(1024)(128)(2,1)} fusion(bf16[512]{0:T(512)(128)(2,1)S(1)} %reshape.134, s32[1024]{0:T(1024)} %get-tuple-element.52), kind=kCustom, calls=%fused_computation.2 | custom fusion | bytes 6144 | tf_op jit(solution)/shard_map/gather | solution.py:80
  40.8 1.3 select_convert_fusion
  42.1 0.8 broadcast_in_dim.39
  42.9 0.2 broadcast_select_fusion.1
  43.1 0.2 pad_maximum_fusion
  43.3 30.6 %all_to_all.36 = bf16[32,24,1024]{2,1,0:T(8,128)(2,1)S(1)} all-to-all(bf16[32,24,1024]{2,1,0:T(8,128)(2,1)S(1)} %pad_maximum_fusion), channel_id=1, replica_groups=mesh['ctx'=32,'head'=8] {'ctx'}, dimensions={0} | all-to-all | bytes 3145728 | tf_op jit(solution)/shard_map/all_to_all | solution.py:88
  74.1 2.8 convolution_convert_fusion.1
  76.8 2.8 convolution_convert_fusion.2
  79.7 2.8 convolution_convert_fusion
  82.5 0.7 copy-done.19
  83.3 12.2 %all_to_all.37 = bf16[32,1,24]{2,1,0:T(2,128)(2,1)S(1)} all-to-all(bf16[32,1,24]{2,1,0:T(2,128)(2,1)S(1)} %convert_element_type.128), channel_id=1, replica_groups=mesh['ctx'=32,'head'=8] {'ctx'}, dimensions={0} | all-to-all | bytes 3072 | tf_op jit(solution)/shard_map/all_to_all | solution.py:95
  95.6 137.8 %all-reduce.3.cloned.1.call-done = (bf16[768,1408]{1,0:T(8,128)(2,1)}, bf16[768,1408]{1,0:T(8,128)(2,1)}, bf16[768,1408]{1,0:T(8,128)(2,1)}) async-done(((bf16[768,1408]{1,0:T(8,128)(2,1)}, bf16[768,1408]{1,0:T(8,128)(2,1)}, bf16[768,1408]{1,0:T(8,128)(2,1)}), (bf16[768,1408]{1,0:T(8,128)(2,1)}, bf16[768,1408]{1,0:T(8,128)(2,1)}, bf16[768,1408]{1,0:T(8,128)(2,1)})) %all-reduce.3.cloned.1.call-update) | async-done | bytes 6488080 | tf_op jit(solution)/shard_map/psum | solution.py:108
  233.4 5.0 %fusion.3 = (bf16[768,1408]{1,0:T(8,128)(2,1)S(1)}, bf16[768,1408]{1,0:T(8,128)(2,1)S(1)}, bf16[768,1408]{1,0:T(8,128)(2,1)S(1)}) fusion(bf16[768,1408]{1,0:T(8,128)(2,1)} %get-tuple-element.34, bf16[768,1408]{1,0:T(8,128)(2,1)} %get-tuple-element.33, bf16[768,1408]{1,0:T(8,128)(2,1)} %get-tuple-element.32, f32[768]{0:T(1024)S(1)} %reshape.141), kind=kLoop, calls=%fused_computation.13 | loop fusion | flops 20545536 | bytes 12979200 | tf_op jit(solution)/shard_map/convert_element_type | solution.py:29
  238.4 1.5 fusion.15
  239.9 0.5 copy-done.4
  240.4 1.5 fusion.21
  241.9 1.5 add_convert_fusion
  243.5 1.6 copy.66
  245.2 8.6 %all-to-all-start.3 = ((bf16[32,24,1024]{2,1,0:T(8,128)(2,1)}), bf16[32,24,1024]{2,1,0:T(8,128)(2,1)S(1)}, u32[]{:S(2)}, u32[]{:S(2)}) async-start(bf16[32,24,1024]{2,1,0:T(8,128)(2,1)} %bitcast.72), calls=%async_computation.3 | async-start | bytes 3145728 | tf_op jit(solution)/shard_map/all_to_all | solution.py:123
  253.8 0.9 convert_element_type.120
  254.7 4.4 %fusion.8 = bf16[1,1408,512]{2,1,0:T(8,128)(2,1)} fusion(bf16[768,1408]{1,0:T(8,128)(2,1)} %copy-done.6, bf16[768,512]{1,0:T(8,128)(2,1)} %bitcast.79), kind=kOutput, calls=%fused_computation.27 | convolution fusion | flops 1108017152 | bytes 4390912 | tf_op jit(solution)/shard_map/dot_general | solution.py:8
  259.1 2.5 fusion.10
  261.6 14.4 %all-to-all-done.3 = bf16[32,24,1024]{2,1,0:T(8,128)(2,1)S(1)} async-done(((bf16[32,24,1024]{2,1,0:T(8,128)(2,1)}), bf16[32,24,1024]{2,1,0:T(8,128)(2,1)S(1)}, u32[]{:S(2)}, u32[]{:S(2)}) %all-to-all-start.3) | async-done | bytes 1572896 | tf_op jit(solution)/shard_map/all_to_all | solution.py:123
  276.0 2.8 gather_fusion.3
  278.8 1.5 reshape.138
  280.3 3.2 fusion.28
  283.6 0.6 broadcast_in_dim.76
  284.3 9.9 %all-to-all-start.4 = ((f32[8,256,2]{1,2,0:T(2,128)}), f32[8,256,2]{1,2,0:T(2,128)S(1)}, u32[]{:S(2)}, u32[]{:S(2)}) async-start(f32[8,256,2]{1,2,0:T(2,128)} %broadcast_in_dim.76), calls=%async_computation.4 | async-start | bytes 32768 | tf_op jit(solution)/shard_map/all_to_all | solution.py:39
  294.2 4.2 %fusion.9 = bf16[1,1408,512]{2,1,0:T(8,128)(2,1)} fusion(bf16[768,1408]{1,0:T(8,128)(2,1)} %copy-done.3, bf16[768,512]{1,0:T(8,128)(2,1)} %bitcast.80), kind=kOutput, calls=%fused_computation.28 | convolution fusion | flops 1108017152 | bytes 4390912 | tf_op jit(solution)/shard_map/dot_general | solution.py:8
  298.4 1.2 all-to-all-done.4
  299.7 0.2 convolution_bitcast_fusion
  300.1 0.8 reshape.195
  300.9 4.4 %all-to-all-start.5 = ((f32[32,1,512]{2,1,0:T(1,128)}), f32[32,1,512]{2,1,0:T(1,128)S(1)}, u32[]{:S(2)}, u32[]{:S(2)}) async-start(f32[32,1,512]{2,1,0:T(1,128)} %reshape.195), calls=%async_computation.5 | async-start | bytes 131072 | tf_op jit(solution)/shard_map/all_to_all | solution.py:47
  305.3 1.5 fusion.39
  306.8 7.0 %all-to-all-done.5 = f32[32,1,512]{2,1,0:T(1,128)S(1)} async-done(((f32[32,1,512]{2,1,0:T(1,128)}), f32[32,1,512]{2,1,0:T(1,128)S(1)}, u32[]{:S(2)}, u32[]{:S(2)}) %all-to-all-start.5) | async-done | bytes 65568 | tf_op jit(solution)/shard_map/all_to_all | solution.py:47
  313.8 0.6 broadcast.162
  314.4 0.8 reduce.6
  315.4 0.8 reshape.197
  316.2 3.9 %all-to-all-start.6 = ((f32[32,1,512]{2,1,0:T(1,128)}), f32[32,1,512]{2,1,0:T(1,128)S(1)}, u32[]{:S(2)}, u32[]{:S(2)}) async-start(f32[32,1,512]{2,1,0:T(1,128)} %reshape.197), calls=%async_computation.6 | async-start | bytes 131072 | tf_op jit(solution)/shard_map/all_to_all | solution.py:49
  320.0 2.2 fusion.26
  322.2 6.3 %all-to-all-done.6 = f32[32,1,512]{2,1,0:T(1,128)S(1)} async-done(((f32[32,1,512]{2,1,0:T(1,128)}), f32[32,1,512]{2,1,0:T(1,128)S(1)}, u32[]{:S(2)}, u32[]{:S(2)}) %all-to-all-start.6) | async-done | bytes 65568 | tf_op jit(solution)/shard_map/all_to_all | solution.py:49
  328.5 0.8 reduce.7
  329.4 0.7 copy.71
  (70 shorter events, 1.3 us)
Async XLA Ops:
  7.2 66.9 %copy-start = (bf16[1,1408,512]{2,1,0:T(8,128)(2,1)S(1)}, bf16[1,1408,512]{2,1,0:T(8,128)(2,1)}, u32[]{:S(2)}) copy-start(bf16[1,1408,512]{2,1,0:T(8,128)(2,1)} %param.12) | copy-start | bytes 4325380
  7.2 18.1 %copy-start.1 = (bf16[256,512]{1,0:T(8,128)(2,1)S(1)}, bf16[256,512]{1,0:T(8,128)(2,1)}, u32[]{:S(2)}) copy-start(bf16[256,512]{1,0:T(8,128)(2,1)} %param.7) | copy-start | bytes 786436
  9.8 21.0 %all-to-all-start = ((f32[8,256,2]{1,2,0:T(2,128)}), f32[8,256,2]{1,2,0:T(2,128)S(1)}, u32[]{:S(2)}, u32[]{:S(2)}) async-start(f32[8,256,2]{1,2,0:T(2,128)} %broadcast_in_dim.38), calls=%async_computation | async-start | bytes 32768 | tf_op jit(solution)/shard_map/all_to_all | solution.py:39
  17.9 215.5 %all-reduce.3.cloned.1.call-start = ((), (), s32[]{:S(2)}) async-start(), calls=%async_computation.7 | async-start | bytes 12976128 | tf_op jit(solution)/shard_map/psum | solution.py:108
  21.5 3.1 copy-start.17
  24.0 0.6 copy-start.14
  24.6 0.6 copy-start.13
  25.2 2.7 copy-start.2
  31.4 9.5 %copy-start.15 = (s32[768]{0:T(1024)S(1)}, s32[768]{0:T(1024)}, u32[]{:S(2)}) copy-start(s32[768]{0:T(1024)} %copy-done.14) | copy-start | bytes 9220
  74.0 2.8 copy-start.9
  74.0 5.7 %copy-start.10 = (bf16[32,24,512]{2,1,0:T(8,128)(2,1)}, bf16[32,24,512]{2,1,0:T(8,128)(2,1)S(1)}, u32[]{:S(2)}) copy-start(bf16[32,24,512]{2,1,0:T(8,128)(2,1)S(1)} %get-tuple-element.43) | copy-start | bytes 2359300
  74.0 2.8 copy-start.21
  76.8 2.8 copy-start.20
  82.5 0.7 copy-start.19
  238.4 1.5 copy-start.3
  238.4 2.0 copy-start.4
  238.4 3.5 %copy-start.6 = (bf16[768,1408]{1,0:T(8,128)(2,1)}, bf16[768,1408]{1,0:T(8,128)(2,1)S(1)}, u32[]{:S(2)}) copy-start(bf16[768,1408]{1,0:T(8,128)(2,1)S(1)} %get-tuple-element.39) | copy-start | bytes 6488068
  240.4 1.5 copy-start.22
  245.2 9.5 %copy-start.18 = (s32[512,1]{0,1:T(1,128)S(1)}, s32[512,1]{0,1:T(1,128)}, u32[]{:S(2)}) copy-start(s32[512,1]{0,1:T(1,128)} %copy-done.17) | copy-start | bytes 6148
  245.2 30.8 %all-to-all-start.3 = ((bf16[32,24,1024]{2,1,0:T(8,128)(2,1)}), bf16[32,24,1024]{2,1,0:T(8,128)(2,1)S(1)}, u32[]{:S(2)}, u32[]{:S(2)}) async-start(bf16[32,24,1024]{2,1,0:T(8,128)(2,1)} %bitcast.72), calls=%async_computation.3 | async-start | bytes 3145728 | tf_op jit(solution)/shard_map/all_to_all | solution.py:123
  254.7 4.4 %copy-start.5 = (bf16[768,1408]{1,0:T(8,128)(2,1)S(1)}, bf16[768,1408]{1,0:T(8,128)(2,1)}, u32[]{:S(2)}) copy-start(bf16[768,1408]{1,0:T(8,128)(2,1)} %copy-done.4) | copy-start | bytes 6488068
  254.7 4.4 %copy-start.11 = (bf16[32,24,512]{2,1,0:T(8,128)(2,1)S(1)}, bf16[32,24,512]{2,1,0:T(8,128)(2,1)}, u32[]{:S(2)}) copy-start(bf16[32,24,512]{2,1,0:T(8,128)(2,1)} %copy-done.10) | copy-start | bytes 2359300
  278.8 1.5 copy-start.7
  278.8 1.6 copy-start.8
  284.3 15.4 %all-to-all-start.4 = ((f32[8,256,2]{1,2,0:T(2,128)}), f32[8,256,2]{1,2,0:T(2,128)S(1)}, u32[]{:S(2)}, u32[]{:S(2)}) async-start(f32[8,256,2]{1,2,0:T(2,128)} %broadcast_in_dim.76), calls=%async_computation.4 | async-start | bytes 32768 | tf_op jit(solution)/shard_map/all_to_all | solution.py:39
  294.2 5.5 %copy-start.16 = (s32[256,2]{0,1:T(2,128)S(1)}, s32[256,2]{0,1:T(2,128)}, u32[]{:S(2)}) copy-start(s32[256,2]{0,1:T(2,128)} %param.9) | copy-start | bytes 6148
  299.9 20.1 %copy-start.12 = (bf16[512,32]{0,1:T(8,128)(2,1)S(1)}, bf16[512,32]{0,1:T(8,128)(2,1)}, u32[]{:S(2)}) copy-start(bf16[512,32]{0,1:T(8,128)(2,1)} %param.10) | copy-start | bytes 98308
  300.9 12.9 %all-to-all-start.5 = ((f32[32,1,512]{2,1,0:T(1,128)}), f32[32,1,512]{2,1,0:T(1,128)S(1)}, u32[]{:S(2)}, u32[]{:S(2)}) async-start(f32[32,1,512]{2,1,0:T(1,128)} %reshape.195), calls=%async_computation.5 | async-start | bytes 131072 | tf_op jit(solution)/shard_map/all_to_all | solution.py:47
  316.2 12.3 %all-to-all-start.6 = ((f32[32,1,512]{2,1,0:T(1,128)}), f32[32,1,512]{2,1,0:T(1,128)S(1)}, u32[]{:S(2)}, u32[]{:S(2)}) async-start(f32[32,1,512]{2,1,0:T(1,128)} %reshape.197), calls=%async_computation.6 | async-start | bytes 131072 | tf_op jit(solution)/shard_map/all_to_all | solution.py:49
Sparse Core Ops, SparseCore 0:
  82.6 150.6 all-reduce.2

commit v4 on v3

--- a/solution.py
+++ b/solution.py
@@ -69,31 +69,27 @@
     id_hits = (flat_ids[:, None] == jnp.arange(experts, dtype=jnp.int32)[None, :]).astype(jnp.int32)
     places = jnp.sum((jnp.cumsum(id_hits, axis=0) - 1) * id_hits, axis=1)
     slot_index = flat_ids * capacity + places
-    slot_table = (
-        jnp.zeros((experts * capacity,), jnp.int32)
-        .at[slot_index]
-        .set(jnp.arange(tok_rows * pick_count, dtype=jnp.int32) + 1)
-    )
-    occupied = slot_table > 0
-    source = jnp.maximum(slot_table - 1, 0)
-    row_index = source // pick_count
-    prob_send = jnp.where(occupied, prob_pairs.reshape(-1)[source], jnp.float32(0.0)).reshape(
-        experts, capacity
-    )
-
-    def pack_rows(values):
-        picked = jnp.where(occupied[:, None], values[row_index], jnp.zeros((), values.dtype))
-        return picked.reshape(experts, capacity, values.shape[1])
-
+    slot_ids = jnp.arange(experts * capacity, dtype=jnp.int32)
+    pick_hit = slot_ids[:, None] == slot_index[None, :]
+    token_hit = pick_hit.reshape(experts * capacity, tok_rows, pick_count).any(axis=2)
+    rows_in = jnp.concatenate([tokens, cotangent], axis=1)
+    packed = jnp.dot(
+        token_hit.astype(jnp.bfloat16), rows_in, preferred_element_type=jnp.float32
+    ).astype(jnp.bfloat16)
+    prob_send = jnp.sum(jnp.where(pick_hit, prob_pairs.reshape(-1)[None, :], 0.0), axis=1)
     both = lax.all_to_all(
-        jnp.concatenate([pack_rows(tokens), pack_rows(cotangent)], axis=2),
+        packed.reshape(experts, capacity, 2 * shard_width),
         "ctx",
         split_axis=0,
         concat_axis=0,
         tiled=True,
     )
     recv_p = lax.all_to_all(
-        prob_send.astype(jnp.bfloat16), "ctx", split_axis=0, concat_axis=0, tiled=True
+        prob_send.astype(jnp.bfloat16).reshape(experts, capacity),
+        "ctx",
+        split_axis=0,
+        concat_axis=0,
+        tiled=True,
     )
     slot_count = both.shape[0] * both.shape[1]
     x_rows = both[:, :, :shard_width].reshape(slot_count, shard_width)
@@ -127,9 +123,12 @@
         concat_axis=0,
         tiled=True,
     )
-    both_pairs = back_both.reshape(experts * capacity, 2 * shard_width)[slot_index].reshape(
-        tok_rows, pick_count, 2 * shard_width
-    )
+    both_pairs = lax.dot_general(
+        pick_hit.astype(jnp.bfloat16),
+        back_both.reshape(experts * capacity, 2 * shard_width),
+        (((0,), (0,)), ((), ())),
+        preferred_element_type=jnp.float32,
+    ).astype(jnp.bfloat16).reshape(tok_rows, pick_count, 2 * shard_width)
     out_pairs = both_pairs[:, :, :shard_width]
     dx_pairs = both_pairs[:, :, shard_width:]
     mixed = jnp.sum(prob_pairs[:, :, None] * out_pairs.astype(jnp.float32), axis=1).astype(

time: 340 us -> 313 us (0.921)
  local copies, waits for them, and re-layouts: 33.1 us -> 13 us
  waiting for transfers between devices: 167 us -> 162 us
  other arithmetic: 17.4 us -> 12.9 us
  matrix products: 27.7 us -> 31.4 us
    gather x4 -> x0, local copies, waits for them, and re-layouts: 15.1 us -> none  [the longest x1 6.84 us: local(): prob_pairs.reshape(-1)[source]]
    psum x1, waiting for transfers between devices: 138 us -> 126 us  [local(): lax.psum((gate_part, up_part, back_part), 'head')]
    all_to_all x2, waiting for transfers between devices: 1.2 us -> 6.86 us  [head_sum(): lax.all_to_all(spread, 'head', split_axis=0, concat_axis=0, tiled=True)]
    dot_general x0 -> x2, matrix products: none -> 5.01 us  [the longest x1 3.41 us: local(): lax.dot_general(pick_hit.astype(jnp.bfloat16), back_both.reshape(experts...]
  transfers between devices with their start and end apart: 6 -> 6, of which waited for: 5 -> 6; matrix products, arithmetic and copies ran while one was open for 8% -> 5% of each run, Pallas kernels for 0% -> 0%
where the time goes in v4:
time: 313 us; the launch traced here: 311 us
  waiting for transfers between devices  162 us (52%)
  blocking collectives  43.3 us (14%)
  starting transfers between devices  34.1 us (11%)
  matrix products  31.4 us (10%)
  between operations  14.4 us (5%)
  local copies, waits for them, and re-layouts  13 us (4%)
  other arithmetic  12.9 us (4%)
    psum x1, waiting for transfers between devices, local(): lax.psum((gate_part, up_part, back_part), 'head')  126 us
    all_to_all x1, blocking collectives, local(): lax.all_to_all(packed.reshape(experts, capacity, 2 * shard_width), 'ctx',...  31.3 us
    all_to_all x2, starting transfers between devices, head_sum(): lax.all_to_all(spread, 'head', split_axis=0, concat_axis=0, tiled=True)  17.1 us
    all_to_all x1, waiting for transfers between devices, local(): lax.all_to_all(jnp.concatenate([out_rows, dx_rows], axis=1).reshape(ctx_c...  15.4 us
    all_to_all x1, blocking collectives, local(): lax.all_to_all(prob_send.astype(jnp.bfloat16).reshape(experts, capacity),...  12 us
    dot_general x3, matrix products, contract_rows(): lax.dot_general(left, right, (((0,), (0,)), ((), ())), preferred_element_...  10.9 us
    all_to_all x1, starting transfers between devices, local(): lax.all_to_all(jnp.concatenate([out_rows, dx_rows], axis=1).reshape(ctx_c...  8.67 us
    dot_general x3, matrix products, contract_last(): lax.dot_general(left, right, (((1,), (1,)), ((), ())), preferred_element_...  8.4 us
  transfers between devices with their start and end apart: 6, of which 6 were waited for; matrix products, arithmetic and copies ran while one was open for 5% of the time, Pallas kernels for 0%

profile of v4, /device:TPU:64, one launch (start us, length us, event | category | flops | bytes accessed | tf_op | source)
XLA Modules:
  0.0 310.7 jit_solution(15233039600629075918)
XLA Ops:
  7.2 0.9 copy.79
  8.1 0.1 eq.63
  8.3 0.1 reshape.112
  8.5 1.2 reduce-window.6
  9.6 0.2 slice_reduce_fusion
  9.9 0.1 fusion.37
  10.0 0.1 reduce_sum.86
  10.1 0.1 copy.82
  10.2 0.7 multiply_add_fusion
  10.9 0.3 fusion.13
  11.2 1.6 convolution_convert_fusion.6
  12.8 31.3 %all_to_all.36 = bf16[32,24,1024]{2,1,0:T(8,128)(2,1)S(1)} all-to-all(bf16[32,24,1024]{2,1,0:T(8,128)(2,1)S(1)} %bitcast.70), channel_id=1, replica_groups=mesh['ctx'=32,'head'=8] {'ctx'}, dimensions={0} | all-to-all | bytes 3145728 | tf_op jit(solution)/shard_map/all_to_all | solution.py:80
  44.1 0.1 fusion.43
  44.2 2.8 convolution_convert_fusion.1
  47.0 2.8 convolution_convert_fusion.2
  49.9 2.8 convolution_convert_fusion
  52.7 0.9 copy-done.1
  53.6 0.2 fusion.45
  53.8 0.6 broadcast_in_dim.26
  54.4 7.2 %all-to-all-start = ((f32[8,256,2]{1,2,0:T(2,128)}), f32[8,256,2]{1,2,0:T(2,128)S(1)}, u32[]{:S(2)}, u32[]{:S(2)}) async-start(f32[8,256,2]{1,2,0:T(2,128)} %broadcast_in_dim.26), calls=%async_computation | async-start | bytes 32768 | tf_op jit(solution)/shard_map/all_to_all | solution.py:39
  61.7 5.7 %all-to-all-done = f32[8,256,2]{1,2,0:T(2,128)S(1)} async-done(((f32[8,256,2]{1,2,0:T(2,128)}), f32[8,256,2]{1,2,0:T(2,128)S(1)}, u32[]{:S(2)}, u32[]{:S(2)}) %all-to-all-start) | async-done | bytes 16416 | tf_op jit(solution)/shard_map/all_to_all | solution.py:39
  67.4 0.1 copy.78
  67.5 0.1 broadcast_in_dim.27
  67.7 0.2 select_reduce_fusion
  67.9 0.1 convert_element_type.139
  68.0 12.0 %all_to_all.37 = bf16[32,1,24]{2,1,0:T(2,128)(2,1)S(1)} all-to-all(bf16[32,1,24]{2,1,0:T(2,128)(2,1)S(1)} %convert_element_type.139), channel_id=1, replica_groups=mesh['ctx'=32,'head'=8] {'ctx'}, dimensions={0} | all-to-all | bytes 3072 | tf_op jit(solution)/shard_map/all_to_all | solution.py:87
  80.1 0.1 reshape.122
  80.2 126.1 %all-reduce.3.cloned.1.call-done = (bf16[768,1408]{1,0:T(8,128)(2,1)}, bf16[768,1408]{1,0:T(8,128)(2,1)}, bf16[768,1408]{1,0:T(8,128)(2,1)}) async-done(((bf16[768,1408]{1,0:T(8,128)(2,1)}, bf16[768,1408]{1,0:T(8,128)(2,1)}, bf16[768,1408]{1,0:T(8,128)(2,1)}), (bf16[768,1408]{1,0:T(8,128)(2,1)}, bf16[768,1408]{1,0:T(8,128)(2,1)}, bf16[768,1408]{1,0:T(8,128)(2,1)})) %all-reduce.3.cloned.1.call-update) | async-done | bytes 6488080 | tf_op jit(solution)/shard_map/psum | solution.py:104
  206.3 5.0 %fusion.3 = (bf16[768,1408]{1,0:T(8,128)(2,1)S(1)}, bf16[768,1408]{1,0:T(8,128)(2,1)S(1)}, bf16[768,1408]{1,0:T(8,128)(2,1)S(1)}) fusion(bf16[768,1408]{1,0:T(8,128)(2,1)} %get-tuple-element.40, bf16[768,1408]{1,0:T(8,128)(2,1)} %get-tuple-element.39, bf16[768,1408]{1,0:T(8,128)(2,1)} %get-tuple-element.38, f32[768]{0:T(1024)S(1)} %reshape.122), kind=kLoop, calls=%fused_computation.8 | loop fusion | flops 20545536 | bytes 12979200 | tf_op jit(solution)/shard_map/convert_element_type | solution.py:29
  211.3 1.5 fusion.18
  212.8 0.5 copy-done.3
  213.3 1.5 fusion.24
  214.8 1.5 add_convert_fusion
  216.3 0.1 pad_maximum_fusion
  216.4 1.7 copy.85
  218.2 8.7 %all-to-all-start.3 = ((bf16[32,24,1024]{2,1,0:T(8,128)(2,1)}), bf16[32,24,1024]{2,1,0:T(8,128)(2,1)}, u32[]{:S(2)}, u32[]{:S(2)}) async-start(bf16[32,24,1024]{2,1,0:T(8,128)(2,1)} %bitcast.7), calls=%async_computation.3 | async-start | bytes 3145728 | tf_op jit(solution)/shard_map/all_to_all | solution.py:119
  226.9 0.1 convert_element_type.131
  226.9 4.2 %fusion.8 = bf16[1,1408,512]{2,1,0:T(8,128)(2,1)} fusion(bf16[768,1408]{1,0:T(8,128)(2,1)} %copy-done.5, bf16[768,512]{1,0:T(8,128)(2,1)S(1)} %bitcast.76), kind=kOutput, calls=%fused_computation.22 | convolution fusion | flops 1108017152 | bytes 4390912 | tf_op jit(solution)/shard_map/dot_general | solution.py:8
  231.1 2.5 fusion.10
  233.7 15.4 %all-to-all-done.3 = bf16[32,24,1024]{2,1,0:T(8,128)(2,1)} async-done(((bf16[32,24,1024]{2,1,0:T(8,128)(2,1)}), bf16[32,24,1024]{2,1,0:T(8,128)(2,1)}, u32[]{:S(2)}, u32[]{:S(2)}) %all-to-all-start.3) | async-done | bytes 1572896 | tf_op jit(solution)/shard_map/all_to_all | solution.py:119
  249.1 3.4 %fusion.14 = bf16[512,1024]{1,0:T(8,128)(2,1)} fusion(bf16[768,1024]{1,0:T(8,128)(2,1)} %bitcast.8, s32[512]{0:T(512)S(1)} %multiply_add_fusion.1), kind=kOutput, calls=%fused_computation.34 | convolution fusion | flops 806223872 | bytes 2623488 | tf_op jit(solution)/shard_map/dot_general | solution.py:126
  252.5 1.5 reshape.119
  254.0 3.2 %fusion.31 = (f32[256,2]{1,0:T(8,128)S(1)}, bf16[256,512]{1,0:T(8,128)(2,1)}) fusion(f32[256,512]{1,0:T(8,128)S(1)} %convert_element_type.131, bf16[256,2,1024]{2,1,0:T(2,128)(2,1)S(1)} %reshape.119, f32[256,2]{1,0:T(8,128)S(1)} %copy.78), kind=kLoop, calls=%fused_computation.51 | loop fusion | flops 1179136 | bytes 1314816 | tf_op jit(solution)/shard_map/reduce_sum | solution.py:137
  257.2 0.1 copy.88
  257.3 0.6 broadcast_in_dim.30
  257.9 9.9 %all-to-all-start.4 = ((f32[8,256,2]{1,2,0:T(2,128)}), f32[8,256,2]{1,2,0:T(2,128)S(1)}, u32[]{:S(2)}, u32[]{:S(2)}) async-start(f32[8,256,2]{1,2,0:T(2,128)} %broadcast_in_dim.30), calls=%async_computation.4 | async-start | bytes 32768 | tf_op jit(solution)/shard_map/all_to_all | solution.py:39
  267.8 4.2 %fusion.9 = bf16[1,1408,512]{2,1,0:T(8,128)(2,1)} fusion(bf16[768,1408]{1,0:T(8,128)(2,1)} %copy-done.2, bf16[768,512]{1,0:T(8,128)(2,1)} %bitcast.75), kind=kOutput, calls=%fused_computation.23 | convolution fusion | flops 1108017152 | bytes 4390912 | tf_op jit(solution)/shard_map/dot_general | solution.py:8
  272.0 1.2 all-to-all-done.4
  273.3 0.2 convolution_bitcast_fusion
  273.5 0.1 copy.89
  273.7 0.8 reshape.131
  274.5 4.4 %all-to-all-start.5 = ((f32[32,1,512]{2,1,0:T(1,128)}), f32[32,1,512]{2,1,0:T(1,128)S(1)}, u32[]{:S(2)}, u32[]{:S(2)}) async-start(f32[32,1,512]{2,1,0:T(1,128)} %reshape.131), calls=%async_computation.5 | async-start | bytes 131072 | tf_op jit(solution)/shard_map/all_to_all | solution.py:47
  278.9 1.5 fusion.44
  280.4 7.0 %all-to-all-done.5 = f32[32,1,512]{2,1,0:T(1,128)S(1)} async-done(((f32[32,1,512]{2,1,0:T(1,128)}), f32[32,1,512]{2,1,0:T(1,128)S(1)}, u32[]{:S(2)}, u32[]{:S(2)}) %all-to-all-start.5) | async-done | bytes 65568 | tf_op jit(solution)/shard_map/all_to_all | solution.py:47
  287.4 0.6 broadcast.86
  288.0 0.8 reduce.6
  288.8 0.1 reshape.132
  289.0 0.8 reshape.133
  289.8 3.9 %all-to-all-start.6 = ((f32[32,1,512]{2,1,0:T(1,128)}), f32[32,1,512]{2,1,0:T(1,128)S(1)}, u32[]{:S(2)}, u32[]{:S(2)}) async-start(f32[32,1,512]{2,1,0:T(1,128)} %reshape.133), calls=%async_computation.6 | async-start | bytes 131072 | tf_op jit(solution)/shard_map/all_to_all | solution.py:49
  293.7 2.2 fusion.29
  295.9 6.3 %all-to-all-done.6 = f32[32,1,512]{2,1,0:T(1,128)S(1)} async-done(((f32[32,1,512]{2,1,0:T(1,128)}), f32[32,1,512]{2,1,0:T(1,128)S(1)}, u32[]{:S(2)}, u32[]{:S(2)}) %all-to-all-start.6) | async-done | bytes 65568 | tf_op jit(solution)/shard_map/all_to_all | solution.py:49
  302.2 0.8 reduce.7
  303.0 0.1 reshape.134
  303.1 0.7 copy.90
  (49 shorter events, 0.5 us)
Async XLA Ops:
  7.2 37.1 %copy-start = (bf16[1,1408,512]{2,1,0:T(8,128)(2,1)S(1)}, bf16[1,1408,512]{2,1,0:T(8,128)(2,1)}, u32[]{:S(2)}) copy-start(bf16[1,1408,512]{2,1,0:T(8,128)(2,1)} %param.12) | copy-start | bytes 4325380
  7.2 199.1 %all-reduce.3.cloned.1.call-start = ((), (), s32[]{:S(2)}) async-start(), calls=%async_computation.7 | async-start | bytes 12976128 | tf_op jit(solution)/shard_map/psum | solution.py:104
  44.2 2.8 copy-start.7
  44.2 5.6 %copy-start.9 = (bf16[32,24,512]{2,1,0:T(8,128)(2,1)}, bf16[32,24,512]{2,1,0:T(8,128)(2,1)S(1)}, u32[]{:S(2)}) copy-start(bf16[32,24,512]{2,1,0:T(8,128)(2,1)S(1)} %get-tuple-element.47) | copy-start | bytes 2359300
  44.2 2.8 copy-start.15
  47.0 2.8 copy-start.14
  52.7 0.9 copy-start.1
  52.7 1.0 copy-start.11
  52.7 1.1 copy-start.13
  54.4 12.9 %all-to-all-start = ((f32[8,256,2]{1,2,0:T(2,128)}), f32[8,256,2]{1,2,0:T(2,128)S(1)}, u32[]{:S(2)}, u32[]{:S(2)}) async-start(f32[8,256,2]{1,2,0:T(2,128)} %broadcast_in_dim.26), calls=%async_computation | async-start | bytes 32768 | tf_op jit(solution)/shard_map/all_to_all | solution.py:39
  211.3 1.5 copy-start.2
  211.3 2.0 copy-start.3
  211.3 3.5 %copy-start.5 = (bf16[768,1408]{1,0:T(8,128)(2,1)}, bf16[768,1408]{1,0:T(8,128)(2,1)S(1)}, u32[]{:S(2)}) copy-start(bf16[768,1408]{1,0:T(8,128)(2,1)S(1)} %get-tuple-element.43) | copy-start | bytes 6488068
  213.3 1.5 copy-start.16
  218.2 8.7 %copy-start.6 = (bf16[256,512]{1,0:T(8,128)(2,1)S(1)}, bf16[256,512]{1,0:T(8,128)(2,1)}, u32[]{:S(2)}) copy-start(bf16[256,512]{1,0:T(8,128)(2,1)} %param.8) | copy-start | bytes 786436
  218.2 8.8 %copy-start.8 = (bf16[32,24,512]{2,1,0:T(8,128)(2,1)S(1)}, bf16[32,24,512]{2,1,0:T(8,128)(2,1)}, u32[]{:S(2)}) copy-start(bf16[32,24,512]{2,1,0:T(8,128)(2,1)} %copy-done.7) | copy-start | bytes 2359300
  218.2 30.9 %all-to-all-start.3 = ((bf16[32,24,1024]{2,1,0:T(8,128)(2,1)}), bf16[32,24,1024]{2,1,0:T(8,128)(2,1)}, u32[]{:S(2)}, u32[]{:S(2)}) async-start(bf16[32,24,1024]{2,1,0:T(8,128)(2,1)} %bitcast.7), calls=%async_computation.3 | async-start | bytes 3145728 | tf_op jit(solution)/shard_map/all_to_all | solution.py:119
  226.9 4.2 %copy-start.4 = (bf16[768,1408]{1,0:T(8,128)(2,1)S(1)}, bf16[768,1408]{1,0:T(8,128)(2,1)}, u32[]{:S(2)}) copy-start(bf16[768,1408]{1,0:T(8,128)(2,1)} %copy-done.3) | copy-start | bytes 6488068
  226.9 4.2 %copy-start.10 = (bf16[32,24,512]{2,1,0:T(8,128)(2,1)S(1)}, bf16[32,24,512]{2,1,0:T(8,128)(2,1)}, u32[]{:S(2)}) copy-start(bf16[32,24,512]{2,1,0:T(8,128)(2,1)} %copy-done.9) | copy-start | bytes 2359300
  257.9 15.3 %all-to-all-start.4 = ((f32[8,256,2]{1,2,0:T(2,128)}), f32[8,256,2]{1,2,0:T(2,128)S(1)}, u32[]{:S(2)}, u32[]{:S(2)}) async-start(f32[8,256,2]{1,2,0:T(2,128)} %broadcast_in_dim.30), calls=%async_computation.4 | async-start | bytes 32768 | tf_op jit(solution)/shard_map/all_to_all | solution.py:39
  273.5 20.2 %copy-start.12 = (bf16[512,32]{0,1:T(8,128)(2,1)S(1)}, bf16[512,32]{0,1:T(8,128)(2,1)}, u32[]{:S(2)}) copy-start(bf16[512,32]{0,1:T(8,128)(2,1)} %param.10) | copy-start | bytes 98308
  274.5 12.9 %all-to-all-start.5 = ((f32[32,1,512]{2,1,0:T(1,128)}), f32[32,1,512]{2,1,0:T(1,128)S(1)}, u32[]{:S(2)}, u32[]{:S(2)}) async-start(f32[32,1,512]{2,1,0:T(1,128)} %reshape.131), calls=%async_computation.5 | async-start | bytes 131072 | tf_op jit(solution)/shard_map/all_to_all | solution.py:47
  289.8 12.3 %all-to-all-start.6 = ((f32[32,1,512]{2,1,0:T(1,128)}), f32[32,1,512]{2,1,0:T(1,128)S(1)}, u32[]{:S(2)}, u32[]{:S(2)}) async-start(f32[32,1,512]{2,1,0:T(1,128)} %reshape.133), calls=%async_computation.6 | async-start | bytes 131072 | tf_op jit(solution)/shard_map/all_to_all | solution.py:49
Sparse Core Ops, SparseCore 0:
  52.8 153.4 all-reduce.2

commit v5 on v4

--- a/solution.py
+++ b/solution.py
@@ -76,7 +76,21 @@
     packed = jnp.dot(
         token_hit.astype(jnp.bfloat16), rows_in, preferred_element_type=jnp.float32
     ).astype(jnp.bfloat16)
-    prob_send = jnp.sum(jnp.where(pick_hit, prob_pairs.reshape(-1)[None, :], 0.0), axis=1)
+    pair_prod = prob_pairs[:, 0] * prob_pairs[:, 1]
+    q_hi = pair_prod.astype(jnp.bfloat16).astype(jnp.float32)
+    q_lo = pair_prod - q_hi
+    pick_values = jnp.stack(
+        [
+            prob_pairs.reshape(-1),
+            jnp.repeat(q_hi, pick_count),
+            jnp.repeat(q_lo, pick_count),
+            expert_ids[:, ::-1].reshape(-1).astype(jnp.float32),
+        ],
+        axis=0,
+    )
+    slot_values = jnp.sum(
+        jnp.where(pick_hit[None], pick_values[:, None, :], 0.0), axis=2
+    ).astype(jnp.bfloat16)
     both = lax.all_to_all(
         packed.reshape(experts, capacity, 2 * shard_width),
         "ctx",
@@ -85,7 +99,7 @@
         tiled=True,
     )
     recv_p = lax.all_to_all(
-        prob_send.astype(jnp.bfloat16).reshape(experts, capacity),
+        slot_values.reshape(4, experts, capacity).transpose(1, 0, 2),
         "ctx",
         split_axis=0,
         concat_axis=0,
@@ -94,7 +108,10 @@
     slot_count = both.shape[0] * both.shape[1]
     x_rows = both[:, :, :shard_width].reshape(slot_count, shard_width)
     cot_rows = both[:, :, shard_width:].reshape(slot_count, shard_width)
-    prob_rows = recv_p.reshape(slot_count).astype(jnp.float32)
+    row_values = recv_p.transpose(1, 0, 2).reshape(4, slot_count).astype(jnp.float32)
+    prob_rows = row_values[0]
+    pair_rows = row_values[1] + row_values[2]
+    other_rows = row_values[3].astype(jnp.int32)
     gate_w = w_gate[0]
     up_w = w_up[0]
     down_w = w_down[0]
@@ -116,28 +133,44 @@
     grad_down = contract_rows(scaled, cot_rows).astype(jnp.bfloat16)[None]
     grad_gate = contract_rows(gate_grad, x_rows).astype(jnp.bfloat16)[None]
     grad_up = contract_rows(up_grad, x_rows).astype(jnp.bfloat16)[None]
+    score_rows = head_sum(
+        jnp.sum(cot_rows.astype(jnp.float32) * out_rows.astype(jnp.float32), axis=1)
+    )
+    own = lax.axis_index("ctx")
+    expert_ids_row = jnp.arange(experts, dtype=jnp.int32)[None, :]
+    direction = (expert_ids_row == own).astype(jnp.float32) - (
+        expert_ids_row == other_rows[:, None]
+    ).astype(jnp.float32)
+    router_weight = (pair_rows * score_rows)[:, None] * direction
+    router_part = jnp.dot(
+        x_rows.astype(jnp.float32).T, router_weight, precision=lax.Precision.HIGHEST
+    )
+    s_hi = score_rows.astype(jnp.bfloat16)
+    s_lo = (score_rows - s_hi.astype(jnp.float32)).astype(jnp.bfloat16)
+    extra = jnp.zeros((slot_count, 128), jnp.bfloat16).at[:, 0].set(s_hi).at[:, 1].set(s_lo)
     back_both = lax.all_to_all(
-        jnp.concatenate([out_rows, dx_rows], axis=1).reshape(ctx_count, capacity, 2 * shard_width),
+        jnp.concatenate([out_rows, dx_rows, extra], axis=1).reshape(
+            ctx_count, capacity, 2 * shard_width + 128
+        ),
         "ctx",
         split_axis=0,
         concat_axis=0,
         tiled=True,
     )
+    router_part, back_both = lax.optimization_barrier((router_part, back_both))
+    grad_router = ctx_sum(router_part)
     both_pairs = lax.dot_general(
         pick_hit.astype(jnp.bfloat16),
-        back_both.reshape(experts * capacity, 2 * shard_width),
+        back_both.reshape(experts * capacity, 2 * shard_width + 128),
         (((0,), (0,)), ((), ())),
         preferred_element_type=jnp.float32,
-    ).astype(jnp.bfloat16).reshape(tok_rows, pick_count, 2 * shard_width)
-    out_pairs = both_pairs[:, :, :shard_width]
-    dx_pairs = both_pairs[:, :, shard_width:]
+    ).reshape(tok_rows, pick_count, 2 * shard_width + 128)
+    out_pairs = both_pairs[:, :, :shard_width].astype(jnp.bfloat16)
+    dx_pairs = both_pairs[:, :, shard_width : 2 * shard_width].astype(jnp.bfloat16)
+    score_grad = both_pairs[:, :, 2 * shard_width] + both_pairs[:, :, 2 * shard_width + 1]
     mixed = jnp.sum(prob_pairs[:, :, None] * out_pairs.astype(jnp.float32), axis=1).astype(
         jnp.bfloat16
     )
-    score_part = jnp.sum(
-        cotangent.astype(jnp.float32)[:, None, :] * out_pairs.astype(jnp.float32), axis=2
-    )
-    score_grad = head_sum(score_part)
     logit_lead = prob_pairs[:, 0] * prob_pairs[:, 1] * (score_grad[:, 0] - score_grad[:, 1])
     logit_grad = jnp.stack([logit_lead, -logit_lead], axis=1)
     dense_grad = jnp.sum(logit_grad[:, :, None] * onehot, axis=1)
@@ -147,8 +180,6 @@
     grad_tokens = (
         dx_pairs[:, 0].astype(jnp.float32) + dx_pairs[:, 1].astype(jnp.float32) + router_term
     ).astype(jnp.bfloat16)
-    router_part = jnp.dot(tokens.astype(jnp.float32).T, dense_grad, precision=lax.Precision.HIGHEST)
-    grad_router = ctx_sum(router_part)
     return (mixed, grad_tokens, grad_router, grad_gate, grad_up, grad_down)
 
 

time: 313 us -> 316 us (level)
  blocking collectives: 43.3 us -> 31.3 us
  other arithmetic: 12.9 us -> 18.2 us
  matrix products: 31.4 us -> 35.7 us
    all_to_all x1 -> x0, blocking collectives: 12 us -> none  [local(): lax.all_to_all(prob_send.astype(jnp.bfloat16).reshape(experts, capacity),...]
    all_to_all x1 -> x2, waiting for transfers between devices: 15.4 us -> 22.8 us  [the longest x1 14.2 us: local(): lax.all_to_all(jnp.concatenate([out_rows, dx_rows, extra], axis=1).reshap...]
    psum x1, waiting for transfers between devices: 126 us -> 122 us  [local(): lax.psum((gate_part, up_part, back_part), 'head')]
    dot_general x1, matrix products: 1.51 us -> 4.81 us  [local(): jnp.dot(gate_grad, gate_w, preferred_element_type=jnp.float32)]
    all_to_all x1 -> x2, starting transfers between devices: 8.67 us -> 11.5 us  [the longest x1 7.42 us: local(): lax.all_to_all(jnp.concatenate([out_rows, dx_rows, extra], axis=1).reshap...]
  transfers between devices with their start and end apart: 6 -> 7, of which waited for: 6 -> 7; matrix products, arithmetic and copies ran while one was open for 5% -> 8% of each run, Pallas kernels for 0% -> 0%
where the time goes in v5:
time: 316 us; the launch traced here: 313 us
  waiting for transfers between devices  163 us (52%)
  starting transfers between devices  36.1 us (11%)
  matrix products  35.7 us (11%)
  blocking collectives  31.3 us (10%)
  other arithmetic  18.2 us (6%)
  between operations  14.4 us (5%)
  local copies, waits for them, and re-layouts  14.3 us (5%)
    psum x1, waiting for transfers between devices, local(): lax.psum((gate_part, up_part, back_part), 'head')  122 us
    all_to_all x1, blocking collectives, local(): lax.all_to_all(packed.reshape(experts, capacity, 2 * shard_width), 'ctx',...  31.3 us
    all_to_all x2, starting transfers between devices, head_sum(): lax.all_to_all(spread, 'head', split_axis=0, concat_axis=0, tiled=True)  15.7 us
    all_to_all x1, waiting for transfers between devices, local(): lax.all_to_all(jnp.concatenate([out_rows, dx_rows, extra], axis=1).reshap...  14.2 us
    dot_general x3, matrix products, contract_rows(): lax.dot_general(left, right, (((0,), (0,)), ((), ())), preferred_element_...  9.14 us
    all_to_all x1, waiting for transfers between devices, local(): lax.all_to_all(slot_values.reshape(4, experts, capacity).transpose(1, 0,...  8.6 us
    dot_general x3, matrix products, contract_last(): lax.dot_general(left, right, (((1,), (1,)), ((), ())), preferred_element_...  8.37 us
    all_to_all x1, starting transfers between devices, local(): lax.all_to_all(jnp.concatenate([out_rows, dx_rows, extra], axis=1).reshap...  7.42 us
  transfers between devices with their start and end apart: 7, of which 7 were waited for; matrix products, arithmetic and copies ran while one was open for 8% of the time, Pallas kernels for 0%

profile of v5, /device:TPU:64, one launch (start us, length us, event | category | flops | bytes accessed | tf_op | source)
XLA Modules:
  0.0 313.2 jit_solution(16263275082815167552)
XLA Ops:
  7.2 0.9 copy.79
  8.1 0.1 eq.106
  8.3 0.1 reshape.265
  8.5 1.2 reduce-window.6
  9.6 0.2 slice_reduce_fusion
  10.0 0.1 reduce_sum.88
  10.2 0.7 multiply_add_fusion
  10.9 0.3 fusion.12
  11.2 1.6 convolution_convert_fusion.6
  12.8 31.3 %all_to_all.36 = bf16[32,24,1024]{2,1,0:T(8,128)(2,1)S(1)} all-to-all(bf16[32,24,1024]{2,1,0:T(8,128)(2,1)S(1)} %bitcast.75), channel_id=1, replica_groups=mesh['ctx'=32,'head'=8] {'ctx'}, dimensions={0} | all-to-all | bytes 3145728 | tf_op jit(solution)/shard_map/all_to_all | solution.py:94
  44.2 1.8 copy-done.12
  46.0 2.8 convolution_convert_fusion.1
  48.8 2.8 convolution_convert_fusion.2
  51.6 2.8 convolution_convert_fusion
  54.4 0.9 copy-done.9
  55.3 0.2 fusion.54
  55.6 0.6 broadcast_in_dim.36
  56.2 7.2 %all-to-all-start = ((f32[8,256,2]{1,2,0:T(2,128)}), f32[8,256,2]{1,2,0:T(2,128)S(1)}, u32[]{:S(2)}, u32[]{:S(2)}) async-start(f32[8,256,2]{1,2,0:T(2,128)} %broadcast_in_dim.36), calls=%async_computation | async-start | bytes 32768 | tf_op jit(solution)/shard_map/all_to_all | solution.py:39
  63.4 0.3 iota_compare_fusion
  63.9 0.1 convert_element_type.173
  64.1 5.0 %all-to-all-done = f32[8,256,2]{1,2,0:T(2,128)S(1)} async-done(((f32[8,256,2]{1,2,0:T(2,128)}), f32[8,256,2]{1,2,0:T(2,128)S(1)}, u32[]{:S(2)}, u32[]{:S(2)}) %all-to-all-start) | async-done | bytes 16416 | tf_op jit(solution)/shard_map/all_to_all | solution.py:39
  69.3 0.1 stack_reshape.9
  69.5 0.1 stack_reshape.10
  69.8 0.1 stack_reshape.11
  69.9 1.0 select_reduce_fusion
  71.0 0.6 copy.85
  71.6 4.0 %all-to-all-start.2 = ((bf16[32,4,24]{2,1,0:T(4,128)(2,1)}), bf16[32,4,24]{2,1,0:T(4,128)(2,1)S(1)}, u32[]{:S(2)}, u32[]{:S(2)}) async-start(bf16[32,4,24]{2,1,0:T(4,128)(2,1)} %copy.85), calls=%async_computation.2 | async-start | bytes 65536 | tf_op jit(solution)/shard_map/all_to_all | solution.py:101
  75.7 0.6 compare_reduce_fusion
  76.3 0.6 compare_reduce_fusion.1
  76.9 8.6 %all-to-all-done.2 = bf16[32,4,24]{2,1,0:T(4,128)(2,1)S(1)} async-done(((bf16[32,4,24]{2,1,0:T(4,128)(2,1)}), bf16[32,4,24]{2,1,0:T(4,128)(2,1)S(1)}, u32[]{:S(2)}, u32[]{:S(2)}) %all-to-all-start.2) | async-done | bytes 6176 | tf_op jit(solution)/shard_map/all_to_all | solution.py:101
  85.8 0.3 copy.86
  86.0 121.9 %all-reduce.4.cloned.1.call-done = (bf16[768,1408]{1,0:T(8,128)(2,1)}, bf16[768,1408]{1,0:T(8,128)(2,1)}, bf16[768,1408]{1,0:T(8,128)(2,1)}) async-done(((bf16[768,1408]{1,0:T(8,128)(2,1)}, bf16[768,1408]{1,0:T(8,128)(2,1)}, bf16[768,1408]{1,0:T(8,128)(2,1)}), (bf16[768,1408]{1,0:T(8,128)(2,1)}, bf16[768,1408]{1,0:T(8,128)(2,1)}, bf16[768,1408]{1,0:T(8,128)(2,1)})) %all-reduce.4.cloned.1.call-update) | async-done | bytes 6488080 | tf_op jit(solution)/shard_map/psum | solution.py:121
  207.9 6.1 %fusion.3 = (bf16[768,1408]{1,0:T(8,128)(2,1)}, bf16[768,1408]{1,0:T(8,128)(2,1)S(1)}, bf16[768,1408]{1,0:T(8,128)(2,1)S(1)}) fusion(bf16[768,1408]{1,0:T(8,128)(2,1)} %get-tuple-element.66, bf16[768,1408]{1,0:T(8,128)(2,1)} %get-tuple-element.67, bf16[768,1408]{1,0:T(8,128)(2,1)} %get-tuple-element.68, f32[768]{0:T(1024)S(1)} %mul.126), kind=kLoop, calls=%fused_computation.9 | loop fusion | flops 20545536 | bytes 12979200 | tf_op jit(solution)/shard_map/convert_element_type | solution.py:29
  214.1 2.7 fusion.18
  216.7 2.4 multiply_reduce_fusion
  219.1 0.6 broadcast_in_dim.42
  219.7 8.4 %all-to-all-start.3 = ((f32[8,1,768]{2,1,0:T(1,128)}), f32[8,1,768]{2,1,0:T(1,128)S(1)}, u32[]{:S(2)}, u32[]{:S(2)}) async-start(f32[8,1,768]{2,1,0:T(1,128)} %broadcast_in_dim.42), calls=%async_computation.3 | async-start | bytes 49152 | tf_op jit(solution)/shard_map/all_to_all | solution.py:39
  228.2 4.8 %add_convert_fusion = bf16[768,512]{0,1:T(8,128)(2,1)} fusion(f32[768,512]{0,1:T(8,128)} %fusion.18, bf16[768,1408]{1,0:T(8,128)(2,1)} %get-tuple-element.74, bf16[1,1408,512]{2,1,0:T(8,128)(2,1)} %param.15), kind=kOutput, calls=%fused_computation.29 | convolution fusion | flops 1108082688 | bytes 5963776 | tf_op jit(solution)/shard_map/dot_general | solution.py:128
  233.0 0.7 all-to-all-done.3
  233.7 1.3 broadcast_select_fusion
  235.1 1.5 pad_maximum_fusion
  236.6 2.3 copy.88
  238.9 7.4 %all-to-all-start.4 = ((bf16[32,24,1152]{2,1,0:T(8,128)(2,1)}), bf16[32,24,1152]{2,1,0:T(8,128)(2,1)}, u32[]{:S(2)}, u32[]{:S(2)}) async-start(bf16[32,24,1152]{2,1,0:T(8,128)(2,1)} %bitcast.10), calls=%async_computation.4 | async-start | bytes 3538944 | tf_op jit(solution)/shard_map/all_to_all | solution.py:151
  246.3 0.3 iota_compare_fusion.2
  246.6 0.5 eq.112
  247.4 4.2 %fusion.8 = bf16[1,1408,512]{2,1,0:T(8,128)(2,1)} fusion(bf16[768,1408]{1,0:T(8,128)(2,1)} %get-tuple-element.74, bf16[768,512]{1,0:T(8,128)(2,1)S(1)} %bitcast.78), kind=kOutput, calls=%fused_computation.23 | convolution fusion | flops 1108017152 | bytes 4390912 | tf_op jit(solution)/shard_map/dot_general | solution.py:8
  251.6 2.4 fusion.9
  254.0 2.5 fusion.10
  256.6 0.8 fusion.33
  257.3 14.2 %all-to-all-done.4 = bf16[32,24,1152]{2,1,0:T(8,128)(2,1)} async-done(((bf16[32,24,1152]{2,1,0:T(8,128)(2,1)}), bf16[32,24,1152]{2,1,0:T(8,128)(2,1)}, u32[]{:S(2)}, u32[]{:S(2)}) %all-to-all-start.4) | async-done | bytes 1769504 | tf_op jit(solution)/shard_map/all_to_all | solution.py:151
  271.5 3.7 %fusion.53 = (bf16[256,2,1152]{2,0,1:T(8,128)(2,1)}, f32[256,2,1152]{2,0,1:T(8,128)S(1)}) fusion(bf16[768,1152,1]{1,0,2:T(8,128)(2,1)} %bitcast.12, pred[256,2,768]{2,1,0:T(4,128)(4,1)S(1)} %eq.112), kind=kOutput, calls=%fused_computation.101 | convolution fusion | flops 906559488 | bytes 5701632 | tf_op jit(solution)/shard_map/dot_general | solution.py:162
  275.2 0.2 fusion.37
  275.6 0.8 reshape.301
  276.4 5.1 %all-to-all-start.5 = ((f32[32,1,512]{2,1,0:T(1,128)}), f32[32,1,512]{2,1,0:T(1,128)S(1)}, u32[]{:S(2)}, u32[]{:S(2)}) async-start(f32[32,1,512]{2,1,0:T(1,128)} %reshape.301), calls=%async_computation.5 | async-start | bytes 131072 | tf_op jit(solution)/shard_map/all_to_all | solution.py:47
  281.5 2.2 fusion.29
  283.7 6.3 %all-to-all-done.5 = f32[32,1,512]{2,1,0:T(1,128)S(1)} async-done(((f32[32,1,512]{2,1,0:T(1,128)}), f32[32,1,512]{2,1,0:T(1,128)S(1)}, u32[]{:S(2)}, u32[]{:S(2)}) %all-to-all-start.5) | async-done | bytes 65568 | tf_op jit(solution)/shard_map/all_to_all | solution.py:47
  290.0 0.6 broadcast.210
  290.6 0.8 reduce.33
  291.5 0.8 reshape.303
  292.3 3.9 %all-to-all-start.6 = ((f32[32,1,512]{2,1,0:T(1,128)}), f32[32,1,512]{2,1,0:T(1,128)S(1)}, u32[]{:S(2)}, u32[]{:S(2)}) async-start(f32[32,1,512]{2,1,0:T(1,128)} %reshape.303), calls=%async_computation.6 | async-start | bytes 131072 | tf_op jit(solution)/shard_map/all_to_all | solution.py:49
  296.2 2.0 multiply_reduce_fusion.1
  298.2 6.5 %all-to-all-done.6 = f32[32,1,512]{2,1,0:T(1,128)S(1)} async-done(((f32[32,1,512]{2,1,0:T(1,128)}), f32[32,1,512]{2,1,0:T(1,128)S(1)}, u32[]{:S(2)}, u32[]{:S(2)}) %all-to-all-start.6) | async-done | bytes 65568 | tf_op jit(solution)/shard_map/all_to_all | solution.py:49
  304.7 0.8 reduce.34
  305.6 0.7 copy.91
  (69 shorter events, 2.2 us)
Async XLA Ops:
  7.2 44.5 %copy-start = (bf16[1,1408,512]{2,1,0:T(8,128)(2,1)S(1)}, bf16[1,1408,512]{2,1,0:T(8,128)(2,1)}, u32[]{:S(2)}) copy-start(bf16[1,1408,512]{2,1,0:T(8,128)(2,1)} %param.17) | copy-start | bytes 4325380
  7.2 200.7 %all-reduce.4.cloned.1.call-start = ((), (), s32[]{:S(2)}) async-start(), calls=%async_computation.7 | async-start | bytes 12976128 | tf_op jit(solution)/shard_map/psum | solution.py:121
  44.1 1.9 copy-start.12
  44.2 4.6 %copy-start.1 = (bf16[32,24,512]{2,1,0:T(8,128)(2,1)}, bf16[32,24,512]{2,1,0:T(8,128)(2,1)S(1)}, u32[]{:S(2)}) copy-start(bf16[32,24,512]{2,1,0:T(8,128)(2,1)S(1)} %get-tuple-element.78) | copy-start | bytes 2359300
  44.2 41.6 %copy-start.3 = (bf16[32,24,512]{2,1,0:T(8,128)(2,1)}, bf16[32,24,512]{2,1,0:T(8,128)(2,1)S(1)}, u32[]{:S(2)}) copy-start(bf16[32,24,512]{2,1,0:T(8,128)(2,1)S(1)} %get-tuple-element.77) | copy-start | bytes 2359300
  46.0 2.8 copy-start.14
  54.4 0.9 copy-start.9
  54.4 1.0 copy-start.11
  54.4 1.1 copy-start.10
  56.2 12.9 %all-to-all-start = ((f32[8,256,2]{1,2,0:T(2,128)}), f32[8,256,2]{1,2,0:T(2,128)S(1)}, u32[]{:S(2)}, u32[]{:S(2)}) async-start(f32[8,256,2]{1,2,0:T(2,128)} %broadcast_in_dim.36), calls=%async_computation | async-start | bytes 32768 | tf_op jit(solution)/shard_map/all_to_all | solution.py:39
  71.6 13.9 %all-to-all-start.2 = ((bf16[32,4,24]{2,1,0:T(4,128)(2,1)}), bf16[32,4,24]{2,1,0:T(4,128)(2,1)S(1)}, u32[]{:S(2)}, u32[]{:S(2)}) async-start(bf16[32,4,24]{2,1,0:T(4,128)(2,1)} %copy.85), calls=%async_computation.2 | async-start | bytes 65536 | tf_op jit(solution)/shard_map/all_to_all | solution.py:101
  207.9 6.1 %copy-start.13 = (bf16[1,1408,512]{2,1,0:T(8,128)(2,1)S(1)}, bf16[1,1408,512]{2,1,0:T(8,128)(2,1)}, u32[]{:S(2)}) copy-start(bf16[1,1408,512]{2,1,0:T(8,128)(2,1)} %param.16) | copy-start | bytes 4325380
  214.1 2.7 copy-start.7
  214.1 2.7 copy-start.5
  219.7 14.0 %all-to-all-start.3 = ((f32[8,1,768]{2,1,0:T(1,128)}), f32[8,1,768]{2,1,0:T(1,128)S(1)}, u32[]{:S(2)}, u32[]{:S(2)}) async-start(f32[8,1,768]{2,1,0:T(1,128)} %broadcast_in_dim.42), calls=%async_computation.3 | async-start | bytes 49152 | tf_op jit(solution)/shard_map/all_to_all | solution.py:39
  238.9 8.5 %copy-start.2 = (bf16[32,24,512]{2,1,0:T(8,128)(2,1)S(1)}, bf16[32,24,512]{2,1,0:T(8,128)(2,1)}, u32[]{:S(2)}) copy-start(bf16[32,24,512]{2,1,0:T(8,128)(2,1)} %copy-done.1) | copy-start | bytes 2359300
  238.9 32.6 %all-to-all-start.4 = ((bf16[32,24,1152]{2,1,0:T(8,128)(2,1)}), bf16[32,24,1152]{2,1,0:T(8,128)(2,1)}, u32[]{:S(2)}, u32[]{:S(2)}) async-start(bf16[32,24,1152]{2,1,0:T(8,128)(2,1)} %bitcast.10), calls=%async_computation.4 | async-start | bytes 3538944 | tf_op jit(solution)/shard_map/all_to_all | solution.py:151
  247.4 4.2 %copy-start.8 = (bf16[768,1408]{1,0:T(8,128)(2,1)S(1)}, bf16[768,1408]{1,0:T(8,128)(2,1)}, u32[]{:S(2)}) copy-start(bf16[768,1408]{1,0:T(8,128)(2,1)} %copy-done.7) | copy-start | bytes 6488068
  251.6 2.4 copy-start.4
  251.6 2.4 copy-start.6
  276.4 13.6 %all-to-all-start.5 = ((f32[32,1,512]{2,1,0:T(1,128)}), f32[32,1,512]{2,1,0:T(1,128)S(1)}, u32[]{:S(2)}, u32[]{:S(2)}) async-start(f32[32,1,512]{2,1,0:T(1,128)} %reshape.301), calls=%async_computation.5 | async-start | bytes 131072 | tf_op jit(solution)/shard_map/all_to_all | solution.py:47
  292.3 12.3 %all-to-all-start.6 = ((f32[32,1,512]{2,1,0:T(1,128)}), f32[32,1,512]{2,1,0:T(1,128)S(1)}, u32[]{:S(2)}, u32[]{:S(2)}) async-start(f32[32,1,512]{2,1,0:T(1,128)} %reshape.303), calls=%async_computation.6 | async-start | bytes 131072 | tf_op jit(solution)/shard_map/all_to_all | solution.py:49
Sparse Core Ops, SparseCore 0:
  54.5 153.3 all-reduce.3

commit v6 on v5

--- a/solution.py
+++ b/solution.py
@@ -122,7 +122,8 @@
     gate_pre = gate_sum.astype(jnp.float32)
     up_pre = up_sum.astype(jnp.float32)
     hidden = forward_act(gate_pre, up_pre)
-    gate_grad, up_grad = backward_act(gate_pre, up_pre, back_sum.astype(jnp.float32), prob_rows)
+    back_proj = back_sum.astype(jnp.float32)
+    gate_grad, up_grad = backward_act(gate_pre, up_pre, back_proj, prob_rows)
     out_rows = jnp.dot(hidden, down_w, preferred_element_type=jnp.float32).astype(jnp.bfloat16)
     dx_rows = (
         jnp.dot(gate_grad, gate_w, preferred_element_type=jnp.float32)
@@ -133,9 +134,7 @@
     grad_down = contract_rows(scaled, cot_rows).astype(jnp.bfloat16)[None]
     grad_gate = contract_rows(gate_grad, x_rows).astype(jnp.bfloat16)[None]
     grad_up = contract_rows(up_grad, x_rows).astype(jnp.bfloat16)[None]
-    score_rows = head_sum(
-        jnp.sum(cot_rows.astype(jnp.float32) * out_rows.astype(jnp.float32), axis=1)
-    )
+    score_rows = jnp.sum(hidden.astype(jnp.float32) * back_proj, axis=1)
     own = lax.axis_index("ctx")
     expert_ids_row = jnp.arange(experts, dtype=jnp.int32)[None, :]
     direction = (expert_ids_row == own).astype(jnp.float32) - (
@@ -157,7 +156,6 @@
         concat_axis=0,
         tiled=True,
     )
-    router_part, back_both = lax.optimization_barrier((router_part, back_both))
     grad_router = ctx_sum(router_part)
     both_pairs = lax.dot_general(
         pick_hit.astype(jnp.bfloat16),

time: 316 us -> 303 us (0.959)
  waiting for transfers between devices: 163 us -> 158 us
    reduce_sum x0 -> x1, other arithmetic: none -> 8.56 us  [local(): score_rows = jnp.sum(hidden.astype(jnp.float32) * back_proj, axis=1)]
    all_to_all x2 -> x1, starting transfers between devices: 15.7 us -> 7.22 us  [head_sum(): lax.all_to_all(spread, 'head', split_axis=0, concat_axis=0, tiled=True)]
    all_to_all x1, waiting for transfers between devices: 6.32 us -> 0.01 us  [ctx_sum(): lax.all_to_all(pieces, 'ctx', split_axis=0, concat_axis=0, tiled=True)]
    convert_element_type x1 -> x0, other arithmetic: 6.14 us -> none  [backward_act(): (hidden_grad * up_pre * sigma * (1.0 + gate_pre * (1.0 - sigma))).astype(...]
    all_to_all x1, starting transfers between devices: 3.86 us -> 8.3 us  [ctx_sum(): lax.all_to_all(spread, 'ctx', split_axis=0, concat_axis=0, tiled=True)]
    all_to_all x1, waiting for transfers between devices: 14.2 us -> 18.5 us  [local(): lax.all_to_all(jnp.concatenate([out_rows, dx_rows, extra], axis=1).reshap...]
    all_to_all x1, starting transfers between devices: 5.1 us -> 8.48 us  [ctx_sum(): lax.all_to_all(pieces, 'ctx', split_axis=0, concat_axis=0, tiled=True)]
  transfers between devices with their start and end apart: 7 -> 6, of which waited for: 7 -> 5; matrix products, arithmetic and copies ran while one was open for 8% -> 10% of each run, Pallas kernels for 0% -> 0%
where the time goes in v6:
time: 303 us; the launch traced here: 302 us
  waiting for transfers between devices  158 us (52%)
  matrix products  33.8 us (11%)
  starting transfers between devices  33.1 us (11%)
  blocking collectives  31.3 us (10%)
  other arithmetic  19.5 us (6%)
  between operations  14.5 us (5%)
  local copies, waits for them, and re-layouts  11.7 us (4%)
    psum x1, waiting for transfers between devices, local(): lax.psum((gate_part, up_part, back_part), 'head')  122 us
    all_to_all x1, blocking collectives, local(): lax.all_to_all(packed.reshape(experts, capacity, 2 * shard_width), 'ctx',...  31.3 us
    all_to_all x1, waiting for transfers between devices, local(): lax.all_to_all(jnp.concatenate([out_rows, dx_rows, extra], axis=1).reshap...  18.5 us
    dot_general x3, matrix products, contract_rows(): lax.dot_general(left, right, (((0,), (0,)), ((), ())), preferred_element_...  9.13 us
    all_to_all x1, waiting for transfers between devices, local(): lax.all_to_all(slot_values.reshape(4, experts, capacity).transpose(1, 0,...  8.57 us
    reduce_sum x1, other arithmetic, local(): score_rows = jnp.sum(hidden.astype(jnp.float32) * back_proj, axis=1)  8.56 us
    all_to_all x1, starting transfers between devices, ctx_sum(): lax.all_to_all(pieces, 'ctx', split_axis=0, concat_axis=0, tiled=True)  8.48 us
    all_to_all x1, starting transfers between devices, ctx_sum(): lax.all_to_all(spread, 'ctx', split_axis=0, concat_axis=0, tiled=True)  8.3 us
  transfers between devices with their start and end apart: 6, of which 5 were waited for; matrix products, arithmetic and copies ran while one was open for 10% of the time, Pallas kernels for 0%

profile of v6, /device:TPU:64, one launch (start us, length us, event | category | flops | bytes accessed | tf_op | source)
XLA Modules:
  0.0 302.3 jit_solution(13956387580562348560)
XLA Ops:
  7.2 0.9 copy.61
  8.1 0.1 eq.106
  8.3 0.1 reshape.258
  8.5 1.2 reduce-window.6
  9.6 0.2 slice_reduce_fusion
  9.9 0.1 fusion.43
  10.0 0.1 reduce_sum.79
  10.2 0.7 multiply_add_fusion
  10.9 0.3 fusion.15
  11.2 1.6 convolution_convert_fusion.6
  12.8 31.3 %all_to_all.30 = bf16[32,24,1024]{2,1,0:T(8,128)(2,1)S(1)} all-to-all(bf16[32,24,1024]{2,1,0:T(8,128)(2,1)S(1)} %bitcast.78), channel_id=1, replica_groups=mesh['ctx'=32,'head'=8] {'ctx'}, dimensions={0} | all-to-all | bytes 3145728 | tf_op jit(solution)/shard_map/all_to_all | solution.py:94
  44.2 2.7 convolution_convert_fusion.1
  47.0 2.8 convolution_convert_fusion.2
  49.8 2.8 convolution_convert_fusion
  52.6 0.9 copy-done.7
  53.5 0.2 fusion.59
  53.7 0.6 broadcast_in_dim.34
  54.3 7.2 %all-to-all-start = ((f32[8,256,2]{1,2,0:T(2,128)}), f32[8,256,2]{1,2,0:T(2,128)S(1)}, u32[]{:S(2)}, u32[]{:S(2)}) async-start(f32[8,256,2]{1,2,0:T(2,128)} %broadcast_in_dim.34), calls=%async_computation | async-start | bytes 32768 | tf_op jit(solution)/shard_map/all_to_all | solution.py:39
  61.5 0.3 iota_compare_fusion
  61.9 0.1 copy.66
  62.1 0.1 convert_element_type.176
  62.2 5.0 %all-to-all-done = f32[8,256,2]{1,2,0:T(2,128)S(1)} async-done(((f32[8,256,2]{1,2,0:T(2,128)}), f32[8,256,2]{1,2,0:T(2,128)S(1)}, u32[]{:S(2)}, u32[]{:S(2)}) %all-to-all-start) | async-done | bytes 16416 | tf_op jit(solution)/shard_map/all_to_all | solution.py:39
  67.3 0.1 copy.65
  67.4 0.1 stack_reshape.9
  67.7 0.1 stack_reshape.10
  67.9 0.1 stack_reshape.11
  68.1 1.0 select_reduce_fusion
  69.1 0.6 copy.67
  69.8 4.0 %all-to-all-start.2 = ((bf16[32,4,24]{2,1,0:T(4,128)(2,1)}), bf16[32,4,24]{2,1,0:T(4,128)(2,1)S(1)}, u32[]{:S(2)}, u32[]{:S(2)}) async-start(bf16[32,4,24]{2,1,0:T(4,128)(2,1)} %copy.67), calls=%async_computation.2 | async-start | bytes 65536 | tf_op jit(solution)/shard_map/all_to_all | solution.py:101
  73.8 0.6 compare_reduce_fusion
  74.5 0.6 compare_reduce_fusion.1
  75.1 8.6 %all-to-all-done.2 = bf16[32,4,24]{2,1,0:T(4,128)(2,1)S(1)} async-done(((bf16[32,4,24]{2,1,0:T(4,128)(2,1)}), bf16[32,4,24]{2,1,0:T(4,128)(2,1)S(1)}, u32[]{:S(2)}, u32[]{:S(2)}) %all-to-all-start.2) | async-done | bytes 6176 | tf_op jit(solution)/shard_map/all_to_all | solution.py:101
  84.1 0.3 copy.70
  84.4 121.6 %all-reduce.4.cloned.1.call-done = (bf16[768,1408]{1,0:T(8,128)(2,1)}, bf16[768,1408]{1,0:T(8,128)(2,1)}, bf16[768,1408]{1,0:T(8,128)(2,1)}) async-done(((bf16[768,1408]{1,0:T(8,128)(2,1)}, bf16[768,1408]{1,0:T(8,128)(2,1)}, bf16[768,1408]{1,0:T(8,128)(2,1)}), (bf16[768,1408]{1,0:T(8,128)(2,1)}, bf16[768,1408]{1,0:T(8,128)(2,1)}, bf16[768,1408]{1,0:T(8,128)(2,1)})) %all-reduce.4.cloned.1.call-update) | async-done | bytes 6488080 | tf_op jit(solution)/shard_map/psum | solution.py:121
  206.1 8.6 %fusion.6 = (f32[768]{0:T(1024)S(1)}, bf16[768,1408]{1,0:T(8,128)(2,1)}, bf16[768,1408]{1,0:T(8,128)(2,1)}, bf16[768,1408]{1,0:T(8,128)(2,1)S(1)}) fusion(bf16[768,1408]{1,0:T(8,128)(2,1)} %get-tuple-element.56, bf16[768,1408]{1,0:T(8,128)(2,1)} %get-tuple-element.57, bf16[768,1408]{1,0:T(8,128)(2,1)} %get-tuple-element.58, f32[768]{0:T(1024)S(1)} %mul.122), kind=kLoop, calls=%fused_computation.14 | loop fusion | flops 23788800 | bytes 12982272 | tf_op jit(solution)/shard_map/reduce_sum | solution.py:137
  214.6 2.6 fusion.21
  217.3 0.8 fusion.37
  218.1 0.8 reshape.294
  218.9 8.5 %all-to-all-start.4 = ((f32[32,1,512]{2,1,0:T(1,128)}), f32[32,1,512]{2,1,0:T(1,128)S(1)}, u32[]{:S(2)}, u32[]{:S(2)}) async-start(f32[32,1,512]{2,1,0:T(1,128)} %reshape.294), calls=%async_computation.4 | async-start | bytes 131072 | tf_op jit(solution)/shard_map/all_to_all | solution.py:47
  227.4 5.0 %add_convert_fusion = bf16[768,512]{0,1:T(8,128)(2,1)} fusion(f32[768,512]{0,1:T(8,128)} %fusion.21, bf16[768,1408]{1,0:T(8,128)(2,1)} %get-tuple-element.66, bf16[1,1408,512]{2,1,0:T(8,128)(2,1)} %param.15), kind=kOutput, calls=%fused_computation.32 | convolution fusion | flops 1108082688 | bytes 5963776 | tf_op jit(solution)/shard_map/dot_general | solution.py:129
  232.4 2.4 fusion.27
  234.8 1.3 broadcast_select_fusion
  236.2 0.5 broadcast.208
  236.7 0.8 reduce.32
  237.5 0.1 reshape.295
  237.7 0.8 reshape.296
  238.5 8.3 %all-to-all-start.5 = ((f32[32,1,512]{2,1,0:T(1,128)}), f32[32,1,512]{2,1,0:T(1,128)S(1)}, u32[]{:S(2)}, u32[]{:S(2)}) async-start(f32[32,1,512]{2,1,0:T(1,128)} %reshape.296), calls=%async_computation.5 | async-start | bytes 131072 | tf_op jit(solution)/shard_map/all_to_all | solution.py:49
  246.8 1.5 pad_maximum_fusion
  248.3 2.3 copy.68
  250.5 4.7 %all-to-all-done.5 = f32[32,1,512]{2,1,0:T(1,128)S(1)} async-done(((f32[32,1,512]{2,1,0:T(1,128)}), f32[32,1,512]{2,1,0:T(1,128)S(1)}, u32[]{:S(2)}, u32[]{:S(2)}) %all-to-all-start.5) | async-done | bytes 65568 | tf_op jit(solution)/shard_map/all_to_all | solution.py:49
  255.3 5.1 %all-to-all-start.3 = ((bf16[32,24,1152]{2,1,0:T(8,128)(2,1)}), bf16[32,24,1152]{2,1,0:T(8,128)(2,1)}, u32[]{:S(2)}, u32[]{:S(2)}) async-start(bf16[32,24,1152]{2,1,0:T(8,128)(2,1)} %bitcast.10), calls=%async_computation.3 | async-start | bytes 3538944 | tf_op jit(solution)/shard_map/all_to_all | solution.py:150
  260.3 0.3 iota_compare_fusion.2
  260.6 0.5 eq.112
  261.2 4.2 %fusion.11 = bf16[1,1408,512]{2,1,0:T(8,128)(2,1)} fusion(bf16[768,1408]{1,0:T(8,128)(2,1)} %get-tuple-element.66, bf16[768,512]{1,0:T(8,128)(2,1)S(1)} %bitcast.82), kind=kOutput, calls=%fused_computation.26 | convolution fusion | flops 1108017152 | bytes 4390912 | tf_op jit(solution)/shard_map/dot_general | solution.py:8
  265.4 2.4 fusion.12
  267.8 2.5 fusion.13
  270.3 0.8 reduce.33
  271.1 0.1 reshape.297
  271.2 0.7 copy.71
  272.0 18.5 %all-to-all-done.3 = bf16[32,24,1152]{2,1,0:T(8,128)(2,1)} async-done(((bf16[32,24,1152]{2,1,0:T(8,128)(2,1)}), bf16[32,24,1152]{2,1,0:T(8,128)(2,1)}, u32[]{:S(2)}, u32[]{:S(2)}) %all-to-all-start.3) | async-done | bytes 1769504 | tf_op jit(solution)/shard_map/all_to_all | solution.py:150
  290.5 2.7 fusion.58
  293.2 0.2 fusion.36
  293.5 0.9 multiply_reduce_fusion
  294.3 1.1 fusion.32
  (64 shorter events, 1.4 us)
Async XLA Ops:
  7.2 37.0 %copy-start = (bf16[1,1408,512]{2,1,0:T(8,128)(2,1)S(1)}, bf16[1,1408,512]{2,1,0:T(8,128)(2,1)}, u32[]{:S(2)}) copy-start(bf16[1,1408,512]{2,1,0:T(8,128)(2,1)} %param.16) | copy-start | bytes 4325380
  7.2 198.9 %all-reduce.4.cloned.1.call-start = ((), (), s32[]{:S(2)}) async-start(), calls=%async_computation.6 | async-start | bytes 12976128 | tf_op jit(solution)/shard_map/psum | solution.py:121
  44.2 5.6 %copy-start.8 = (bf16[32,24,512]{2,1,0:T(8,128)(2,1)}, bf16[32,24,512]{2,1,0:T(8,128)(2,1)S(1)}, u32[]{:S(2)}) copy-start(bf16[32,24,512]{2,1,0:T(8,128)(2,1)S(1)} %get-tuple-element.69) | copy-start | bytes 2359300
  44.2 39.9 %copy-start.1 = (bf16[32,24,512]{2,1,0:T(8,128)(2,1)}, bf16[32,24,512]{2,1,0:T(8,128)(2,1)S(1)}, u32[]{:S(2)}) copy-start(bf16[32,24,512]{2,1,0:T(8,128)(2,1)S(1)} %get-tuple-element.68) | copy-start | bytes 2359300
  44.2 2.8 copy-start.12
  47.0 2.8 copy-start.13
  52.5 0.9 copy-start.7
  52.5 1.0 copy-start.11
  52.5 1.1 copy-start.10
  54.3 12.9 %all-to-all-start = ((f32[8,256,2]{1,2,0:T(2,128)}), f32[8,256,2]{1,2,0:T(2,128)S(1)}, u32[]{:S(2)}, u32[]{:S(2)}) async-start(f32[8,256,2]{1,2,0:T(2,128)} %broadcast_in_dim.34), calls=%async_computation | async-start | bytes 32768 | tf_op jit(solution)/shard_map/all_to_all | solution.py:39
  69.8 13.9 %all-to-all-start.2 = ((bf16[32,4,24]{2,1,0:T(4,128)(2,1)}), bf16[32,4,24]{2,1,0:T(4,128)(2,1)S(1)}, u32[]{:S(2)}, u32[]{:S(2)}) async-start(bf16[32,4,24]{2,1,0:T(4,128)(2,1)} %copy.67), calls=%async_computation.2 | async-start | bytes 65536 | tf_op jit(solution)/shard_map/all_to_all | solution.py:101
  214.6 2.6 copy-start.5
  218.9 17.3 %all-to-all-start.4 = ((f32[32,1,512]{2,1,0:T(1,128)}), f32[32,1,512]{2,1,0:T(1,128)S(1)}, u32[]{:S(2)}, u32[]{:S(2)}) async-start(f32[32,1,512]{2,1,0:T(1,128)} %reshape.294), calls=%async_computation.4 | async-start | bytes 131072 | tf_op jit(solution)/shard_map/all_to_all | solution.py:47
  227.4 5.0 %copy-start.3 = (bf16[768,1408]{1,0:T(8,128)(2,1)S(1)}, bf16[768,1408]{1,0:T(8,128)(2,1)}, u32[]{:S(2)}) copy-start(bf16[768,1408]{1,0:T(8,128)(2,1)} %get-tuple-element.65) | copy-start | bytes 6488068
  227.4 5.0 %copy-start.14 = (bf16[1,1408,512]{2,1,0:T(8,128)(2,1)S(1)}, bf16[1,1408,512]{2,1,0:T(8,128)(2,1)}, u32[]{:S(2)}) copy-start(bf16[1,1408,512]{2,1,0:T(8,128)(2,1)} %param.17) | copy-start | bytes 4325380
  238.5 16.8 %all-to-all-start.5 = ((f32[32,1,512]{2,1,0:T(1,128)}), f32[32,1,512]{2,1,0:T(1,128)S(1)}, u32[]{:S(2)}, u32[]{:S(2)}) async-start(f32[32,1,512]{2,1,0:T(1,128)} %reshape.296), calls=%async_computation.5 | async-start | bytes 131072 | tf_op jit(solution)/shard_map/all_to_all | solution.py:49
  255.3 5.9 %copy-start.2 = (bf16[32,24,512]{2,1,0:T(8,128)(2,1)S(1)}, bf16[32,24,512]{2,1,0:T(8,128)(2,1)}, u32[]{:S(2)}) copy-start(bf16[32,24,512]{2,1,0:T(8,128)(2,1)} %copy-done.1) | copy-start | bytes 2359300
  255.3 35.2 %all-to-all-start.3 = ((bf16[32,24,1152]{2,1,0:T(8,128)(2,1)}), bf16[32,24,1152]{2,1,0:T(8,128)(2,1)}, u32[]{:S(2)}, u32[]{:S(2)}) async-start(bf16[32,24,1152]{2,1,0:T(8,128)(2,1)} %bitcast.10), calls=%async_computation.3 | async-start | bytes 3538944 | tf_op jit(solution)/shard_map/all_to_all | solution.py:150
  261.2 4.2 %copy-start.6 = (bf16[768,1408]{1,0:T(8,128)(2,1)S(1)}, bf16[768,1408]{1,0:T(8,128)(2,1)}, u32[]{:S(2)}) copy-start(bf16[768,1408]{1,0:T(8,128)(2,1)} %copy-done.5) | copy-start | bytes 6488068
  265.4 2.4 copy-start.4
  265.4 2.4 copy-start.9
Sparse Core Ops, SparseCore 0:
  52.7 153.3 all-reduce.3

commit v7 on v6

--- a/solution.py
+++ b/solution.py
@@ -106,9 +106,19 @@
         tiled=True,
     )
     slot_count = both.shape[0] * both.shape[1]
-    x_rows = both[:, :, :shard_width].reshape(slot_count, shard_width)
-    cot_rows = both[:, :, shard_width:].reshape(slot_count, shard_width)
-    row_values = recv_p.transpose(1, 0, 2).reshape(4, slot_count).astype(jnp.float32)
+    half = slot_count // 2
+    swapped = lax.axis_index("head") % 2 == 1
+
+    def local_order(rows):
+        turned = jnp.concatenate([rows[half:], rows[:half]], axis=0)
+        return jnp.where(swapped, turned, rows)
+
+    both = local_order(both.reshape(slot_count, 2 * shard_width))
+    x_rows = both[:, :shard_width]
+    cot_rows = both[:, shard_width:]
+    row_values = local_order(
+        recv_p.transpose(0, 2, 1).reshape(slot_count, 4)
+    ).T.astype(jnp.float32)
     prob_rows = row_values[0]
     pair_rows = row_values[1] + row_values[2]
     other_rows = row_values[3].astype(jnp.int32)
@@ -118,7 +128,17 @@
     gate_part = contract_last(x_rows, gate_w).astype(jnp.bfloat16)
     up_part = contract_last(x_rows, up_w).astype(jnp.bfloat16)
     back_part = contract_last(cot_rows, down_w).astype(jnp.bfloat16)
-    gate_sum, up_sum, back_sum = lax.psum((gate_part, up_part, back_part), "head")
+    head_count = lax.axis_size("head")
+    partner = [(i, i ^ 1) for i in range(head_count)]
+    same_core = [list(range(c, head_count, 2)) for c in range(2)]
+    parts = jnp.stack([gate_part, up_part, back_part])
+    pair_sum = (
+        parts[:, :half].astype(jnp.float32)
+        + lax.ppermute(parts[:, half:], "head", partner).astype(jnp.float32)
+    ).astype(jnp.bfloat16)
+    mine = lax.psum(pair_sum, "head", axis_index_groups=same_core)
+    sums = jnp.concatenate([mine, lax.ppermute(mine, "head", partner)], axis=1)
+    gate_sum, up_sum, back_sum = sums[0], sums[1], sums[2]
     gate_pre = gate_sum.astype(jnp.float32)
     up_pre = up_sum.astype(jnp.float32)
     hidden = forward_act(gate_pre, up_pre)
@@ -148,7 +168,7 @@
     s_lo = (score_rows - s_hi.astype(jnp.float32)).astype(jnp.bfloat16)
     extra = jnp.zeros((slot_count, 128), jnp.bfloat16).at[:, 0].set(s_hi).at[:, 1].set(s_lo)
     back_both = lax.all_to_all(
-        jnp.concatenate([out_rows, dx_rows, extra], axis=1).reshape(
+        local_order(jnp.concatenate([out_rows, dx_rows, extra], axis=1)).reshape(
             ctx_count, capacity, 2 * shard_width + 128
         ),
         "ctx",

time: 303 us -> 318 us (1.050)
  waiting for transfers between devices: 158 us -> 195 us
  blocking collectives: 31.3 us -> 0 us
  local copies, waits for them, and re-layouts: 11.7 us -> 16.9 us
  matrix products: 33.8 us -> 29.9 us
  other arithmetic: 19.5 us -> 23.1 us
    all_to_all x1 -> x0, blocking collectives: 31.3 us -> none  [local(): lax.all_to_all(packed.reshape(experts, capacity, 2 * shard_width), 'ctx',...]
    psum x1, waiting for transfers between devices: 122 us -> 135 us  [local(): mine = lax.psum(pair_sum, 'head', axis_index_groups=same_core)]
    all_to_all x1 -> x2, waiting for transfers between devices: 18.5 us -> 30 us  [the longest x1 22.9 us: local(): lax.all_to_all(packed.reshape(experts, capacity, 2 * shard_width), 'ctx',...]
    all_to_all x1 -> x2, starting transfers between devices: 5.07 us -> 13.6 us  [the longest x1 8.68 us: local(): lax.all_to_all(packed.reshape(experts, capacity, 2 * shard_width), 'ctx',...]
    all_to_all x1, waiting for transfers between devices: 0.01 us -> 8.3 us  [ctx_sum(): lax.all_to_all(pieces, 'ctx', split_axis=0, concat_axis=0, tiled=True)]
    ppermute x0 -> x2, waiting for transfers between devices: none -> 5.79 us  [the longest x1 5.79 us: local(): lax.ppermute(parts[:, half:], 'head', partner).astype(jnp.float32)]
    reduce_sum x1, other arithmetic: 8.56 us -> 3.35 us  [local(): score_rows = jnp.sum(hidden.astype(jnp.float32) * back_proj, axis=1)]
    all_to_all x1, starting transfers between devices: 8.3 us -> 3.86 us  [ctx_sum(): lax.all_to_all(spread, 'ctx', split_axis=0, concat_axis=0, tiled=True)]
  transfers between devices with their start and end apart: 6 -> 9, of which waited for: 5 -> 8; matrix products, arithmetic and copies ran while one was open for 10% -> 8% of each run, Pallas kernels for 0% -> 0%
where the time goes in v7:
time: 318 us; the launch traced here: 315 us
  waiting for transfers between devices  195 us (61%)
  starting transfers between devices  35 us (11%)
  matrix products  29.9 us (9%)
  other arithmetic  23.1 us (7%)
  local copies, waits for them, and re-layouts  16.9 us (5%)
  between operations  14.7 us (5%)
    psum x1, waiting for transfers between devices, local(): mine = lax.psum(pair_sum, 'head', axis_index_groups=same_core)  135 us
    all_to_all x1, waiting for transfers between devices, local(): lax.all_to_all(packed.reshape(experts, capacity, 2 * shard_width), 'ctx',...  22.9 us
    dot_general x3, matrix products, contract_rows(): lax.dot_general(left, right, (((0,), (0,)), ((), ())), preferred_element_...  11.6 us
    all_to_all x1, starting transfers between devices, local(): lax.all_to_all(packed.reshape(experts, capacity, 2 * shard_width), 'ctx',...  8.68 us
    all_to_all x1, waiting for transfers between devices, ctx_sum(): lax.all_to_all(pieces, 'ctx', split_axis=0, concat_axis=0, tiled=True)  8.3 us
    all_to_all x1, starting transfers between devices, local(): lax.all_to_all(slot_values.reshape(4, experts, capacity).transpose(1, 0,...  8.08 us
    unnamed x59, local copies, waits for them, and re-layouts  7.95 us
    all_to_all x1, waiting for transfers between devices, local(): lax.all_to_all(local_order(jnp.concatenate([out_rows, dx_rows, extra], ax...  7.06 us
  transfers between devices with their start and end apart: 9, of which 8 were waited for; matrix products, arithmetic and copies ran while one was open for 8% of the time, Pallas kernels for 0%

profile of v7, /device:TPU:64, one launch (start us, length us, event | category | flops | bytes accessed | tf_op | source)
XLA Modules:
  0.0 315.0 jit_solution(543044834666939551)
XLA Ops:
  7.2 0.9 copy.83
  8.4 1.2 reduce-window.6
  10.2 0.7 multiply_add_fusion
  10.9 0.3 fusion.49
  11.2 2.8 convolution_convert_fusion.6
  13.9 8.7 %all-to-all-start.1 = ((bf16[32,24,1024]{2,1,0:T(8,128)(2,1)}), bf16[32,24,1024]{2,1,0:T(8,128)(2,1)S(1)}, u32[]{:S(2)}, u32[]{:S(2)}) async-start(bf16[32,24,1024]{2,1,0:T(8,128)(2,1)} %bitcast.160), calls=%async_computation.1 | async-start | bytes 3145728 | tf_op jit(solution)/shard_map/all_to_all | solution.py:94
  22.7 22.9 %all-to-all-done.1 = bf16[32,24,1024]{2,1,0:T(8,128)(2,1)S(1)} async-done(((bf16[32,24,1024]{2,1,0:T(8,128)(2,1)}), bf16[32,24,1024]{2,1,0:T(8,128)(2,1)S(1)}, u32[]{:S(2)}, u32[]{:S(2)}) %all-to-all-start.1) | async-done | bytes 1572896 | tf_op jit(solution)/shard_map/all_to_all | solution.py:94
  45.7 0.8 maximum_select_fusion.1
  46.6 0.5 copy-done.21
  47.1 1.4 fusion.28
  48.5 0.5 copy-done.19
  49.0 1.4 fusion.29
  50.5 1.4 fusion.30
  51.9 0.9 pad_maximum_fusion
  52.8 0.2 slice.175
  53.2 5.8 %collective-permute-done = bf16[3,384,1408]{2,1,0:T(8,128)(2,1)S(1)} collective-permute-done((bf16[3,384,1408]{2,1,0:T(8,128)(2,1)S(1)}, bf16[3,384,1408]{2,1,0:T(8,128)(2,1)S(1)}, u32[]{:S(2)}, u32[]{:S(2)}) %collective-permute-start) | collective-permute-done | bytes 3244064 | tf_op jit(solution)/shard_map/ppermute | solution.py:137
  59.0 2.6 add_convert_fusion
  61.6 134.9 %all-reduce.3.cloned.1.call-done = bf16[3,384,1408]{2,1,0:T(8,128)(2,1)} async-done(((bf16[3,384,1408]{2,1,0:T(8,128)(2,1)}), bf16[3,384,1408]{2,1,0:T(8,128)(2,1)}) %all-reduce.3.cloned.1.call-update) | async-done | bytes 3244048 | tf_op jit(solution)/shard_map/psum | solution.py:139
  196.7 0.6 broadcast_in_dim.34
  197.3 4.7 %all-to-all-start = ((f32[8,256,2]{1,2,0:T(2,128)}), f32[8,256,2]{1,2,0:T(2,128)S(1)}, u32[]{:S(2)}, u32[]{:S(2)}) async-start(f32[8,256,2]{1,2,0:T(2,128)} %broadcast_in_dim.34), calls=%async_computation | async-start | bytes 32768 | tf_op jit(solution)/shard_map/all_to_all | solution.py:39
  202.0 0.3 iota_compare_fusion
  202.7 4.7 %all-to-all-done = f32[8,256,2]{1,2,0:T(2,128)S(1)} async-done(((f32[8,256,2]{1,2,0:T(2,128)}), f32[8,256,2]{1,2,0:T(2,128)S(1)}, u32[]{:S(2)}, u32[]{:S(2)}) %all-to-all-start) | async-done | bytes 16416 | tf_op jit(solution)/shard_map/all_to_all | solution.py:39
  208.3 1.0 select_reduce_fusion
  209.4 0.6 copy.89
  210.0 8.1 %all-to-all-start.2 = ((bf16[32,4,24]{2,1,0:T(4,128)(2,1)}), bf16[32,4,24]{2,1,0:T(4,128)(2,1)S(1)}, u32[]{:S(2)}, u32[]{:S(2)}) async-start(bf16[32,4,24]{2,1,0:T(4,128)(2,1)} %copy.89), calls=%async_computation.2 | async-start | bytes 65536 | tf_op jit(solution)/shard_map/all_to_all | solution.py:101
  218.1 0.5 compare_convert_fusion
  218.6 0.6 compare_reduce_fusion
  219.3 0.6 compare_reduce_fusion.1
  219.9 6.4 %all-to-all-done.2 = bf16[32,4,24]{2,1,0:T(4,128)(2,1)S(1)} async-done(((bf16[32,4,24]{2,1,0:T(4,128)(2,1)}), bf16[32,4,24]{2,1,0:T(4,128)(2,1)S(1)}, u32[]{:S(2)}, u32[]{:S(2)}) %all-to-all-start.2) | async-done | bytes 6176 | tf_op jit(solution)/shard_map/all_to_all | solution.py:101
  226.7 0.6 fusion.102
  227.3 0.6 fusion.103
  227.9 2.2 constant_dynamic-update-slice_fusion.1
  230.1 2.4 constant_dynamic-update-slice_fusion
  232.5 3.4 %fusion.11 = (f32[768]{0:T(1024)S(1)}, bf16[768,1408]{1,0:T(8,128)(2,1)}) fusion(bf16[3,768,1408]{2,1,0:T(8,128)(2,1)S(1)} %constant_dynamic-update-slice_fusion), kind=kLoop, calls=%fused_computation.23 | loop fusion | flops 12975360 | bytes 8653824 | tf_op jit(solution)/shard_map/reduce_sum | solution.py:157
  235.8 1.5 fusion.60
  237.4 1.8 fusion.39
  239.2 2.8 add_convert_fusion.1
  242.0 1.5 fusion.95
  243.6 1.4 scatter.9
  245.3 0.3 copy-done.5
  245.7 0.8 copy-done.7
  246.5 1.2 fusion.85
  247.7 0.8 reshape.297
  248.5 4.6 %all-to-all-start.4 = ((f32[32,1,512]{2,1,0:T(1,128)}), f32[32,1,512]{2,1,0:T(1,128)}, u32[]{:S(2)}, u32[]{:S(2)}) async-start(f32[32,1,512]{2,1,0:T(1,128)} %reshape.297), calls=%async_computation.4 | async-start | bytes 131072 | tf_op jit(solution)/shard_map/all_to_all | solution.py:47
  253.2 8.3 %all-to-all-done.4 = f32[32,1,512]{2,1,0:T(1,128)} async-done(((f32[32,1,512]{2,1,0:T(1,128)}), f32[32,1,512]{2,1,0:T(1,128)}, u32[]{:S(2)}, u32[]{:S(2)}) %all-to-all-start.4) | async-done | bytes 65568 | tf_op jit(solution)/shard_map/all_to_all | solution.py:47
  261.5 0.5 broadcast.240
  262.0 1.6 reduce.26
  263.8 0.8 reshape.299
  264.6 3.9 %all-to-all-start.5 = ((f32[32,1,512]{2,1,0:T(1,128)}), f32[32,1,512]{2,1,0:T(1,128)S(1)}, u32[]{:S(2)}, u32[]{:S(2)}) async-start(f32[32,1,512]{2,1,0:T(1,128)} %reshape.299), calls=%async_computation.5 | async-start | bytes 131072 | tf_op jit(solution)/shard_map/all_to_all | solution.py:49
  268.5 3.1 maximum_select_fusion
  271.6 5.3 %all-to-all-done.5 = f32[32,1,512]{2,1,0:T(1,128)S(1)} async-done(((f32[32,1,512]{2,1,0:T(1,128)}), f32[32,1,512]{2,1,0:T(1,128)S(1)}, u32[]{:S(2)}, u32[]{:S(2)}) %all-to-all-start.5) | async-done | bytes 65568 | tf_op jit(solution)/shard_map/all_to_all | solution.py:49
  277.0 4.9 %all-to-all-start.3 = ((bf16[32,24,1152]{2,1,0:T(8,128)(2,1)}), bf16[32,24,1152]{2,1,0:T(8,128)(2,1)}, u32[]{:S(2)}, u32[]{:S(2)}) async-start(bf16[32,24,1152]{2,1,0:T(8,128)(2,1)} %maximum_select_fusion), calls=%async_computation.3 | async-start | bytes 3538944 | tf_op jit(solution)/shard_map/all_to_all | solution.py:170
  281.9 0.3 iota_compare_fusion.2
  282.2 0.5 eq.117
  282.8 4.5 %fusion.33 = bf16[1,1408,512]{2,1,0:T(8,128)(2,1)} fusion(bf16[768,1408]{1,0:T(8,128)(2,1)} %get-tuple-element.68, f32[768]{0:T(1024)S(1)} %copy-done.17, bf16[768,1024]{1,0:T(8,128)(2,1)} %copy-done.6), kind=kOutput, calls=%fused_computation.52 | convolution fusion | flops 1111261184 | bytes 4393984 | tf_op jit(solution)/shard_map/dot_general | solution.py:8
  287.3 3.2 %fusion.32 = bf16[1,1408,512]{2,1,0:T(8,128)(2,1)} fusion(f32[768]{0:T(1024)S(1)} %copy-done.17, bf16[3,768,1408]{2,1,0:T(8,128)(2,1)S(1)} %bitcast.158, bf16[768,1024]{1,0:T(8,128)(2,1)S(1)} %copy-done.8), kind=kOutput, calls=%fused_computation.51 | convolution fusion | flops 1117749248 | bytes 6557696 | tf_op jit(solution)/shard_map/dot_general | solution.py:8
  290.4 3.9 %fusion.31 = bf16[1,1408,512]{2,1,0:T(8,128)(2,1)} fusion(f32[768]{0:T(1024)S(1)} %copy-done.17, bf16[3,768,1408]{2,1,0:T(8,128)(2,1)S(1)} %bitcast.158, bf16[768,1024]{1,0:T(8,128)(2,1)S(1)} %copy-done.8), kind=kOutput, calls=%fused_computation.50 | convolution fusion | flops 1123155968 | bytes 8720384 | tf_op jit(solution)/shard_map/dot_general | solution.py:8
  294.4 0.8 reduce.27
  295.3 0.7 copy.97
  296.0 7.1 %all-to-all-done.3 = bf16[32,24,1152]{2,1,0:T(8,128)(2,1)} async-done(((bf16[32,24,1152]{2,1,0:T(8,128)(2,1)}), bf16[32,24,1152]{2,1,0:T(8,128)(2,1)}, u32[]{:S(2)}, u32[]{:S(2)}) %all-to-all-start.3) | async-done | bytes 1769504 | tf_op jit(solution)/shard_map/all_to_all | solution.py:170
  303.1 2.8 fusion.119
  305.9 0.2 fusion.93
  306.2 0.9 multiply_reduce_fusion
  307.1 1.1 fusion.68
  (103 shorter events, 3.9 us)
Async XLA Ops:
  7.2 43.3 %copy-start = (bf16[1,1408,512]{2,1,0:T(8,128)(2,1)S(1)}, bf16[1,1408,512]{2,1,0:T(8,128)(2,1)}, u32[]{:S(2)}) copy-start(bf16[1,1408,512]{2,1,0:T(8,128)(2,1)} %param.17) | copy-start | bytes 4325380
  13.9 31.7 %all-to-all-start.1 = ((bf16[32,24,1024]{2,1,0:T(8,128)(2,1)}), bf16[32,24,1024]{2,1,0:T(8,128)(2,1)S(1)}, u32[]{:S(2)}, u32[]{:S(2)}) async-start(bf16[32,24,1024]{2,1,0:T(8,128)(2,1)} %bitcast.160), calls=%async_computation.1 | async-start | bytes 3145728 | tf_op jit(solution)/shard_map/all_to_all | solution.py:94
  22.6 173.9 %all-reduce.3.cloned.1.call-start = ((), (), s32[]{:S(2)}) async-start(), calls=%async_computation.6 | async-start | bytes 6488064 | tf_op jit(solution)/shard_map/psum | solution.py:139
  45.7 1.4 copy-start.21
  47.1 3.4 %copy-start.6 = (bf16[768,1024]{1,0:T(8,128)(2,1)}, bf16[768,1024]{1,0:T(8,128)(2,1)S(1)}, u32[]{:S(2)}) copy-start(bf16[768,1024]{1,0:T(8,128)(2,1)S(1)} %maximum_select_fusion.1) | copy-start | bytes 4718596
  47.1 1.9 copy-start.19
  53.1 5.9 %collective-permute-start = (bf16[3,384,1408]{2,1,0:T(8,128)(2,1)S(1)}, bf16[3,384,1408]{2,1,0:T(8,128)(2,1)S(1)}, u32[]{:S(2)}, u32[]{:S(2)}) collective-permute-start(bf16[3,384,1408]{2,1,0:T(8,128)(2,1)S(1)} %slice.175), channel_id=1, source_target_pairs={{0,1},{1,0},{2,3},{3,2},{4,5},{5,4},{6,7},{7,6},{8,9},{9,8},{10,11... | collective-permute-start | bytes 9732104 | tf_op jit(solution)/shard_map/ppermute | solution.py:137
  61.5 134.9 %copy-start.9 = (bf16[256,512]{1,0:T(8,128)(2,1)S(1)}, bf16[256,512]{1,0:T(8,128)(2,1)}, u32[]{:S(2)}) copy-start(bf16[256,512]{1,0:T(8,128)(2,1)} %param.11) | copy-start | bytes 786436
  61.5 134.9 %copy-start.11 = (bf16[512,32]{0,1:T(8,128)(2,1)S(1)}, bf16[512,32]{0,1:T(8,128)(2,1)}, u32[]{:S(2)}) copy-start(bf16[512,32]{0,1:T(8,128)(2,1)} %param.14) | copy-start | bytes 98308
  61.5 135.1 %copy-start.10 = (s32[256,2]{0,1:T(2,128)S(1)}, s32[256,2]{0,1:T(2,128)}, u32[]{:S(2)}) copy-start(s32[256,2]{0,1:T(2,128)} %param.13) | copy-start | bytes 6148
  196.5 33.6 %collective-permute-start.1 = (bf16[3,384,1408]{2,1,0:T(8,128)(2,1)}, bf16[3,384,1408]{2,1,0:T(8,128)(2,1)}, u32[]{:S(2)}, u32[]{:S(2)}) collective-permute-start(bf16[3,384,1408]{2,1,0:T(8,128)(2,1)} %all-reduce.3.cloned.1.call-done), channel_id=1, source_target_pairs={{0,1},{1,0},{2,3},{3,2},{4,5},{5,4},{6,7},{7,6},{8,9},{9,8},{10,11... | collective-permute-start | bytes 9732104 | tf_op jit(solution)/shard_map/ppermute | solution.py:140
  197.3 10.1 %all-to-all-start = ((f32[8,256,2]{1,2,0:T(2,128)}), f32[8,256,2]{1,2,0:T(2,128)S(1)}, u32[]{:S(2)}, u32[]{:S(2)}) async-start(f32[8,256,2]{1,2,0:T(2,128)} %broadcast_in_dim.34), calls=%async_computation | async-start | bytes 32768 | tf_op jit(solution)/shard_map/all_to_all | solution.py:39
  207.5 22.6 %copy-start.14 = (f32[256,1]{0,1:T(1,128)}, f32[256,1]{0,1:T(1,128)S(1)}, u32[]{:S(2)}) copy-start(f32[256,1]{0,1:T(1,128)S(1)} %get-tuple-element.64) | copy-start | bytes 3076
  210.0 16.3 %all-to-all-start.2 = ((bf16[32,4,24]{2,1,0:T(4,128)(2,1)}), bf16[32,4,24]{2,1,0:T(4,128)(2,1)S(1)}, u32[]{:S(2)}, u32[]{:S(2)}) async-start(bf16[32,4,24]{2,1,0:T(4,128)(2,1)} %copy.89), calls=%async_computation.2 | async-start | bytes 65536 | tf_op jit(solution)/shard_map/all_to_all | solution.py:101
  227.9 11.3 %copy-start.16 = (f32[768]{0:T(1024)}, f32[768]{0:T(1024)S(1)}, u32[]{:S(2)}) copy-start(f32[768]{0:T(1024)S(1)} %get-tuple-element.61) | copy-start | bytes 9220
  232.5 6.7 %copy-start.2 = (bf16[3,768,1408]{2,1,0:T(8,128)(2,1)}, bf16[3,768,1408]{2,1,0:T(8,128)(2,1)S(1)}, u32[]{:S(2)}) copy-start(bf16[3,768,1408]{2,1,0:T(8,128)(2,1)S(1)} %constant_dynamic-update-slice_fusion) | copy-start | bytes 19464196
  235.8 1.5 copy-start.20
  237.3 7.6 %copy-start.3 = (bf16[768,512]{1,0:T(8,128)(2,1)}, bf16[768,512]{1,0:T(8,128)(2,1)S(1)}, u32[]{:S(2)}) copy-start(bf16[768,512]{1,0:T(8,128)(2,1)S(1)} %fusion.60) | copy-start | bytes 2359300
  237.4 1.8 copy-start.22
  242.0 11.1 %copy-start.4 = (bf16[768,512]{1,0:T(8,128)(2,1)}, bf16[768,512]{1,0:T(8,128)(2,1)S(1)}, u32[]{:S(2)}) copy-start(bf16[768,512]{1,0:T(8,128)(2,1)S(1)} %add_convert_fusion.1) | copy-start | bytes 2359300
  245.0 0.7 copy-start.5
  245.0 0.7 copy-start.13
  245.0 1.5 copy-start.7
  245.0 1.5 copy-start.18
  245.0 1.5 copy-start.23
  248.5 13.0 %all-to-all-start.4 = ((f32[32,1,512]{2,1,0:T(1,128)}), f32[32,1,512]{2,1,0:T(1,128)}, u32[]{:S(2)}, u32[]{:S(2)}) async-start(f32[32,1,512]{2,1,0:T(1,128)} %reshape.297), calls=%async_computation.4 | async-start | bytes 131072 | tf_op jit(solution)/shard_map/all_to_all | solution.py:47
  264.6 12.3 %all-to-all-start.5 = ((f32[32,1,512]{2,1,0:T(1,128)}), f32[32,1,512]{2,1,0:T(1,128)S(1)}, u32[]{:S(2)}, u32[]{:S(2)}) async-start(f32[32,1,512]{2,1,0:T(1,128)} %reshape.299), calls=%async_computation.5 | async-start | bytes 131072 | tf_op jit(solution)/shard_map/all_to_all | solution.py:49
  271.6 11.1 %copy-start.17 = (f32[768]{0:T(1024)S(1)}, f32[768]{0:T(1024)}, u32[]{:S(2)}) copy-start(f32[768]{0:T(1024)} %copy-done.16) | copy-start | bytes 9220
  277.0 26.1 %all-to-all-start.3 = ((bf16[32,24,1152]{2,1,0:T(8,128)(2,1)}), bf16[32,24,1152]{2,1,0:T(8,128)(2,1)}, u32[]{:S(2)}, u32[]{:S(2)}) async-start(bf16[32,24,1152]{2,1,0:T(8,128)(2,1)} %maximum_select_fusion), calls=%async_computation.3 | async-start | bytes 3538944 | tf_op jit(solution)/shard_map/all_to_all | solution.py:170
  282.2 5.0 %slice-start = ((s8[6488064]{0:T(1024)(128)(4,1)}), s8[2293760]{0:T(1024)(128)(4,1)S(1)}, s32[]{:S(2)}) async-start(s8[6488064]{0:T(1024)(128)(4,1)} %bitcast.157), calls=%async_computation.7 | async-start | bytes 4587520
  282.8 4.5 %slice-start.1 = ((s8[6488064]{0:T(1024)(128)(4,1)}), s8[4194304]{0:T(1024)(128)(4,1)S(1)}, s32[]{:S(2)}) async-start(s8[6488064]{0:T(1024)(128)(4,1)} %bitcast.157), calls=%async_computation.8 | async-start | bytes 8388608
  282.8 4.5 %copy-start.8 = (bf16[768,1024]{1,0:T(8,128)(2,1)S(1)}, bf16[768,1024]{1,0:T(8,128)(2,1)}, u32[]{:S(2)}) copy-start(bf16[768,1024]{1,0:T(8,128)(2,1)} %copy-done.6) | copy-start | bytes 4718596
  303.1 5.1 %copy-start.1 = (bf16[1,1408,512]{2,1,0:T(8,128)(2,1)S(1)}, bf16[1,1408,512]{2,1,0:T(8,128)(2,1)}, u32[]{:S(2)}) copy-start(bf16[1,1408,512]{2,1,0:T(8,128)(2,1)} %param.17) | copy-start | bytes 4325380
  303.1 3.0 copy-start.15
  303.1 4.0 %copy-start.12 = (bf16[512,32]{0,1:T(8,128)(2,1)S(1)}, bf16[512,32]{0,1:T(8,128)(2,1)}, u32[]{:S(2)}) copy-start(bf16[512,32]{0,1:T(8,128)(2,1)} %param.14) | copy-start | bytes 98308
Sparse Core Ops, SparseCore 0:
  61.7 134.7 all-reduce.2

commit v8 on v7

--- a/solution.py
+++ b/solution.py
@@ -60,11 +60,7 @@
     onehot = (expert_ids[:, :, None] == jnp.arange(experts, dtype=jnp.int32)[None, None, :]).astype(
         jnp.float32
     )
-    chosen = head_sum(jnp.sum(partial_logits[:, None, :] * onehot, axis=2))
-    prob_pairs = jnp.stack(
-        [jax.nn.sigmoid(chosen[:, 0] - chosen[:, 1]), jax.nn.sigmoid(chosen[:, 1] - chosen[:, 0])],
-        axis=1,
-    )
+    chosen_part = jnp.sum(partial_logits[:, None, :] * onehot, axis=2)
     flat_ids = expert_ids.reshape(-1)
     id_hits = (flat_ids[:, None] == jnp.arange(experts, dtype=jnp.int32)[None, :]).astype(jnp.int32)
     places = jnp.sum((jnp.cumsum(id_hits, axis=0) - 1) * id_hits, axis=1)
@@ -76,21 +72,6 @@
     packed = jnp.dot(
         token_hit.astype(jnp.bfloat16), rows_in, preferred_element_type=jnp.float32
     ).astype(jnp.bfloat16)
-    pair_prod = prob_pairs[:, 0] * prob_pairs[:, 1]
-    q_hi = pair_prod.astype(jnp.bfloat16).astype(jnp.float32)
-    q_lo = pair_prod - q_hi
-    pick_values = jnp.stack(
-        [
-            prob_pairs.reshape(-1),
-            jnp.repeat(q_hi, pick_count),
-            jnp.repeat(q_lo, pick_count),
-            expert_ids[:, ::-1].reshape(-1).astype(jnp.float32),
-        ],
-        axis=0,
-    )
-    slot_values = jnp.sum(
-        jnp.where(pick_hit[None], pick_values[:, None, :], 0.0), axis=2
-    ).astype(jnp.bfloat16)
     both = lax.all_to_all(
         packed.reshape(experts, capacity, 2 * shard_width),
         "ctx",
@@ -98,13 +79,6 @@
         concat_axis=0,
         tiled=True,
     )
-    recv_p = lax.all_to_all(
-        slot_values.reshape(4, experts, capacity).transpose(1, 0, 2),
-        "ctx",
-        split_axis=0,
-        concat_axis=0,
-        tiled=True,
-    )
     slot_count = both.shape[0] * both.shape[1]
     half = slot_count // 2
     swapped = lax.axis_index("head") % 2 == 1
@@ -116,12 +90,6 @@
     both = local_order(both.reshape(slot_count, 2 * shard_width))
     x_rows = both[:, :shard_width]
     cot_rows = both[:, shard_width:]
-    row_values = local_order(
-        recv_p.transpose(0, 2, 1).reshape(slot_count, 4)
-    ).T.astype(jnp.float32)
-    prob_rows = row_values[0]
-    pair_rows = row_values[1] + row_values[2]
-    other_rows = row_values[3].astype(jnp.int32)
     gate_w = w_gate[0]
     up_w = w_up[0]
     down_w = w_down[0]
@@ -136,9 +104,44 @@
         parts[:, :half].astype(jnp.float32)
         + lax.ppermute(parts[:, half:], "head", partner).astype(jnp.float32)
     ).astype(jnp.bfloat16)
+    pair_sum, chosen_part = lax.optimization_barrier((pair_sum, chosen_part))
     mine = lax.psum(pair_sum, "head", axis_index_groups=same_core)
+    chosen = head_sum(chosen_part)
+    prob_pairs = jnp.stack(
+        [jax.nn.sigmoid(chosen[:, 0] - chosen[:, 1]), jax.nn.sigmoid(chosen[:, 1] - chosen[:, 0])],
+        axis=1,
+    )
+    pair_prod = prob_pairs[:, 0] * prob_pairs[:, 1]
+    q_hi = pair_prod.astype(jnp.bfloat16).astype(jnp.float32)
+    q_lo = pair_prod - q_hi
+    pick_values = jnp.stack(
+        [
+            prob_pairs.reshape(-1),
+            jnp.repeat(q_hi, pick_count),
+            jnp.repeat(q_lo, pick_count),
+            expert_ids[:, ::-1].reshape(-1).astype(jnp.float32),
+        ],
+        axis=0,
+    )
+    slot_values = jnp.sum(
+        jnp.where(pick_hit[None], pick_values[:, None, :], 0.0), axis=2
+    ).astype(jnp.bfloat16)
+    recv_p = lax.all_to_all(
+        slot_values.reshape(4, experts, capacity).transpose(1, 0, 2),
+        "ctx",
+        split_axis=0,
+        concat_axis=0,
+        tiled=True,
+    )
+    row_values = local_order(
+        recv_p.transpose(0, 2, 1).reshape(slot_count, 4)
+    ).T.astype(jnp.float32)
+    mine, row_values = lax.optimization_barrier((mine, row_values))
     sums = jnp.concatenate([mine, lax.ppermute(mine, "head", partner)], axis=1)
     gate_sum, up_sum, back_sum = sums[0], sums[1], sums[2]
+    prob_rows = row_values[0]
+    pair_rows = row_values[1] + row_values[2]
+    other_rows = row_values[3].astype(jnp.int32)
     gate_pre = gate_sum.astype(jnp.float32)
     up_pre = up_sum.astype(jnp.float32)
     hidden = forward_act(gate_pre, up_pre)

time: 318 us -> 294 us (0.925)
  waiting for transfers between devices: 195 us -> 153 us
  blocking collectives: 0 us -> 13.1 us
  matrix products: 29.9 us -> 37 us
    psum x1, waiting for transfers between devices: 135 us -> 107 us  [local(): mine = lax.psum(pair_sum, 'head', axis_index_groups=same_core)]
    all_to_all x0 -> x1, blocking collectives: none -> 13.1 us  [local(): lax.all_to_all(slot_values.reshape(4, experts, capacity).transpose(1, 0,...]
    all_to_all x1, waiting for transfers between devices: 8.3 us -> 0.01 us  [ctx_sum(): lax.all_to_all(pieces, 'ctx', split_axis=0, concat_axis=0, tiled=True)]
    all_to_all x1 -> x0, starting transfers between devices: 8.08 us -> none  [local(): lax.all_to_all(slot_values.reshape(4, experts, capacity).transpose(1, 0,...]
    all_to_all x1 -> x0, waiting for transfers between devices: 6.39 us -> none  [local(): lax.all_to_all(slot_values.reshape(4, experts, capacity).transpose(1, 0,...]
    all_to_all x1, starting transfers between devices: 3.86 us -> 8.3 us  [ctx_sum(): lax.all_to_all(spread, 'ctx', split_axis=0, concat_axis=0, tiled=True)]
    unnamed x59 -> x39, local copies, waits for them, and re-layouts: 7.95 us -> 7.32 us
  transfers between devices with their start and end apart: 9 -> 8, of which waited for: 8 -> 7; matrix products, arithmetic and copies ran while one was open for 8% -> 14% of each run, Pallas kernels for 0% -> 0%
where the time goes in v8:
time: 294 us; the launch traced here: 290 us
  waiting for transfers between devices  153 us (52%)
  matrix products  37 us (13%)
  starting transfers between devices  35.6 us (12%)
  other arithmetic  20.6 us (7%)
  local copies, waits for them, and re-layouts  16.4 us (6%)
  between operations  14.6 us (5%)
  blocking collectives  13.1 us (4%)
    psum x1, waiting for transfers between devices, local(): mine = lax.psum(pair_sum, 'head', axis_index_groups=same_core)  107 us
    all_to_all x1, waiting for transfers between devices, local(): lax.all_to_all(packed.reshape(experts, capacity, 2 * shard_width), 'ctx',...  22.9 us
    dot_general x3, matrix products, contract_rows(): lax.dot_general(left, right, (((0,), (0,)), ((), ())), preferred_element_...  13.9 us
    all_to_all x1, blocking collectives, local(): lax.all_to_all(slot_values.reshape(4, experts, capacity).transpose(1, 0,...  13.1 us
    all_to_all x1, starting transfers between devices, local(): lax.all_to_all(packed.reshape(experts, capacity, 2 * shard_width), 'ctx',...  8.68 us
    all_to_all x1, starting transfers between devices, ctx_sum(): lax.all_to_all(spread, 'ctx', split_axis=0, concat_axis=0, tiled=True)  8.3 us
    unnamed x39, local copies, waits for them, and re-layouts  7.32 us
    all_to_all x1, starting transfers between devices, head_sum(): lax.all_to_all(spread, 'head', split_axis=0, concat_axis=0, tiled=True)  7.22 us
  transfers between devices with their start and end apart: 8, of which 7 were waited for; matrix products, arithmetic and copies ran while one was open for 14% of the time, Pallas kernels for 0%

profile of v8, /device:TPU:64, one launch (start us, length us, event | category | flops | bytes accessed | tf_op | source)
XLA Modules:
  0.0 290.3 jit_solution(13625655693066579940)
XLA Ops:
  7.2 0.9 copy.83
  8.4 1.2 reduce-window.6
  9.6 0.2 slice_reduce_fusion
  10.2 0.7 multiply_add_fusion.1
  10.9 0.3 fusion.49
  11.2 2.8 convolution_convert_fusion.6
  13.9 8.7 %all-to-all-start = ((bf16[32,24,1024]{2,1,0:T(8,128)(2,1)}), bf16[32,24,1024]{2,1,0:T(8,128)(2,1)S(1)}, u32[]{:S(2)}, u32[]{:S(2)}) async-start(bf16[32,24,1024]{2,1,0:T(8,128)(2,1)} %bitcast.160), calls=%async_computation | async-start | bytes 3145728 | tf_op jit(solution)/shard_map/all_to_all | solution.py:75
  22.7 22.9 %all-to-all-done = bf16[32,24,1024]{2,1,0:T(8,128)(2,1)S(1)} async-done(((bf16[32,24,1024]{2,1,0:T(8,128)(2,1)}), bf16[32,24,1024]{2,1,0:T(8,128)(2,1)S(1)}, u32[]{:S(2)}, u32[]{:S(2)}) %all-to-all-start) | async-done | bytes 1572896 | tf_op jit(solution)/shard_map/all_to_all | solution.py:75
  45.7 0.8 maximum_select_fusion.1
  46.6 0.5 copy-done.12
  47.1 1.4 fusion.28
  48.5 0.5 copy-done.11
  49.0 1.4 fusion.29
  50.5 1.4 fusion.30
  51.9 0.9 pad_maximum_fusion
  52.9 0.2 slice.173
  53.2 0.6 copy-done.8
  53.8 0.2 fusion.118
  54.0 5.0 %collective-permute-done = bf16[3,384,1408]{2,1,0:T(8,128)(2,1)S(1)} collective-permute-done((bf16[3,384,1408]{2,1,0:T(8,128)(2,1)S(1)}, bf16[3,384,1408]{2,1,0:T(8,128)(2,1)S(1)}, u32[]{:S(2)}, u32[]{:S(2)}) %collective-permute-start) | collective-permute-done | bytes 3244064 | tf_op jit(solution)/shard_map/ppermute | solution.py:105
  59.0 2.6 add_convert_fusion
  61.6 0.6 broadcast_in_dim.34
  62.2 7.2 %all-to-all-start.1 = ((f32[8,256,2]{1,2,0:T(2,128)}), f32[8,256,2]{1,2,0:T(2,128)S(1)}, u32[]{:S(2)}, u32[]{:S(2)}) async-start(f32[8,256,2]{1,2,0:T(2,128)} %broadcast_in_dim.34), calls=%async_computation.1 | async-start | bytes 32768 | tf_op jit(solution)/shard_map/all_to_all | solution.py:39
  69.4 0.3 iota_compare_fusion
  70.0 0.1 convert_element_type.220
  70.1 4.8 %all-to-all-done.1 = f32[8,256,2]{1,2,0:T(2,128)S(1)} async-done(((f32[8,256,2]{1,2,0:T(2,128)}), f32[8,256,2]{1,2,0:T(2,128)S(1)}, u32[]{:S(2)}, u32[]{:S(2)}) %all-to-all-start.1) | async-done | bytes 16416 | tf_op jit(solution)/shard_map/all_to_all | solution.py:39
  75.2 0.1 stack_reshape.9
  75.4 0.1 stack_reshape.10
  75.7 0.1 stack_reshape.11
  75.8 1.0 select_reduce_fusion
  76.9 13.1 %all_to_all.30 = bf16[32,4,24]{2,1,0:T(4,128)(2,1)S(1)} all-to-all(bf16[32,4,24]{2,1,0:T(4,128)(2,1)S(1)} %copy.89), channel_id=1, replica_groups=mesh['ctx'=32,'head'=8] {'ctx'}, dimensions={0} | all-to-all | bytes 12288 | tf_op jit(solution)/shard_map/all_to_all | solution.py:129
  90.4 106.6 %all-reduce.3.cloned.1.call-done = bf16[3,384,1408]{2,1,0:T(8,128)(2,1)} async-done(((bf16[3,384,1408]{2,1,0:T(8,128)(2,1)}), bf16[3,384,1408]{2,1,0:T(8,128)(2,1)}) %all-reduce.3.cloned.1.call-update) | async-done | bytes 3244048 | tf_op jit(solution)/shard_map/psum | solution.py:108
  197.0 0.6 compare_reduce_fusion
  197.6 0.6 compare_reduce_fusion.1
  198.3 2.2 constant_dynamic-update-slice_fusion.1
  200.5 2.6 collective-permute-done.1
  203.1 2.4 constant_dynamic-update-slice_fusion
  205.5 3.4 %fusion.11 = (f32[768]{0:T(1024)S(1)}, bf16[768,1408]{1,0:T(8,128)(2,1)}) fusion(bf16[3,768,1408]{2,1,0:T(8,128)(2,1)S(1)} %constant_dynamic-update-slice_fusion), kind=kLoop, calls=%fused_computation.23 | loop fusion | flops 12975360 | bytes 8653824 | tf_op jit(solution)/shard_map/reduce_sum | solution.py:160
  208.9 1.5 fusion.60
  210.4 1.2 fusion.85
  211.6 0.8 reshape.294
  212.4 7.1 %all-to-all-start.4 = ((f32[32,1,512]{2,1,0:T(1,128)}), f32[32,1,512]{2,1,0:T(1,128)S(1)}, u32[]{:S(2)}, u32[]{:S(2)}) async-start(f32[32,1,512]{2,1,0:T(1,128)} %reshape.294), calls=%async_computation.4 | async-start | bytes 131072 | tf_op jit(solution)/shard_map/all_to_all | solution.py:47
  219.4 4.2 %fusion.39 = f32[768,512]{1,0:T(8,128)S(1)} fusion(f32[768]{0:T(1024)S(1)} %get-tuple-element.69, bf16[1,1408,512]{2,1,0:T(8,128)(2,1)} %param.16, bf16[3,768,1408]{2,1,0:T(8,128)(2,1)} %copy-done.2), kind=kOutput, calls=%fused_computation.56 | convolution fusion | flops 1117028352 | bytes 7343104 | tf_op jit(solution)/shard_map/dot_general | solution.py:153
  223.7 5.4 %add_convert_fusion.1 = bf16[768,512]{1,0:T(8,128)(2,1)S(1)} fusion(f32[768,512]{1,0:T(8,128)S(1)} %fusion.39, f32[768]{0:T(1024)S(1)} %get-tuple-element.69, bf16[1,1408,512]{2,1,0:T(8,128)(2,1)S(1)} %copy-done.13, bf16[3,768,1408]{2,1,0:T(8,128)(2,1)} %copy-done.2), kind=kOutput, calls=%fused_computation.67 | convolution fusion | flops 1123221504 | bytes 10292224 | tf_op jit(solution)/shard_map/dot_general | solution.py:152
  229.1 1.6 fusion.95
  230.7 1.4 scatter.9
  232.6 0.5 broadcast.240
  233.1 0.8 reduce.26
  234.1 0.8 reshape.296
  234.9 8.3 %all-to-all-start.5 = ((f32[32,1,512]{2,1,0:T(1,128)}), f32[32,1,512]{2,1,0:T(1,128)S(1)}, u32[]{:S(2)}, u32[]{:S(2)}) async-start(f32[32,1,512]{2,1,0:T(1,128)} %reshape.296), calls=%async_computation.5 | async-start | bytes 131072 | tf_op jit(solution)/shard_map/all_to_all | solution.py:49
  243.2 3.1 %maximum_select_fusion = bf16[32,24,1152]{2,1,0:T(8,128)(2,1)} fusion(bf16[32,24,1152]{2,1,0:T(8,128)(2,1)S(1)} %bitcast.159, bf16[32,24,128]{2,1,0:T(8,128)(2,1)S(1)} %bitcast.165, bf16[32,24,512]{2,1,0:T(8,128)(2,1)} %bitcast.164, bf16[32,24,512]{2,1,0:T(8,128)(2,1)} %bitcast.163, pred[]{:T(512)S(6)} %eq.106), kind=kLoop, calls=%fused_computation.64 | loop fusion | flops 6193152 | bytes 5308417 | tf_op jit(solution)/shard_map/jit(_where)/select_n | solution.py:88
  246.3 5.4 %all-to-all-done.5 = f32[32,1,512]{2,1,0:T(1,128)S(1)} async-done(((f32[32,1,512]{2,1,0:T(1,128)}), f32[32,1,512]{2,1,0:T(1,128)S(1)}, u32[]{:S(2)}, u32[]{:S(2)}) %all-to-all-start.5) | async-done | bytes 65568 | tf_op jit(solution)/shard_map/all_to_all | solution.py:49
  251.7 4.2 %all-to-all-start.3 = ((bf16[32,24,1152]{2,1,0:T(8,128)(2,1)}), bf16[32,24,1152]{2,1,0:T(8,128)(2,1)S(1)}, u32[]{:S(2)}, u32[]{:S(2)}) async-start(bf16[32,24,1152]{2,1,0:T(8,128)(2,1)} %maximum_select_fusion), calls=%async_computation.3 | async-start | bytes 3538944 | tf_op jit(solution)/shard_map/all_to_all | solution.py:173
  255.9 0.3 iota_compare_fusion.1
  256.2 1.3 eq.124
  257.5 4.4 %fusion.33 = bf16[1,1408,512]{2,1,0:T(8,128)(2,1)} fusion(bf16[768,1408]{1,0:T(8,128)(2,1)} %get-tuple-element.73, f32[768]{0:T(1024)S(1)} %get-tuple-element.69, bf16[768,1024]{1,0:T(8,128)(2,1)} %copy-done.5), kind=kOutput, calls=%fused_computation.52 | convolution fusion | flops 1111261184 | bytes 4393984 | tf_op jit(solution)/shard_map/dot_general | solution.py:8
  261.9 5.6 %fusion.32 = bf16[1,1408,512]{2,1,0:T(8,128)(2,1)} fusion(f32[768]{0:T(1024)S(1)} %get-tuple-element.69, bf16[3,768,1408]{2,1,0:T(8,128)(2,1)} %copy-done.2, bf16[768,1024]{1,0:T(8,128)(2,1)S(1)} %copy-done.7), kind=kOutput, calls=%fused_computation.51 | convolution fusion | flops 1117749248 | bytes 6557696 | tf_op jit(solution)/shard_map/dot_general | solution.py:8
  267.5 3.9 %fusion.31 = bf16[1,1408,512]{2,1,0:T(8,128)(2,1)} fusion(f32[768]{0:T(1024)S(1)} %get-tuple-element.69, bf16[3,768,1408]{2,1,0:T(8,128)(2,1)S(1)} %bitcast.158, bf16[768,1024]{1,0:T(8,128)(2,1)S(1)} %copy-done.7), kind=kOutput, calls=%fused_computation.50 | convolution fusion | flops 1123155968 | bytes 8720384 | tf_op jit(solution)/shard_map/dot_general | solution.py:8
  271.4 0.8 reduce.27
  272.3 0.7 copy.97
  273.1 5.6 %all-to-all-done.3 = bf16[32,24,1152]{2,1,0:T(8,128)(2,1)S(1)} async-done(((bf16[32,24,1152]{2,1,0:T(8,128)(2,1)}), bf16[32,24,1152]{2,1,0:T(8,128)(2,1)S(1)}, u32[]{:S(2)}, u32[]{:S(2)}) %all-to-all-start.3) | async-done | bytes 1769504 | tf_op jit(solution)/shard_map/all_to_all | solution.py:173
  278.7 2.4 fusion.117
  281.1 0.2 fusion.93
  281.4 0.9 multiply_reduce_fusion
  282.3 1.1 fusion.68
  (82 shorter events, 3.0 us)
Async XLA Ops:
  7.2 43.3 %copy-start = (bf16[1,1408,512]{2,1,0:T(8,128)(2,1)S(1)}, bf16[1,1408,512]{2,1,0:T(8,128)(2,1)}, u32[]{:S(2)}) copy-start(bf16[1,1408,512]{2,1,0:T(8,128)(2,1)} %param.17) | copy-start | bytes 4325380
  13.9 31.7 %all-to-all-start = ((bf16[32,24,1024]{2,1,0:T(8,128)(2,1)}), bf16[32,24,1024]{2,1,0:T(8,128)(2,1)S(1)}, u32[]{:S(2)}, u32[]{:S(2)}) async-start(bf16[32,24,1024]{2,1,0:T(8,128)(2,1)} %bitcast.160), calls=%async_computation | async-start | bytes 3145728 | tf_op jit(solution)/shard_map/all_to_all | solution.py:75
  22.6 174.4 %all-reduce.3.cloned.1.call-start = ((), (), s32[]{:S(2)}) async-start(), calls=%async_computation.6 | async-start | bytes 6488064 | tf_op jit(solution)/shard_map/psum | solution.py:108
  45.7 1.4 copy-start.12
  47.1 3.4 %copy-start.5 = (bf16[768,1024]{1,0:T(8,128)(2,1)}, bf16[768,1024]{1,0:T(8,128)(2,1)S(1)}, u32[]{:S(2)}) copy-start(bf16[768,1024]{1,0:T(8,128)(2,1)S(1)} %maximum_select_fusion.1) | copy-start | bytes 4718596
  47.1 1.9 copy-start.11
  52.8 1.0 copy-start.8
  52.8 0.9 copy-start.10
  52.9 1.1 copy-start.9
  53.1 5.9 %collective-permute-start = (bf16[3,384,1408]{2,1,0:T(8,128)(2,1)S(1)}, bf16[3,384,1408]{2,1,0:T(8,128)(2,1)S(1)}, u32[]{:S(2)}, u32[]{:S(2)}) collective-permute-start(bf16[3,384,1408]{2,1,0:T(8,128)(2,1)S(1)} %slice.173), channel_id=1, source_target_pairs={{0,1},{1,0},{2,3},{3,2},{4,5},{5,4},{6,7},{7,6},{8,9},{9,8},{10,11... | collective-permute-start | bytes 9732104 | tf_op jit(solution)/shard_map/ppermute | solution.py:105
  62.2 12.7 %all-to-all-start.1 = ((f32[8,256,2]{1,2,0:T(2,128)}), f32[8,256,2]{1,2,0:T(2,128)S(1)}, u32[]{:S(2)}, u32[]{:S(2)}) async-start(f32[8,256,2]{1,2,0:T(2,128)} %broadcast_in_dim.34), calls=%async_computation.1 | async-start | bytes 32768 | tf_op jit(solution)/shard_map/all_to_all | solution.py:39
  197.0 6.1 %collective-permute-start.1 = (bf16[3,384,1408]{2,1,0:T(8,128)(2,1)}, bf16[3,384,1408]{2,1,0:T(8,128)(2,1)}, u32[]{:S(2)}, u32[]{:S(2)}) collective-permute-start(bf16[3,384,1408]{2,1,0:T(8,128)(2,1)} %all-reduce.3.cloned.1.call-done), channel_id=1, source_target_pairs={{0,1},{1,0},{2,3},{3,2},{4,5},{5,4},{6,7},{7,6},{8,9},{9,8},{10,11... | collective-permute-start | bytes 9732104 | tf_op jit(solution)/shard_map/ppermute | solution.py:140
  205.5 3.4 %copy-start.2 = (bf16[3,768,1408]{2,1,0:T(8,128)(2,1)}, bf16[3,768,1408]{2,1,0:T(8,128)(2,1)S(1)}, u32[]{:S(2)}) copy-start(bf16[3,768,1408]{2,1,0:T(8,128)(2,1)S(1)} %constant_dynamic-update-slice_fusion) | copy-start | bytes 19464196
  208.9 1.5 copy-start.6
  210.4 21.8 %copy-start.3 = (bf16[768,512]{1,0:T(8,128)(2,1)}, bf16[768,512]{1,0:T(8,128)(2,1)S(1)}, u32[]{:S(2)}) copy-start(bf16[768,512]{1,0:T(8,128)(2,1)S(1)} %fusion.60) | copy-start | bytes 2359300
  212.4 20.2 %all-to-all-start.4 = ((f32[32,1,512]{2,1,0:T(1,128)}), f32[32,1,512]{2,1,0:T(1,128)S(1)}, u32[]{:S(2)}, u32[]{:S(2)}) async-start(f32[32,1,512]{2,1,0:T(1,128)} %reshape.294), calls=%async_computation.4 | async-start | bytes 131072 | tf_op jit(solution)/shard_map/all_to_all | solution.py:47
  219.4 4.2 %copy-start.13 = (bf16[1,1408,512]{2,1,0:T(8,128)(2,1)S(1)}, bf16[1,1408,512]{2,1,0:T(8,128)(2,1)}, u32[]{:S(2)}) copy-start(bf16[1,1408,512]{2,1,0:T(8,128)(2,1)} %param.15) | copy-start | bytes 4325380
  229.1 3.1 %copy-start.4 = (bf16[768,512]{1,0:T(8,128)(2,1)}, bf16[768,512]{1,0:T(8,128)(2,1)S(1)}, u32[]{:S(2)}) copy-start(bf16[768,512]{1,0:T(8,128)(2,1)S(1)} %add_convert_fusion.1) | copy-start | bytes 2359300
  234.9 16.8 %all-to-all-start.5 = ((f32[32,1,512]{2,1,0:T(1,128)}), f32[32,1,512]{2,1,0:T(1,128)S(1)}, u32[]{:S(2)}, u32[]{:S(2)}) async-start(f32[32,1,512]{2,1,0:T(1,128)} %reshape.296), calls=%async_computation.5 | async-start | bytes 131072 | tf_op jit(solution)/shard_map/all_to_all | solution.py:49
  251.7 27.0 %all-to-all-start.3 = ((bf16[32,24,1152]{2,1,0:T(8,128)(2,1)}), bf16[32,24,1152]{2,1,0:T(8,128)(2,1)S(1)}, u32[]{:S(2)}, u32[]{:S(2)}) async-start(bf16[32,24,1152]{2,1,0:T(8,128)(2,1)} %maximum_select_fusion), calls=%async_computation.3 | async-start | bytes 3538944 | tf_op jit(solution)/shard_map/all_to_all | solution.py:173
  257.5 4.4 %copy-start.7 = (bf16[768,1024]{1,0:T(8,128)(2,1)S(1)}, bf16[768,1024]{1,0:T(8,128)(2,1)}, u32[]{:S(2)}) copy-start(bf16[768,1024]{1,0:T(8,128)(2,1)} %copy-done.5) | copy-start | bytes 4718596
  257.5 10.0 %slice-start = ((s8[6488064]{0:T(1024)(128)(4,1)}), s8[4194304]{0:T(1024)(128)(4,1)S(1)}, s32[]{:S(2)}) async-start(s8[6488064]{0:T(1024)(128)(4,1)} %bitcast.157), calls=%async_computation.7 | async-start | bytes 8388608
  261.9 5.6 %slice-start.1 = ((s8[6488064]{0:T(1024)(128)(4,1)}), s8[2293760]{0:T(1024)(128)(4,1)S(1)}, s32[]{:S(2)}) async-start(s8[6488064]{0:T(1024)(128)(4,1)} %bitcast.157), calls=%async_computation.8 | async-start | bytes 4587520
  278.7 4.7 %copy-start.1 = (bf16[1,1408,512]{2,1,0:T(8,128)(2,1)S(1)}, bf16[1,1408,512]{2,1,0:T(8,128)(2,1)}, u32[]{:S(2)}) copy-start(bf16[1,1408,512]{2,1,0:T(8,128)(2,1)} %param.17) | copy-start | bytes 4325380
Sparse Core Ops, SparseCore 0:
  61.7 135.2 all-reduce.2

commit v9 on v8

--- a/solution.py
+++ b/solution.py
@@ -179,6 +179,7 @@
         concat_axis=0,
         tiled=True,
     )
+    router_part, back_both = lax.optimization_barrier((router_part, back_both))
     grad_router = ctx_sum(router_part)
     both_pairs = lax.dot_general(
         pick_hit.astype(jnp.bfloat16),

time: 294 us -> 295 us (level)
  waiting for transfers between devices: 153 us -> 165 us
  matrix products: 37 us -> 32.5 us
  starting transfers between devices: 35.6 us -> 32.3 us
    all_to_all x1, waiting for transfers between devices: 0.01 us -> 6.32 us  [ctx_sum(): lax.all_to_all(pieces, 'ctx', split_axis=0, concat_axis=0, tiled=True)]
    all_to_all x1, starting transfers between devices: 8.3 us -> 3.86 us  [ctx_sum(): lax.all_to_all(spread, 'ctx', split_axis=0, concat_axis=0, tiled=True)]
    all_to_all x1, waiting for transfers between devices: 5.61 us -> 9.92 us  [local(): lax.all_to_all(local_order(jnp.concatenate([out_rows, dx_rows, extra], ax...]
    all_to_all x1, starting transfers between devices: 4.21 us -> 7.27 us  [local(): lax.all_to_all(local_order(jnp.concatenate([out_rows, dx_rows, extra], ax...]
    unnamed x39 -> x35, local copies, waits for them, and re-layouts: 7.32 us -> 7.32 us
  transfers between devices with their start and end apart: 8 -> 8, of which waited for: 7 -> 8; matrix products, arithmetic and copies ran while one was open for 14% -> 9% of each run, Pallas kernels for 0% -> 0%
where the time goes in v9:
time: 295 us; the launch traced here: 292 us
  waiting for transfers between devices  165 us (56%)
  matrix products  32.5 us (11%)
  starting transfers between devices  32.3 us (11%)
  other arithmetic  20.3 us (7%)
  local copies, waits for them, and re-layouts  14.6 us (5%)
  between operations  14.6 us (5%)
  blocking collectives  13.1 us (4%)
    psum x1, waiting for transfers between devices, local(): mine = lax.psum(pair_sum, 'head', axis_index_groups=same_core)  107 us
    all_to_all x1, waiting for transfers between devices, local(): lax.all_to_all(packed.reshape(experts, capacity, 2 * shard_width), 'ctx',...  22.9 us
    all_to_all x1, blocking collectives, local(): lax.all_to_all(slot_values.reshape(4, experts, capacity).transpose(1, 0,...  13.1 us
    dot_general x3, matrix products, contract_rows(): lax.dot_general(left, right, (((0,), (0,)), ((), ())), preferred_element_...  11.6 us
    all_to_all x1, waiting for transfers between devices, local(): lax.all_to_all(local_order(jnp.concatenate([out_rows, dx_rows, extra], ax...  9.92 us
    all_to_all x1, starting transfers between devices, local(): lax.all_to_all(packed.reshape(experts, capacity, 2 * shard_width), 'ctx',...  8.68 us
    unnamed x35, local copies, waits for them, and re-layouts  7.32 us
    all_to_all x1, starting transfers between devices, local(): lax.all_to_all(local_order(jnp.concatenate([out_rows, dx_rows, extra], ax...  7.27 us
  transfers between devices with their start and end apart: 8, of which 8 were waited for; matrix products, arithmetic and copies ran while one was open for 9% of the time, Pallas kernels for 0%

profile of v9, /device:TPU:64, one launch (start us, length us, event | category | flops | bytes accessed | tf_op | source)
XLA Modules:
  0.0 292.1 jit_solution(4669170823180305576)
XLA Ops:
  7.2 0.9 copy.83
  8.4 1.2 reduce-window.6
  9.6 0.2 slice_reduce_fusion
  10.2 0.7 multiply_add_fusion.1
  10.9 0.3 fusion.49
  11.2 2.8 convolution_convert_fusion.6
  13.9 8.7 %all-to-all-start = ((bf16[32,24,1024]{2,1,0:T(8,128)(2,1)}), bf16[32,24,1024]{2,1,0:T(8,128)(2,1)S(1)}, u32[]{:S(2)}, u32[]{:S(2)}) async-start(bf16[32,24,1024]{2,1,0:T(8,128)(2,1)} %bitcast.160), calls=%async_computation | async-start | bytes 3145728 | tf_op jit(solution)/shard_map/all_to_all | solution.py:75
  22.7 22.9 %all-to-all-done = bf16[32,24,1024]{2,1,0:T(8,128)(2,1)S(1)} async-done(((bf16[32,24,1024]{2,1,0:T(8,128)(2,1)}), bf16[32,24,1024]{2,1,0:T(8,128)(2,1)S(1)}, u32[]{:S(2)}, u32[]{:S(2)}) %all-to-all-start) | async-done | bytes 1572896 | tf_op jit(solution)/shard_map/all_to_all | solution.py:75
  45.7 0.8 maximum_select_fusion.1
  46.6 0.5 copy-done.10
  47.1 1.4 fusion.28
  48.5 0.5 copy-done.8
  49.0 1.4 fusion.29
  50.5 1.4 fusion.30
  51.9 0.9 pad_maximum_fusion
  52.9 0.2 slice.173
  53.2 0.6 copy-done.5
  53.8 0.2 fusion.118
  54.0 5.0 %collective-permute-done = bf16[3,384,1408]{2,1,0:T(8,128)(2,1)S(1)} collective-permute-done((bf16[3,384,1408]{2,1,0:T(8,128)(2,1)S(1)}, bf16[3,384,1408]{2,1,0:T(8,128)(2,1)S(1)}, u32[]{:S(2)}, u32[]{:S(2)}) %collective-permute-start) | collective-permute-done | bytes 3244064 | tf_op jit(solution)/shard_map/ppermute | solution.py:105
  59.0 2.6 add_convert_fusion
  61.6 0.6 broadcast_in_dim.34
  62.2 7.2 %all-to-all-start.1 = ((f32[8,256,2]{1,2,0:T(2,128)}), f32[8,256,2]{1,2,0:T(2,128)S(1)}, u32[]{:S(2)}, u32[]{:S(2)}) async-start(f32[8,256,2]{1,2,0:T(2,128)} %broadcast_in_dim.34), calls=%async_computation.1 | async-start | bytes 32768 | tf_op jit(solution)/shard_map/all_to_all | solution.py:39
  69.4 0.3 iota_compare_fusion
  70.0 0.1 convert_element_type.220
  70.1 4.8 %all-to-all-done.1 = f32[8,256,2]{1,2,0:T(2,128)S(1)} async-done(((f32[8,256,2]{1,2,0:T(2,128)}), f32[8,256,2]{1,2,0:T(2,128)S(1)}, u32[]{:S(2)}, u32[]{:S(2)}) %all-to-all-start.1) | async-done | bytes 16416 | tf_op jit(solution)/shard_map/all_to_all | solution.py:39
  75.2 0.1 stack_reshape.9
  75.4 0.1 stack_reshape.10
  75.8 1.0 select_reduce_fusion
  76.9 13.1 %all_to_all.30 = bf16[32,4,24]{2,1,0:T(4,128)(2,1)S(1)} all-to-all(bf16[32,4,24]{2,1,0:T(4,128)(2,1)S(1)} %copy.89), channel_id=1, replica_groups=mesh['ctx'=32,'head'=8] {'ctx'}, dimensions={0} | all-to-all | bytes 12288 | tf_op jit(solution)/shard_map/all_to_all | solution.py:129
  90.4 106.6 %all-reduce.3.cloned.1.call-done = bf16[3,384,1408]{2,1,0:T(8,128)(2,1)} async-done(((bf16[3,384,1408]{2,1,0:T(8,128)(2,1)}), bf16[3,384,1408]{2,1,0:T(8,128)(2,1)}) %all-reduce.3.cloned.1.call-update) | async-done | bytes 3244048 | tf_op jit(solution)/shard_map/psum | solution.py:108
  197.0 0.6 compare_reduce_fusion
  197.6 0.6 compare_reduce_fusion.1
  198.3 2.2 constant_dynamic-update-slice_fusion.1
  200.4 2.5 collective-permute-done.1
  203.0 0.5 constant_dynamic-update-slice_fusion
  203.5 3.4 %fusion.11 = (f32[768]{0:T(1024)S(1)}, bf16[768,1408]{1,0:T(8,128)(2,1)}) fusion(bf16[3,768,1408]{2,1,0:T(8,128)(2,1)S(1)} %constant_dynamic-update-slice_fusion), kind=kLoop, calls=%fused_computation.23 | loop fusion | flops 12975360 | bytes 8653824 | tf_op jit(solution)/shard_map/reduce_sum | solution.py:160
  206.8 1.5 fusion.60
  208.3 1.8 fusion.39
  210.1 2.8 add_convert_fusion.1
  212.9 1.6 fusion.95
  214.6 1.4 scatter.9
  216.4 1.8 maximum_select_fusion
  218.2 7.3 %all-to-all-start.3 = ((bf16[32,24,1152]{2,1,0:T(8,128)(2,1)}), bf16[32,24,1152]{2,1,0:T(8,128)(2,1)S(1)}, u32[]{:S(2)}, u32[]{:S(2)}) async-start(bf16[32,24,1152]{2,1,0:T(8,128)(2,1)} %maximum_select_fusion), calls=%async_computation.3 | async-start | bytes 3538944 | tf_op jit(solution)/shard_map/all_to_all | solution.py:173
  225.5 0.3 iota_compare_fusion.1
  225.8 1.3 eq.124
  227.1 2.0 fusion.85
  229.1 4.4 %fusion.33 = bf16[1,1408,512]{2,1,0:T(8,128)(2,1)} fusion(bf16[768,1408]{1,0:T(8,128)(2,1)} %get-tuple-element.77, f32[768]{0:T(1024)S(1)} %get-tuple-element.72, bf16[768,1024]{1,0:T(8,128)(2,1)} %copy-done.3), kind=kOutput, calls=%fused_computation.52 | convolution fusion | flops 1111261184 | bytes 4393984 | tf_op jit(solution)/shard_map/dot_general | solution.py:8
  233.6 3.2 %fusion.32 = bf16[1,1408,512]{2,1,0:T(8,128)(2,1)} fusion(f32[768]{0:T(1024)S(1)} %get-tuple-element.72, bf16[3,768,1408]{2,1,0:T(8,128)(2,1)S(1)} %bitcast.158, bf16[768,1024]{1,0:T(8,128)(2,1)S(1)} %copy-done.4), kind=kOutput, calls=%fused_computation.51 | convolution fusion | flops 1117749248 | bytes 6557696 | tf_op jit(solution)/shard_map/dot_general | solution.py:8
  236.8 3.9 %fusion.31 = bf16[1,1408,512]{2,1,0:T(8,128)(2,1)} fusion(f32[768]{0:T(1024)S(1)} %get-tuple-element.72, bf16[3,768,1408]{2,1,0:T(8,128)(2,1)S(1)} %bitcast.158, bf16[768,1024]{1,0:T(8,128)(2,1)S(1)} %copy-done.4), kind=kOutput, calls=%fused_computation.50 | convolution fusion | flops 1123155968 | bytes 8720384 | tf_op jit(solution)/shard_map/dot_general | solution.py:8
  240.7 9.9 %all-to-all-done.3 = bf16[32,24,1152]{2,1,0:T(8,128)(2,1)S(1)} async-done(((bf16[32,24,1152]{2,1,0:T(8,128)(2,1)}), bf16[32,24,1152]{2,1,0:T(8,128)(2,1)S(1)}, u32[]{:S(2)}, u32[]{:S(2)}) %all-to-all-start.3) | async-done | bytes 1769504 | tf_op jit(solution)/shard_map/all_to_all | solution.py:173
  250.7 3.4 %fusion.117 = (bf16[256,2,1152]{2,0,1:T(8,128)(2,1)}, f32[256,2,1152]{2,0,1:T(8,128)S(1)}) fusion(bf16[768,1152,1]{1,0,2:T(8,128)(2,1)S(1)} %bitcast.166, pred[256,2,768]{2,1,0:T(4,128)(4,1)} %eq.124), kind=kOutput, calls=%fused_computation.165 | convolution fusion | flops 906559488 | bytes 5701632 | tf_op jit(solution)/shard_map/dot_general | solution.py:184
  254.1 0.2 fusion.93
  254.5 0.8 reshape.294
  255.3 5.1 %all-to-all-start.4 = ((f32[32,1,512]{2,1,0:T(1,128)}), f32[32,1,512]{2,1,0:T(1,128)S(1)}, u32[]{:S(2)}, u32[]{:S(2)}) async-start(f32[32,1,512]{2,1,0:T(1,128)} %reshape.294), calls=%async_computation.4 | async-start | bytes 131072 | tf_op jit(solution)/shard_map/all_to_all | solution.py:47
  260.5 2.2 fusion.68
  262.6 6.3 %all-to-all-done.4 = f32[32,1,512]{2,1,0:T(1,128)S(1)} async-done(((f32[32,1,512]{2,1,0:T(1,128)}), f32[32,1,512]{2,1,0:T(1,128)S(1)}, u32[]{:S(2)}, u32[]{:S(2)}) %all-to-all-start.4) | async-done | bytes 65568 | tf_op jit(solution)/shard_map/all_to_all | solution.py:47
  269.0 0.6 broadcast.240
  269.5 0.8 reduce.26
  270.5 0.8 reshape.296
  271.3 3.9 %all-to-all-start.5 = ((f32[32,1,512]{2,1,0:T(1,128)}), f32[32,1,512]{2,1,0:T(1,128)S(1)}, u32[]{:S(2)}, u32[]{:S(2)}) async-start(f32[32,1,512]{2,1,0:T(1,128)} %reshape.296), calls=%async_computation.5 | async-start | bytes 131072 | tf_op jit(solution)/shard_map/all_to_all | solution.py:49
  275.2 2.0 multiply_reduce_fusion
  277.1 6.5 %all-to-all-done.5 = f32[32,1,512]{2,1,0:T(1,128)S(1)} async-done(((f32[32,1,512]{2,1,0:T(1,128)}), f32[32,1,512]{2,1,0:T(1,128)S(1)}, u32[]{:S(2)}, u32[]{:S(2)}) %all-to-all-start.5) | async-done | bytes 65568 | tf_op jit(solution)/shard_map/all_to_all | solution.py:49
  283.6 0.8 reduce.27
  284.5 0.7 copy.97
  (79 shorter events, 3.2 us)
Async XLA Ops:
  7.2 43.3 %copy-start = (bf16[1,1408,512]{2,1,0:T(8,128)(2,1)S(1)}, bf16[1,1408,512]{2,1,0:T(8,128)(2,1)}, u32[]{:S(2)}) copy-start(bf16[1,1408,512]{2,1,0:T(8,128)(2,1)} %param.17) | copy-start | bytes 4325380
  13.9 31.7 %all-to-all-start = ((bf16[32,24,1024]{2,1,0:T(8,128)(2,1)}), bf16[32,24,1024]{2,1,0:T(8,128)(2,1)S(1)}, u32[]{:S(2)}, u32[]{:S(2)}) async-start(bf16[32,24,1024]{2,1,0:T(8,128)(2,1)} %bitcast.160), calls=%async_computation | async-start | bytes 3145728 | tf_op jit(solution)/shard_map/all_to_all | solution.py:75
  22.6 174.4 %all-reduce.3.cloned.1.call-start = ((), (), s32[]{:S(2)}) async-start(), calls=%async_computation.6 | async-start | bytes 6488064 | tf_op jit(solution)/shard_map/psum | solution.py:108
  45.7 1.4 copy-start.10
  47.1 3.4 %copy-start.3 = (bf16[768,1024]{1,0:T(8,128)(2,1)}, bf16[768,1024]{1,0:T(8,128)(2,1)S(1)}, u32[]{:S(2)}) copy-start(bf16[768,1024]{1,0:T(8,128)(2,1)S(1)} %maximum_select_fusion.1) | copy-start | bytes 4718596
  47.1 1.9 copy-start.8
  52.8 1.0 copy-start.5
  52.8 0.9 copy-start.7
  52.9 1.1 copy-start.6
  53.1 5.9 %collective-permute-start = (bf16[3,384,1408]{2,1,0:T(8,128)(2,1)S(1)}, bf16[3,384,1408]{2,1,0:T(8,128)(2,1)S(1)}, u32[]{:S(2)}, u32[]{:S(2)}) collective-permute-start(bf16[3,384,1408]{2,1,0:T(8,128)(2,1)S(1)} %slice.173), channel_id=1, source_target_pairs={{0,1},{1,0},{2,3},{3,2},{4,5},{5,4},{6,7},{7,6},{8,9},{9,8},{10,11... | collective-permute-start | bytes 9732104 | tf_op jit(solution)/shard_map/ppermute | solution.py:105
  62.2 12.7 %all-to-all-start.1 = ((f32[8,256,2]{1,2,0:T(2,128)}), f32[8,256,2]{1,2,0:T(2,128)S(1)}, u32[]{:S(2)}, u32[]{:S(2)}) async-start(f32[8,256,2]{1,2,0:T(2,128)} %broadcast_in_dim.34), calls=%async_computation.1 | async-start | bytes 32768 | tf_op jit(solution)/shard_map/all_to_all | solution.py:39
  197.0 6.0 %collective-permute-start.1 = (bf16[3,384,1408]{2,1,0:T(8,128)(2,1)}, bf16[3,384,1408]{2,1,0:T(8,128)(2,1)S(1)}, u32[]{:S(2)}, u32[]{:S(2)}) collective-permute-start(bf16[3,384,1408]{2,1,0:T(8,128)(2,1)} %all-reduce.3.cloned.1.call-done), channel_id=1, source_target_pairs={{0,1},{1,0},{2,3},{3,2},{4,5},{5,4},{6,7},{7,6},{8,9},{9,8},{10,11... | collective-permute-start | bytes 9732104 | tf_op jit(solution)/shard_map/ppermute | solution.py:140
  203.5 6.6 %copy-start.2 = (bf16[3,768,1408]{2,1,0:T(8,128)(2,1)}, bf16[3,768,1408]{2,1,0:T(8,128)(2,1)S(1)}, u32[]{:S(2)}) copy-start(bf16[3,768,1408]{2,1,0:T(8,128)(2,1)S(1)} %constant_dynamic-update-slice_fusion) | copy-start | bytes 19464196
  206.8 1.5 copy-start.9
  208.3 1.8 copy-start.11
  218.2 32.5 %all-to-all-start.3 = ((bf16[32,24,1152]{2,1,0:T(8,128)(2,1)}), bf16[32,24,1152]{2,1,0:T(8,128)(2,1)S(1)}, u32[]{:S(2)}, u32[]{:S(2)}) async-start(bf16[32,24,1152]{2,1,0:T(8,128)(2,1)} %maximum_select_fusion), calls=%async_computation.3 | async-start | bytes 3538944 | tf_op jit(solution)/shard_map/all_to_all | solution.py:173
  227.1 6.5 %slice-start = ((s8[6488064]{0:T(1024)(128)(4,1)}), s8[4194304]{0:T(1024)(128)(4,1)S(1)}, s32[]{:S(2)}) async-start(s8[6488064]{0:T(1024)(128)(4,1)} %bitcast.157), calls=%async_computation.7 | async-start | bytes 8388608
  229.1 4.5 %slice-start.1 = ((s8[6488064]{0:T(1024)(128)(4,1)}), s8[2293760]{0:T(1024)(128)(4,1)S(1)}, s32[]{:S(2)}) async-start(s8[6488064]{0:T(1024)(128)(4,1)} %bitcast.157), calls=%async_computation.8 | async-start | bytes 4587520
  229.1 4.5 %copy-start.4 = (bf16[768,1024]{1,0:T(8,128)(2,1)S(1)}, bf16[768,1024]{1,0:T(8,128)(2,1)}, u32[]{:S(2)}) copy-start(bf16[768,1024]{1,0:T(8,128)(2,1)} %copy-done.3) | copy-start | bytes 4718596
  250.7 34.6 %copy-start.1 = (bf16[1,1408,512]{2,1,0:T(8,128)(2,1)S(1)}, bf16[1,1408,512]{2,1,0:T(8,128)(2,1)}, u32[]{:S(2)}) copy-start(bf16[1,1408,512]{2,1,0:T(8,128)(2,1)} %param.17) | copy-start | bytes 4325380
  255.3 13.6 %all-to-all-start.4 = ((f32[32,1,512]{2,1,0:T(1,128)}), f32[32,1,512]{2,1,0:T(1,128)S(1)}, u32[]{:S(2)}, u32[]{:S(2)}) async-start(f32[32,1,512]{2,1,0:T(1,128)} %reshape.294), calls=%async_computation.4 | async-start | bytes 131072 | tf_op jit(solution)/shard_map/all_to_all | solution.py:47
  271.3 12.3 %all-to-all-start.5 = ((f32[32,1,512]{2,1,0:T(1,128)}), f32[32,1,512]{2,1,0:T(1,128)S(1)}, u32[]{:S(2)}, u32[]{:S(2)}) async-start(f32[32,1,512]{2,1,0:T(1,128)} %reshape.296), calls=%async_computation.5 | async-start | bytes 131072 | tf_op jit(solution)/shard_map/all_to_all | solution.py:49
Sparse Core Ops, SparseCore 0:
  61.7 135.2 all-reduce.2

commit v10 on v8

--- a/solution.py
+++ b/solution.py
@@ -170,22 +170,38 @@
     s_hi = score_rows.astype(jnp.bfloat16)
     s_lo = (score_rows - s_hi.astype(jnp.float32)).astype(jnp.bfloat16)
     extra = jnp.zeros((slot_count, 128), jnp.bfloat16).at[:, 0].set(s_hi).at[:, 1].set(s_lo)
-    back_both = lax.all_to_all(
-        local_order(jnp.concatenate([out_rows, dx_rows, extra], axis=1)).reshape(
-            ctx_count, capacity, 2 * shard_width + 128
-        ),
+    router_pieces = router_part.reshape(ctx_count, -1)
+    router_hi = router_pieces.astype(jnp.bfloat16)
+    router_lo = (router_pieces - router_hi.astype(jnp.float32)).astype(jnp.bfloat16)
+    router_row = jnp.concatenate([router_hi, router_lo], axis=1)
+    row_width = 2 * shard_width + 128
+    router_row = jnp.pad(router_row, ((0, 0), (0, row_width - router_row.shape[1])))
+    payload = jnp.concatenate(
+        [
+            local_order(jnp.concatenate([out_rows, dx_rows, extra], axis=1)).reshape(
+                ctx_count, capacity, row_width
+            ),
+            router_row[:, None, :],
+        ],
+        axis=1,
+    )
+    back_both = lax.all_to_all(payload, "ctx", split_axis=0, concat_axis=0, tiled=True)
+    piece = router_pieces.shape[1]
+    router_in = back_both[:, capacity, : 2 * piece].astype(jnp.float32)
+    router_mine = jnp.sum(router_in[:, :piece] + router_in[:, piece:], axis=0)
+    grad_router = lax.all_to_all(
+        jnp.broadcast_to(router_mine[None], router_pieces.shape),
         "ctx",
         split_axis=0,
         concat_axis=0,
         tiled=True,
-    )
-    grad_router = ctx_sum(router_part)
+    ).reshape(router_part.shape)
     both_pairs = lax.dot_general(
         pick_hit.astype(jnp.bfloat16),
-        back_both.reshape(experts * capacity, 2 * shard_width + 128),
+        back_both[:, :capacity].reshape(experts * capacity, row_width),
         (((0,), (0,)), ((), ())),
         preferred_element_type=jnp.float32,
-    ).reshape(tok_rows, pick_count, 2 * shard_width + 128)
+    ).reshape(tok_rows, pick_count, row_width)
     out_pairs = both_pairs[:, :, :shard_width].astype(jnp.bfloat16)
     dx_pairs = both_pairs[:, :, shard_width : 2 * shard_width].astype(jnp.bfloat16)
     score_grad = both_pairs[:, :, 2 * shard_width] + both_pairs[:, :, 2 * shard_width + 1]

time: 294 us -> 295 us (level)
  waiting for transfers between devices: 153 us -> 166 us
  matrix products: 37 us -> 29 us
  starting transfers between devices: 35.6 us -> 29 us
    all_to_all x3 -> x2, waiting for transfers between devices: 11 us -> 25.9 us  [the longest x1 19.4 us: local(): lax.all_to_all(payload, 'ctx', split_axis=0, concat_axis=0, tiled=True)]
    all_to_all x3 -> x2, starting transfers between devices: 19.6 us -> 13 us  [the longest x1 7.51 us: local(): lax.all_to_all(payload, 'ctx', split_axis=0, concat_axis=0, tiled=True)]
    unnamed x39 -> x50, local copies, waits for them, and re-layouts: 7.32 us -> 6.66 us
  transfers between devices with their start and end apart: 8 -> 7, of which waited for: 7 -> 7; matrix products, arithmetic and copies ran while one was open for 14% -> 8% of each run, Pallas kernels for 0% -> 0%
where the time goes in v10:
time: 295 us; the launch traced here: 292 us
  waiting for transfers between devices  166 us (56%)
  matrix products  29 us (10%)
  starting transfers between devices  29 us (10%)
  other arithmetic  22 us (7%)
  local copies, waits for them, and re-layouts  18.7 us (6%)
  between operations  14.7 us (5%)
  blocking collectives  13.1 us (4%)
    psum x1, waiting for transfers between devices, local(): mine = lax.psum(pair_sum, 'head', axis_index_groups=same_core)  106 us
    all_to_all x1, waiting for transfers between devices, local(): lax.all_to_all(packed.reshape(experts, capacity, 2 * shard_width), 'ctx',...  22.9 us
    all_to_all x1, waiting for transfers between devices, local(): lax.all_to_all(payload, 'ctx', split_axis=0, concat_axis=0, tiled=True)  19.4 us
    all_to_all x1, blocking collectives, local(): lax.all_to_all(slot_values.reshape(4, experts, capacity).transpose(1, 0,...  13.1 us
    dot_general x3, matrix products, contract_rows(): lax.dot_general(left, right, (((0,), (0,)), ((), ())), preferred_element_...  11.6 us
    all_to_all x1, starting transfers between devices, local(): lax.all_to_all(packed.reshape(experts, capacity, 2 * shard_width), 'ctx',...  8.68 us
    all_to_all x1, starting transfers between devices, local(): lax.all_to_all(payload, 'ctx', split_axis=0, concat_axis=0, tiled=True)  7.51 us
    all_to_all x1, starting transfers between devices, head_sum(): lax.all_to_all(spread, 'head', split_axis=0, concat_axis=0, tiled=True)  7.21 us
  transfers between devices with their start and end apart: 7, of which 7 were waited for; matrix products, arithmetic and copies ran while one was open for 8% of the time, Pallas kernels for 0%

profile of v10, /device:TPU:64, one launch (start us, length us, event | category | flops | bytes accessed | tf_op | source)
XLA Modules:
  0.0 292.5 jit_solution(16153964234370472245)
XLA Ops:
  7.2 0.9 copy.87
  8.4 1.2 reduce-window.6
  9.6 0.2 slice_reduce_fusion
  10.2 0.7 multiply_add_fusion.1
  10.9 0.3 fusion.49
  11.2 2.8 convolution_convert_fusion.6
  13.9 8.7 %all-to-all-start = ((bf16[32,24,1024]{2,1,0:T(8,128)(2,1)}), bf16[32,24,1024]{2,1,0:T(8,128)(2,1)S(1)}, u32[]{:S(2)}, u32[]{:S(2)}) async-start(bf16[32,24,1024]{2,1,0:T(8,128)(2,1)} %bitcast.163), calls=%async_computation | async-start | bytes 3145728 | tf_op jit(solution)/shard_map/all_to_all | solution.py:75
  22.7 22.9 %all-to-all-done = bf16[32,24,1024]{2,1,0:T(8,128)(2,1)S(1)} async-done(((bf16[32,24,1024]{2,1,0:T(8,128)(2,1)}), bf16[32,24,1024]{2,1,0:T(8,128)(2,1)S(1)}, u32[]{:S(2)}, u32[]{:S(2)}) %all-to-all-start) | async-done | bytes 1572896 | tf_op jit(solution)/shard_map/all_to_all | solution.py:75
  45.7 0.8 maximum_select_fusion.1
  46.6 0.5 copy-done.18
  47.1 1.4 fusion.28
  48.5 0.5 copy-done.16
  49.0 1.4 fusion.29
  50.5 1.4 fusion.30
  51.9 0.9 pad_maximum_fusion
  52.9 0.2 slice.189
  53.2 0.6 copy-done.6
  54.0 5.0 %collective-permute-done = bf16[3,384,1408]{2,1,0:T(8,128)(2,1)S(1)} collective-permute-done((bf16[3,384,1408]{2,1,0:T(8,128)(2,1)S(1)}, bf16[3,384,1408]{2,1,0:T(8,128)(2,1)S(1)}, u32[]{:S(2)}, u32[]{:S(2)}) %collective-permute-start) | collective-permute-done | bytes 3244064 | tf_op jit(solution)/shard_map/ppermute | solution.py:105
  59.0 2.6 add_convert_fusion
  61.6 0.6 broadcast_in_dim.36
  62.2 7.2 %all-to-all-start.1 = ((f32[8,256,2]{1,2,0:T(2,128)}), f32[8,256,2]{1,2,0:T(2,128)S(1)}, u32[]{:S(2)}, u32[]{:S(2)}) async-start(f32[8,256,2]{1,2,0:T(2,128)} %broadcast_in_dim.36), calls=%async_computation.1 | async-start | bytes 32768 | tf_op jit(solution)/shard_map/all_to_all | solution.py:39
  69.4 0.3 iota_compare_fusion
  70.1 4.8 %all-to-all-done.1 = f32[8,256,2]{1,2,0:T(2,128)S(1)} async-done(((f32[8,256,2]{1,2,0:T(2,128)}), f32[8,256,2]{1,2,0:T(2,128)S(1)}, u32[]{:S(2)}, u32[]{:S(2)}) %all-to-all-start.1) | async-done | bytes 16416 | tf_op jit(solution)/shard_map/all_to_all | solution.py:39
  75.8 1.0 select_reduce_fusion
  76.9 13.1 %all_to_all.26 = bf16[32,4,24]{2,1,0:T(4,128)(2,1)S(1)} all-to-all(bf16[32,4,24]{2,1,0:T(4,128)(2,1)S(1)} %copy.93), channel_id=1, replica_groups=mesh['ctx'=32,'head'=8] {'ctx'}, dimensions={0} | all-to-all | bytes 12288 | tf_op jit(solution)/shard_map/all_to_all | solution.py:129
  90.4 106.4 %all-reduce.4.cloned.1.call-done = bf16[3,384,1408]{2,1,0:T(8,128)(2,1)} async-done(((bf16[3,384,1408]{2,1,0:T(8,128)(2,1)}), bf16[3,384,1408]{2,1,0:T(8,128)(2,1)}) %all-reduce.4.cloned.1.call-update) | async-done | bytes 3244048 | tf_op jit(solution)/shard_map/psum | solution.py:108
  196.7 0.6 compare_reduce_fusion
  197.4 0.6 compare_reduce_fusion.1
  198.0 0.5 compare_convert_fusion
  198.5 0.6 convert_reduce_fusion
  199.1 0.6 slice_reduce_fusion.1
  199.7 2.2 constant_dynamic-update-slice_fusion.1
  201.9 0.9 collective-permute-done.1
  202.9 2.4 constant_dynamic-update-slice_fusion
  205.3 3.4 %fusion.11 = (f32[768]{0:T(1024)S(1)}, bf16[768,1408]{1,0:T(8,128)(2,1)}) fusion(bf16[3,768,1408]{2,1,0:T(8,128)(2,1)S(1)} %constant_dynamic-update-slice_fusion), kind=kLoop, calls=%fused_computation.23 | loop fusion | flops 12975360 | bytes 8653824 | tf_op jit(solution)/shard_map/reduce_sum | solution.py:160
  208.6 1.5 fusion.60
  210.2 1.8 fusion.39
  212.0 2.8 add_convert_fusion.1
  214.8 1.6 fusion.95
  216.4 1.4 scatter.9
  218.2 0.4 copy-done.10
  218.5 0.7 copy-done.4
  219.3 1.9 fusion.85
  221.1 1.7 reshape.285
  222.8 0.9 subtract_convert_fusion
  224.0 0.5 maximum_select_fusion
  224.5 1.7 pad_maximum_fusion.1
  226.3 7.5 %all-to-all-start.3 = ((bf16[32,25,1152]{2,1,0:T(8,128)(2,1)}), bf16[32,25,1152]{2,1,0:T(8,128)(2,1)}, u32[]{:S(2)}, u32[]{:S(2)}) async-start(bf16[32,25,1152]{2,1,0:T(8,128)(2,1)} %pad_maximum_fusion.1), calls=%async_computation.3 | async-start | bytes 4718592 | tf_op jit(solution)/shard_map/all_to_all | solution.py:188
  233.8 0.3 iota_compare_fusion.1
  234.1 0.5 eq.124
  234.6 4.5 %fusion.33 = bf16[1,1408,512]{2,1,0:T(8,128)(2,1)} fusion(bf16[768,1408]{1,0:T(8,128)(2,1)} %get-tuple-element.75, f32[768]{0:T(1024)S(1)} %copy-done.14, bf16[768,1024]{1,0:T(8,128)(2,1)} %copy-done.3), kind=kOutput, calls=%fused_computation.52 | convolution fusion | flops 1111261184 | bytes 4393984 | tf_op jit(solution)/shard_map/dot_general | solution.py:8
  239.1 3.2 %fusion.32 = bf16[1,1408,512]{2,1,0:T(8,128)(2,1)} fusion(f32[768]{0:T(1024)S(1)} %copy-done.14, bf16[3,768,1408]{2,1,0:T(8,128)(2,1)S(1)} %bitcast.161, bf16[768,1024]{1,0:T(8,128)(2,1)S(1)} %copy-done.5), kind=kOutput, calls=%fused_computation.51 | convolution fusion | flops 1117749248 | bytes 6557696 | tf_op jit(solution)/shard_map/dot_general | solution.py:8
  242.3 3.9 %fusion.31 = bf16[1,1408,512]{2,1,0:T(8,128)(2,1)} fusion(f32[768]{0:T(1024)S(1)} %copy-done.14, bf16[3,768,1408]{2,1,0:T(8,128)(2,1)S(1)} %bitcast.161, bf16[768,1024]{1,0:T(8,128)(2,1)S(1)} %copy-done.5), kind=kOutput, calls=%fused_computation.50 | convolution fusion | flops 1123155968 | bytes 8720384 | tf_op jit(solution)/shard_map/dot_general | solution.py:8
  246.2 19.4 %all-to-all-done.3 = bf16[32,25,1152]{2,1,0:T(8,128)(2,1)} async-done(((bf16[32,25,1152]{2,1,0:T(8,128)(2,1)}), bf16[32,25,1152]{2,1,0:T(8,128)(2,1)}, u32[]{:S(2)}, u32[]{:S(2)}) %all-to-all-start.3) | async-done | bytes 1843232 | tf_op jit(solution)/shard_map/all_to_all | solution.py:188
  265.6 1.6 slice.199
  267.3 1.2 fusion.122
  268.5 0.2 fusion.93
  268.8 1.1 slice_convert_fusion
  270.0 0.7 broadcast_in_dim.71
  270.7 5.4 %all-to-all-start.4 = ((f32[32,1,512]{2,1,0:T(1,128)}), f32[32,1,512]{2,1,0:T(1,128)S(1)}, u32[]{:S(2)}, u32[]{:S(2)}) async-start(f32[32,1,512]{2,1,0:T(1,128)} %broadcast_in_dim.71), calls=%async_computation.4 | async-start | bytes 131072 | tf_op jit(solution)/shard_map/all_to_all | solution.py:192
  276.1 1.1 fusion.68
  277.3 0.9 multiply_reduce_fusion
  278.1 6.5 %all-to-all-done.4 = f32[32,1,512]{2,1,0:T(1,128)S(1)} async-done(((f32[32,1,512]{2,1,0:T(1,128)}), f32[32,1,512]{2,1,0:T(1,128)S(1)}, u32[]{:S(2)}, u32[]{:S(2)}) %all-to-all-start.4) | async-done | bytes 65568 | tf_op jit(solution)/shard_map/all_to_all | solution.py:192
  284.9 0.7 copy.102
  (97 shorter events, 3.8 us)
Async XLA Ops:
  7.2 43.3 %copy-start = (bf16[1,1408,512]{2,1,0:T(8,128)(2,1)S(1)}, bf16[1,1408,512]{2,1,0:T(8,128)(2,1)}, u32[]{:S(2)}) copy-start(bf16[1,1408,512]{2,1,0:T(8,128)(2,1)} %param.17) | copy-start | bytes 4325380
  13.9 31.7 %all-to-all-start = ((bf16[32,24,1024]{2,1,0:T(8,128)(2,1)}), bf16[32,24,1024]{2,1,0:T(8,128)(2,1)S(1)}, u32[]{:S(2)}, u32[]{:S(2)}) async-start(bf16[32,24,1024]{2,1,0:T(8,128)(2,1)} %bitcast.163), calls=%async_computation | async-start | bytes 3145728 | tf_op jit(solution)/shard_map/all_to_all | solution.py:75
  22.6 174.1 %all-reduce.4.cloned.1.call-start = ((), (), s32[]{:S(2)}) async-start(), calls=%async_computation.5 | async-start | bytes 6488064 | tf_op jit(solution)/shard_map/psum | solution.py:108
  45.7 1.4 copy-start.18
  47.1 4.8 %copy-start.3 = (bf16[768,1024]{1,0:T(8,128)(2,1)}, bf16[768,1024]{1,0:T(8,128)(2,1)S(1)}, u32[]{:S(2)}) copy-start(bf16[768,1024]{1,0:T(8,128)(2,1)S(1)} %maximum_select_fusion.1) | copy-start | bytes 4718596
  47.1 1.9 copy-start.16
  52.8 1.0 copy-start.6
  52.8 0.9 copy-start.8
  52.9 1.1 copy-start.7
  53.1 5.9 %collective-permute-start = (bf16[3,384,1408]{2,1,0:T(8,128)(2,1)S(1)}, bf16[3,384,1408]{2,1,0:T(8,128)(2,1)S(1)}, u32[]{:S(2)}, u32[]{:S(2)}) collective-permute-start(bf16[3,384,1408]{2,1,0:T(8,128)(2,1)S(1)} %slice.189), channel_id=1, source_target_pairs={{0,1},{1,0},{2,3},{3,2},{4,5},{5,4},{6,7},{7,6},{8,9},{9,8},{10,11... | collective-permute-start | bytes 9732104 | tf_op jit(solution)/shard_map/ppermute | solution.py:105
  62.2 12.7 %all-to-all-start.1 = ((f32[8,256,2]{1,2,0:T(2,128)}), f32[8,256,2]{1,2,0:T(2,128)S(1)}, u32[]{:S(2)}, u32[]{:S(2)}) async-start(f32[8,256,2]{1,2,0:T(2,128)} %broadcast_in_dim.36), calls=%async_computation.1 | async-start | bytes 32768 | tf_op jit(solution)/shard_map/all_to_all | solution.py:39
  75.0 126.9 %copy-start.11 = (f32[256,1]{0,1:T(1,128)}, f32[256,1]{0,1:T(1,128)S(1)}, u32[]{:S(2)}) copy-start(f32[256,1]{0,1:T(1,128)S(1)} %get-tuple-element.76) | copy-start | bytes 3076
  196.7 6.1 %collective-permute-start.1 = (bf16[3,384,1408]{2,1,0:T(8,128)(2,1)}, bf16[3,384,1408]{2,1,0:T(8,128)(2,1)}, u32[]{:S(2)}, u32[]{:S(2)}) collective-permute-start(bf16[3,384,1408]{2,1,0:T(8,128)(2,1)} %all-reduce.4.cloned.1.call-done), channel_id=1, source_target_pairs={{0,1},{1,0},{2,3},{3,2},{4,5},{5,4},{6,7},{7,6},{8,9},{9,8},{10,11... | collective-permute-start | bytes 9732104 | tf_op jit(solution)/shard_map/ppermute | solution.py:140
  199.7 12.2 %copy-start.13 = (f32[768]{0:T(1024)}, f32[768]{0:T(1024)S(1)}, u32[]{:S(2)}) copy-start(f32[768]{0:T(1024)S(1)} %get-tuple-element.68) | copy-start | bytes 9220
  205.3 6.7 %copy-start.2 = (bf16[3,768,1408]{2,1,0:T(8,128)(2,1)}, bf16[3,768,1408]{2,1,0:T(8,128)(2,1)S(1)}, u32[]{:S(2)}) copy-start(bf16[3,768,1408]{2,1,0:T(8,128)(2,1)S(1)} %constant_dynamic-update-slice_fusion) | copy-start | bytes 19464196
  208.6 1.5 copy-start.17
  210.2 1.8 copy-start.19
  217.8 0.7 copy-start.10
  217.8 1.4 copy-start.4
  217.9 1.4 copy-start.15
  217.9 1.4 copy-start.20
  226.3 8.4 %copy-start.14 = (f32[768]{0:T(1024)S(1)}, f32[768]{0:T(1024)}, u32[]{:S(2)}) copy-start(f32[768]{0:T(1024)} %copy-done.13) | copy-start | bytes 9220
  226.3 39.4 %all-to-all-start.3 = ((bf16[32,25,1152]{2,1,0:T(8,128)(2,1)}), bf16[32,25,1152]{2,1,0:T(8,128)(2,1)}, u32[]{:S(2)}, u32[]{:S(2)}) async-start(bf16[32,25,1152]{2,1,0:T(8,128)(2,1)} %pad_maximum_fusion.1), calls=%async_computation.3 | async-start | bytes 4718592 | tf_op jit(solution)/shard_map/all_to_all | solution.py:188
  234.1 5.0 %slice-start = ((s8[6488064]{0:T(1024)(128)(4,1)}), s8[2293760]{0:T(1024)(128)(4,1)S(1)}, s32[]{:S(2)}) async-start(s8[6488064]{0:T(1024)(128)(4,1)} %bitcast.160), calls=%async_computation.6 | async-start | bytes 4587520
  234.6 4.5 %slice-start.1 = ((s8[6488064]{0:T(1024)(128)(4,1)}), s8[4194304]{0:T(1024)(128)(4,1)S(1)}, s32[]{:S(2)}) async-start(s8[6488064]{0:T(1024)(128)(4,1)} %bitcast.160), calls=%async_computation.7 | async-start | bytes 8388608
  234.6 4.5 %copy-start.5 = (bf16[768,1024]{1,0:T(8,128)(2,1)S(1)}, bf16[768,1024]{1,0:T(8,128)(2,1)}, u32[]{:S(2)}) copy-start(bf16[768,1024]{1,0:T(8,128)(2,1)} %copy-done.3) | copy-start | bytes 4718596
  267.3 1.5 copy-start.12
  267.3 8.8 %copy-start.9 = (bf16[512,32]{0,1:T(8,128)(2,1)S(1)}, bf16[512,32]{0,1:T(8,128)(2,1)}, u32[]{:S(2)}) copy-start(bf16[512,32]{0,1:T(8,128)(2,1)} %param.14) | copy-start | bytes 98308
  267.3 18.3 %copy-start.1 = (bf16[1,1408,512]{2,1,0:T(8,128)(2,1)S(1)}, bf16[1,1408,512]{2,1,0:T(8,128)(2,1)}, u32[]{:S(2)}) copy-start(bf16[1,1408,512]{2,1,0:T(8,128)(2,1)} %param.17) | copy-start | bytes 4325380
  270.7 13.9 %all-to-all-start.4 = ((f32[32,1,512]{2,1,0:T(1,128)}), f32[32,1,512]{2,1,0:T(1,128)S(1)}, u32[]{:S(2)}, u32[]{:S(2)}) async-start(f32[32,1,512]{2,1,0:T(1,128)} %broadcast_in_dim.71), calls=%async_computation.4 | async-start | bytes 131072 | tf_op jit(solution)/shard_map/all_to_all | solution.py:192
Sparse Core Ops, SparseCore 0:
  61.7 134.9 all-reduce.3

commit v11 on v10

--- a/solution.py
+++ b/solution.py
@@ -169,25 +169,26 @@
     )
     s_hi = score_rows.astype(jnp.bfloat16)
     s_lo = (score_rows - s_hi.astype(jnp.float32)).astype(jnp.bfloat16)
-    extra = jnp.zeros((slot_count, 128), jnp.bfloat16).at[:, 0].set(s_hi).at[:, 1].set(s_lo)
     router_pieces = router_part.reshape(ctx_count, -1)
     router_hi = router_pieces.astype(jnp.bfloat16)
     router_lo = (router_pieces - router_hi.astype(jnp.float32)).astype(jnp.bfloat16)
-    router_row = jnp.concatenate([router_hi, router_lo], axis=1)
+    spare = 126
+    router_cols = jnp.concatenate([router_hi, router_lo], axis=1)
+    router_cols = jnp.pad(
+        router_cols, ((0, 0), (0, capacity * spare - router_cols.shape[1]))
+    ).reshape(ctx_count, capacity, spare)
     row_width = 2 * shard_width + 128
-    router_row = jnp.pad(router_row, ((0, 0), (0, row_width - router_row.shape[1])))
-    payload = jnp.concatenate(
-        [
-            local_order(jnp.concatenate([out_rows, dx_rows, extra], axis=1)).reshape(
-                ctx_count, capacity, row_width
-            ),
-            router_row[:, None, :],
-        ],
-        axis=1,
-    )
+    main = local_order(
+        jnp.concatenate([out_rows, dx_rows, s_hi[:, None], s_lo[:, None]], axis=1)
+    ).reshape(ctx_count, capacity, row_width - spare)
+    payload = jnp.concatenate([main, router_cols], axis=2)
     back_both = lax.all_to_all(payload, "ctx", split_axis=0, concat_axis=0, tiled=True)
     piece = router_pieces.shape[1]
-    router_in = back_both[:, capacity, : 2 * piece].astype(jnp.float32)
+    router_in = (
+        back_both[:, :, row_width - spare :]
+        .reshape(ctx_count, capacity * spare)[:, : 2 * piece]
+        .astype(jnp.float32)
+    )
     router_mine = jnp.sum(router_in[:, :piece] + router_in[:, piece:], axis=0)
     grad_router = lax.all_to_all(
         jnp.broadcast_to(router_mine[None], router_pieces.shape),
@@ -198,7 +199,7 @@
     ).reshape(router_part.shape)
     both_pairs = lax.dot_general(
         pick_hit.astype(jnp.bfloat16),
-        back_both[:, :capacity].reshape(experts * capacity, row_width),
+        back_both.reshape(experts * capacity, row_width),
         (((0,), (0,)), ((), ())),
         preferred_element_type=jnp.float32,
     ).reshape(tok_rows, pick_count, row_width)

time: 295 us -> 298 us (1.010)
  matrix products: 29 us -> 40.4 us
  waiting for transfers between devices: 166 us -> 160 us
  other arithmetic: 22 us -> 17.2 us
  local copies, waits for them, and re-layouts: 18.7 us -> 22.2 us
    all_to_all x1, waiting for transfers between devices: 19.4 us -> 12.6 us  [local(): lax.all_to_all(payload, 'ctx', split_axis=0, concat_axis=0, tiled=True)]
    concatenate x0 -> x2, local copies, waits for them, and re-layouts: none -> 4.81 us  [local(): jnp.concatenate([out_rows, dx_rows, s_hi[:, None], s_lo[:, None]], axis=1)]
    dot_general x1, matrix products: 2.81 us -> 6.35 us  [local(): jnp.dot(gate_grad, gate_w, preferred_element_type=jnp.float32)]
    unnamed x50 -> x37, local copies, waits for them, and re-layouts: 6.66 us -> 6.18 us
  transfers between devices with their start and end apart: 7 -> 7, of which waited for: 7 -> 7; matrix products, arithmetic and copies ran while one was open for 8% -> 9% of each run, Pallas kernels for 0% -> 0%
where the time goes in v11:
time: 298 us; the launch traced here: 295 us
  waiting for transfers between devices  160 us (54%)
  matrix products  40.4 us (14%)
  starting transfers between devices  27.2 us (9%)
  local copies, waits for them, and re-layouts  22.2 us (7%)
  other arithmetic  17.2 us (6%)
  between operations  14.6 us (5%)
  blocking collectives  13.1 us (4%)
    psum x1, waiting for transfers between devices, local(): mine = lax.psum(pair_sum, 'head', axis_index_groups=same_core)  107 us
    all_to_all x1, waiting for transfers between devices, local(): lax.all_to_all(packed.reshape(experts, capacity, 2 * shard_width), 'ctx',...  22.9 us
    dot_general x3, matrix products, contract_rows(): lax.dot_general(left, right, (((0,), (0,)), ((), ())), preferred_element_...  13.9 us
    all_to_all x1, blocking collectives, local(): lax.all_to_all(slot_values.reshape(4, experts, capacity).transpose(1, 0,...  13.1 us
    all_to_all x1, waiting for transfers between devices, local(): lax.all_to_all(payload, 'ctx', split_axis=0, concat_axis=0, tiled=True)  12.6 us
    all_to_all x1, starting transfers between devices, local(): lax.all_to_all(packed.reshape(experts, capacity, 2 * shard_width), 'ctx',...  8.68 us
    all_to_all x1, starting transfers between devices, local(): lax.all_to_all(payload, 'ctx', split_axis=0, concat_axis=0, tiled=True)  7.27 us
    all_to_all x1, starting transfers between devices, head_sum(): lax.all_to_all(spread, 'head', split_axis=0, concat_axis=0, tiled=True)  7.22 us
  transfers between devices with their start and end apart: 7, of which 7 were waited for; matrix products, arithmetic and copies ran while one was open for 9% of the time, Pallas kernels for 0%

profile of v11, /device:TPU:64, one launch (start us, length us, event | category | flops | bytes accessed | tf_op | source)
XLA Modules:
  0.0 294.8 jit_solution(14332649955627489374)
XLA Ops:
  7.2 0.9 copy.91
  8.4 1.2 reduce-window.6
  9.6 0.2 slice_reduce_fusion
  10.2 0.7 multiply_add_fusion.1
  10.9 0.3 fusion.49
  11.2 2.8 convolution_convert_fusion.6
  13.9 8.7 %all-to-all-start = ((bf16[32,24,1024]{2,1,0:T(8,128)(2,1)}), bf16[32,24,1024]{2,1,0:T(8,128)(2,1)S(1)}, u32[]{:S(2)}, u32[]{:S(2)}) async-start(bf16[32,24,1024]{2,1,0:T(8,128)(2,1)} %bitcast.157), calls=%async_computation | async-start | bytes 3145728 | tf_op jit(solution)/shard_map/all_to_all | solution.py:75
  22.7 22.9 %all-to-all-done = bf16[32,24,1024]{2,1,0:T(8,128)(2,1)S(1)} async-done(((bf16[32,24,1024]{2,1,0:T(8,128)(2,1)}), bf16[32,24,1024]{2,1,0:T(8,128)(2,1)S(1)}, u32[]{:S(2)}, u32[]{:S(2)}) %all-to-all-start) | async-done | bytes 1572896 | tf_op jit(solution)/shard_map/all_to_all | solution.py:75
  45.7 0.8 maximum_select_fusion
  46.6 0.5 copy-done.13
  47.1 1.4 fusion.28
  48.5 0.5 copy-done.11
  49.0 1.4 fusion.29
  50.5 1.4 fusion.30
  51.9 0.9 pad_maximum_fusion
  52.9 0.2 slice.160
  53.2 0.6 copy-done.8
  53.8 0.2 fusion.119
  54.0 5.0 %collective-permute-done = bf16[3,384,1408]{2,1,0:T(8,128)(2,1)S(1)} collective-permute-done((bf16[3,384,1408]{2,1,0:T(8,128)(2,1)S(1)}, bf16[3,384,1408]{2,1,0:T(8,128)(2,1)S(1)}, u32[]{:S(2)}, u32[]{:S(2)}) %collective-permute-start) | collective-permute-done | bytes 3244064 | tf_op jit(solution)/shard_map/ppermute | solution.py:105
  59.0 2.6 add_convert_fusion
  61.6 0.6 broadcast_in_dim.34
  62.2 7.2 %all-to-all-start.1 = ((f32[8,256,2]{1,2,0:T(2,128)}), f32[8,256,2]{1,2,0:T(2,128)S(1)}, u32[]{:S(2)}, u32[]{:S(2)}) async-start(f32[8,256,2]{1,2,0:T(2,128)} %broadcast_in_dim.34), calls=%async_computation.1 | async-start | bytes 32768 | tf_op jit(solution)/shard_map/all_to_all | solution.py:39
  69.4 0.3 iota_compare_fusion
  70.1 4.8 %all-to-all-done.1 = f32[8,256,2]{1,2,0:T(2,128)S(1)} async-done(((f32[8,256,2]{1,2,0:T(2,128)}), f32[8,256,2]{1,2,0:T(2,128)S(1)}, u32[]{:S(2)}, u32[]{:S(2)}) %all-to-all-start.1) | async-done | bytes 16416 | tf_op jit(solution)/shard_map/all_to_all | solution.py:39
  75.8 1.0 select_reduce_fusion
  76.9 13.1 %all_to_all.26 = bf16[32,4,24]{2,1,0:T(4,128)(2,1)S(1)} all-to-all(bf16[32,4,24]{2,1,0:T(4,128)(2,1)S(1)} %copy.97), channel_id=1, replica_groups=mesh['ctx'=32,'head'=8] {'ctx'}, dimensions={0} | all-to-all | bytes 12288 | tf_op jit(solution)/shard_map/all_to_all | solution.py:129
  90.4 106.6 %all-reduce.3.cloned.1.call-done = bf16[3,384,1408]{2,1,0:T(8,128)(2,1)} async-done(((bf16[3,384,1408]{2,1,0:T(8,128)(2,1)}), bf16[3,384,1408]{2,1,0:T(8,128)(2,1)}) %all-reduce.3.cloned.1.call-update) | async-done | bytes 3244048 | tf_op jit(solution)/shard_map/psum | solution.py:108
  197.0 2.2 constant_dynamic-update-slice_fusion.1
  199.2 3.9 %collective-permute-done.1 = bf16[3,384,1408]{2,1,0:T(8,128)(2,1)} collective-permute-done((bf16[3,384,1408]{2,1,0:T(8,128)(2,1)}, bf16[3,384,1408]{2,1,0:T(8,128)(2,1)}, u32[]{:S(2)}, u32[]{:S(2)}) %collective-permute-start.1) | collective-permute-done | bytes 3244064 | tf_op jit(solution)/shard_map/ppermute | solution.py:140
  203.1 2.4 constant_dynamic-update-slice_fusion
  205.5 3.4 %fusion.11 = (f32[768]{0:T(1024)S(1)}, bf16[768,1408]{1,0:T(8,128)(2,1)}) fusion(bf16[3,768,1408]{2,1,0:T(8,128)(2,1)S(1)} %constant_dynamic-update-slice_fusion), kind=kLoop, calls=%fused_computation.23 | loop fusion | flops 12975360 | bytes 8653824 | tf_op jit(solution)/shard_map/reduce_sum | solution.py:160
  208.9 2.4 fusion.60
  211.4 3.7 %fusion.39 = f32[768,512]{1,0:T(8,128)S(1)} fusion(f32[768]{0:T(1024)S(1)} %get-tuple-element.44, bf16[1,1408,512]{2,1,0:T(8,128)(2,1)S(1)} %copy-done.12, bf16[3,768,1408]{2,1,0:T(8,128)(2,1)} %copy-done.2), kind=kOutput, calls=%fused_computation.56 | convolution fusion | flops 1117028352 | bytes 7343104 | tf_op jit(solution)/shard_map/dot_general | solution.py:153
  215.2 6.3 %add_convert_fusion.1 = bf16[768,512]{1,0:T(8,128)(2,1)} fusion(f32[768,512]{1,0:T(8,128)S(1)} %fusion.39, f32[768]{0:T(1024)S(1)} %get-tuple-element.44, bf16[1,1408,512]{2,1,0:T(8,128)(2,1)S(1)} %copy-done.14, bf16[3,768,1408]{2,1,0:T(8,128)(2,1)} %copy-done.2), kind=kOutput, calls=%fused_computation.67 | convolution fusion | flops 1123221504 | bytes 10292224 | tf_op jit(solution)/shard_map/dot_general | solution.py:152
  221.6 0.3 copy.105
  221.9 0.3 copy.106
  222.1 0.2 copy.101
  222.3 0.8 copy.102
  223.2 2.3 concatenate.37
  225.5 1.0 fusion.115
  226.5 0.7 copy-done.6
  227.2 1.2 fusion.85
  228.5 0.3 reshape.265
  228.8 1.4 pad_maximum_fusion.1
  230.2 2.5 concatenate.42
  232.8 0.2 broadcast_select_fusion
  233.0 1.5 pad_maximum_fusion.2
  234.4 7.3 %all-to-all-start.3 = ((bf16[32,24,1152]{2,1,0:T(8,128)(2,1)}), bf16[32,24,1152]{2,1,0:T(8,128)(2,1)S(1)}, u32[]{:S(2)}, u32[]{:S(2)}) async-start(bf16[32,24,1152]{2,1,0:T(8,128)(2,1)} %pad_maximum_fusion.2), calls=%async_computation.3 | async-start | bytes 3538944 | tf_op jit(solution)/shard_map/all_to_all | solution.py:185
  241.7 0.3 iota_compare_fusion.1
  242.0 1.3 eq.124
  243.3 4.4 %fusion.33 = bf16[1,1408,512]{2,1,0:T(8,128)(2,1)} fusion(bf16[768,1408]{1,0:T(8,128)(2,1)} %get-tuple-element.53, f32[768]{0:T(1024)S(1)} %get-tuple-element.44, bf16[768,1024]{1,0:T(8,128)(2,1)} %copy-done.5), kind=kOutput, calls=%fused_computation.52 | convolution fusion | flops 1111261184 | bytes 4393984 | tf_op jit(solution)/shard_map/dot_general | solution.py:8
  247.7 5.6 %fusion.32 = bf16[1,1408,512]{2,1,0:T(8,128)(2,1)} fusion(f32[768]{0:T(1024)S(1)} %get-tuple-element.44, bf16[3,768,1408]{2,1,0:T(8,128)(2,1)} %copy-done.2, bf16[768,1024]{1,0:T(8,128)(2,1)S(1)} %copy-done.7), kind=kOutput, calls=%fused_computation.51 | convolution fusion | flops 1117749248 | bytes 6557696 | tf_op jit(solution)/shard_map/dot_general | solution.py:8
  253.3 3.9 %fusion.31 = bf16[1,1408,512]{2,1,0:T(8,128)(2,1)} fusion(f32[768]{0:T(1024)S(1)} %get-tuple-element.44, bf16[3,768,1408]{2,1,0:T(8,128)(2,1)S(1)} %bitcast.155, bf16[768,1024]{1,0:T(8,128)(2,1)S(1)} %copy-done.7), kind=kOutput, calls=%fused_computation.50 | convolution fusion | flops 1123155968 | bytes 8720384 | tf_op jit(solution)/shard_map/dot_general | solution.py:8
  257.2 12.6 %all-to-all-done.3 = bf16[32,24,1152]{2,1,0:T(8,128)(2,1)S(1)} async-done(((bf16[32,24,1152]{2,1,0:T(8,128)(2,1)}), bf16[32,24,1152]{2,1,0:T(8,128)(2,1)S(1)}, u32[]{:S(2)}, u32[]{:S(2)}) %all-to-all-start.3) | async-done | bytes 1769504 | tf_op jit(solution)/shard_map/all_to_all | solution.py:185
  269.9 3.4 %fusion.118 = (bf16[256,2,1152]{2,0,1:T(8,128)(2,1)}, f32[256,2,1152]{2,0,1:T(8,128)S(1)}) fusion(bf16[768,1152,1]{1,0,2:T(8,128)(2,1)S(1)} %bitcast.162, pred[256,2,768]{2,1,0:T(4,128)(4,1)} %eq.124), kind=kOutput, calls=%fused_computation.168 | convolution fusion | flops 906559488 | bytes 5701632 | tf_op jit(solution)/shard_map/dot_general | solution.py:200
  273.3 0.2 fusion.94
  273.7 0.2 reshape.267
  274.0 0.7 broadcast_in_dim.40
  274.6 3.9 %all-to-all-start.4 = ((f32[32,1,512]{2,1,0:T(1,128)}), f32[32,1,512]{2,1,0:T(1,128)S(1)}, u32[]{:S(2)}, u32[]{:S(2)}) async-start(f32[32,1,512]{2,1,0:T(1,128)} %broadcast_in_dim.40), calls=%async_computation.4 | async-start | bytes 131072 | tf_op jit(solution)/shard_map/all_to_all | solution.py:193
  278.5 2.2 fusion.68
  280.6 2.0 multiply_reduce_fusion
  282.6 4.3 %all-to-all-done.4 = f32[32,1,512]{2,1,0:T(1,128)S(1)} async-done(((f32[32,1,512]{2,1,0:T(1,128)}), f32[32,1,512]{2,1,0:T(1,128)S(1)}, u32[]{:S(2)}, u32[]{:S(2)}) %all-to-all-start.4) | async-done | bytes 65568 | tf_op jit(solution)/shard_map/all_to_all | solution.py:193
  287.0 0.2 reduce.5
  287.2 0.7 copy.109
  (90 shorter events, 3.4 us)
Async XLA Ops:
  7.2 43.3 %copy-start = (bf16[1,1408,512]{2,1,0:T(8,128)(2,1)S(1)}, bf16[1,1408,512]{2,1,0:T(8,128)(2,1)}, u32[]{:S(2)}) copy-start(bf16[1,1408,512]{2,1,0:T(8,128)(2,1)} %param.13) | copy-start | bytes 4325380
  13.9 31.7 %all-to-all-start = ((bf16[32,24,1024]{2,1,0:T(8,128)(2,1)}), bf16[32,24,1024]{2,1,0:T(8,128)(2,1)S(1)}, u32[]{:S(2)}, u32[]{:S(2)}) async-start(bf16[32,24,1024]{2,1,0:T(8,128)(2,1)} %bitcast.157), calls=%async_computation | async-start | bytes 3145728 | tf_op jit(solution)/shard_map/all_to_all | solution.py:75
  22.6 174.4 %all-reduce.3.cloned.1.call-start = ((), (), s32[]{:S(2)}) async-start(), calls=%async_computation.5 | async-start | bytes 6488064 | tf_op jit(solution)/shard_map/psum | solution.py:108
  45.7 1.4 copy-start.13
  47.1 3.4 %copy-start.5 = (bf16[768,1024]{1,0:T(8,128)(2,1)}, bf16[768,1024]{1,0:T(8,128)(2,1)S(1)}, u32[]{:S(2)}) copy-start(bf16[768,1024]{1,0:T(8,128)(2,1)S(1)} %maximum_select_fusion) | copy-start | bytes 4718596
  47.1 1.9 copy-start.11
  52.8 1.0 copy-start.8
  52.8 0.9 copy-start.10
  52.9 1.1 copy-start.9
  53.1 5.9 %collective-permute-start = (bf16[3,384,1408]{2,1,0:T(8,128)(2,1)S(1)}, bf16[3,384,1408]{2,1,0:T(8,128)(2,1)S(1)}, u32[]{:S(2)}, u32[]{:S(2)}) collective-permute-start(bf16[3,384,1408]{2,1,0:T(8,128)(2,1)S(1)} %slice.160), channel_id=1, source_target_pairs={{0,1},{1,0},{2,3},{3,2},{4,5},{5,4},{6,7},{7,6},{8,9},{9,8},{10,11... | collective-permute-start | bytes 9732104 | tf_op jit(solution)/shard_map/ppermute | solution.py:105
  62.2 12.7 %all-to-all-start.1 = ((f32[8,256,2]{1,2,0:T(2,128)}), f32[8,256,2]{1,2,0:T(2,128)S(1)}, u32[]{:S(2)}, u32[]{:S(2)}) async-start(f32[8,256,2]{1,2,0:T(2,128)} %broadcast_in_dim.34), calls=%async_computation.1 | async-start | bytes 32768 | tf_op jit(solution)/shard_map/all_to_all | solution.py:39
  197.0 6.1 %collective-permute-start.1 = (bf16[3,384,1408]{2,1,0:T(8,128)(2,1)}, bf16[3,384,1408]{2,1,0:T(8,128)(2,1)}, u32[]{:S(2)}, u32[]{:S(2)}) collective-permute-start(bf16[3,384,1408]{2,1,0:T(8,128)(2,1)} %all-reduce.3.cloned.1.call-done), channel_id=1, source_target_pairs={{0,1},{1,0},{2,3},{3,2},{4,5},{5,4},{6,7},{7,6},{8,9},{9,8},{10,11... | collective-permute-start | bytes 9732104 | tf_op jit(solution)/shard_map/ppermute | solution.py:140
  205.5 3.4 %copy-start.2 = (bf16[3,768,1408]{2,1,0:T(8,128)(2,1)}, bf16[3,768,1408]{2,1,0:T(8,128)(2,1)S(1)}, u32[]{:S(2)}) copy-start(bf16[3,768,1408]{2,1,0:T(8,128)(2,1)S(1)} %constant_dynamic-update-slice_fusion) | copy-start | bytes 19464196
  208.9 2.5 copy-start.12
  211.4 3.8 %copy-start.14 = (bf16[1,1408,512]{2,1,0:T(8,128)(2,1)S(1)}, bf16[1,1408,512]{2,1,0:T(8,128)(2,1)}, u32[]{:S(2)}) copy-start(bf16[1,1408,512]{2,1,0:T(8,128)(2,1)} %param.11) | copy-start | bytes 4325380
  215.1 8.0 %copy-start.4 = (bf16[768,512]{1,0:T(8,128)(2,1)S(1)}, bf16[768,512]{1,0:T(8,128)(2,1)}, u32[]{:S(2)}) copy-start(bf16[768,512]{1,0:T(8,128)(2,1)} %fusion.60) | copy-start | bytes 2359300
  225.4 1.7 copy-start.6
  226.5 2.3 copy-start.3
  234.4 35.4 %all-to-all-start.3 = ((bf16[32,24,1152]{2,1,0:T(8,128)(2,1)}), bf16[32,24,1152]{2,1,0:T(8,128)(2,1)S(1)}, u32[]{:S(2)}, u32[]{:S(2)}) async-start(bf16[32,24,1152]{2,1,0:T(8,128)(2,1)} %pad_maximum_fusion.2), calls=%async_computation.3 | async-start | bytes 3538944 | tf_op jit(solution)/shard_map/all_to_all | solution.py:185
  243.3 4.5 %copy-start.7 = (bf16[768,1024]{1,0:T(8,128)(2,1)S(1)}, bf16[768,1024]{1,0:T(8,128)(2,1)}, u32[]{:S(2)}) copy-start(bf16[768,1024]{1,0:T(8,128)(2,1)} %copy-done.5) | copy-start | bytes 4718596
  243.3 10.0 %slice-start = ((s8[6488064]{0:T(1024)(128)(4,1)}), s8[4194304]{0:T(1024)(128)(4,1)S(1)}, s32[]{:S(2)}) async-start(s8[6488064]{0:T(1024)(128)(4,1)} %bitcast.154), calls=%async_computation.6 | async-start | bytes 8388608
  247.7 5.6 %slice-start.1 = ((s8[6488064]{0:T(1024)(128)(4,1)}), s8[2293760]{0:T(1024)(128)(4,1)S(1)}, s32[]{:S(2)}) async-start(s8[6488064]{0:T(1024)(128)(4,1)} %bitcast.154), calls=%async_computation.7 | async-start | bytes 4587520
  269.9 18.1 %copy-start.1 = (bf16[1,1408,512]{2,1,0:T(8,128)(2,1)S(1)}, bf16[1,1408,512]{2,1,0:T(8,128)(2,1)}, u32[]{:S(2)}) copy-start(bf16[1,1408,512]{2,1,0:T(8,128)(2,1)} %param.13) | copy-start | bytes 4325380
  274.6 12.3 %all-to-all-start.4 = ((f32[32,1,512]{2,1,0:T(1,128)}), f32[32,1,512]{2,1,0:T(1,128)S(1)}, u32[]{:S(2)}, u32[]{:S(2)}) async-start(f32[32,1,512]{2,1,0:T(1,128)} %broadcast_in_dim.40), calls=%async_computation.4 | async-start | bytes 131072 | tf_op jit(solution)/shard_map/all_to_all | solution.py:193
Sparse Core Ops, SparseCore 0:
  61.7 135.2 all-reduce.2

commit v12 on v8

--- a/solution.py
+++ b/solution.py
@@ -179,6 +179,9 @@
         concat_axis=0,
         tiled=True,
     )
+    router_part, grad_gate, grad_up, grad_down = lax.optimization_barrier(
+        (router_part, grad_gate, grad_up, grad_down)
+    )
     grad_router = ctx_sum(router_part)
     both_pairs = lax.dot_general(
         pick_hit.astype(jnp.bfloat16),

time: 294 us -> 301 us (1.024)
  waiting for transfers between devices: 153 us -> 167 us
  matrix products: 37 us -> 31.9 us
    all_to_all x1, waiting for transfers between devices: 5.61 us -> 19.6 us  [local(): lax.all_to_all(local_order(jnp.concatenate([out_rows, dx_rows, extra], ax...]
    dot_general x3, matrix products: 13.9 us -> 9.71 us  [contract_rows(): lax.dot_general(left, right, (((0,), (0,)), ((), ())), preferred_element_...]
    unnamed x39 -> x33, local copies, waits for them, and re-layouts: 7.32 us -> 7.05 us
  transfers between devices with their start and end apart: 8 -> 8, of which waited for: 7 -> 7; matrix products, arithmetic and copies ran while one was open for 14% -> 8% of each run, Pallas kernels for 0% -> 0%
where the time goes in v12:
time: 301 us; the launch traced here: 298 us
  waiting for transfers between devices  167 us (55%)
  starting transfers between devices  35.4 us (12%)
  matrix products  31.9 us (11%)
  other arithmetic  19.5 us (6%)
  local copies, waits for them, and re-layouts  16.2 us (5%)
  between operations  14.6 us (5%)
  blocking collectives  13.1 us (4%)
    psum x1, waiting for transfers between devices, local(): mine = lax.psum(pair_sum, 'head', axis_index_groups=same_core)  107 us
    all_to_all x1, waiting for transfers between devices, local(): lax.all_to_all(packed.reshape(experts, capacity, 2 * shard_width), 'ctx',...  22.9 us
    all_to_all x1, waiting for transfers between devices, local(): lax.all_to_all(local_order(jnp.concatenate([out_rows, dx_rows, extra], ax...  19.6 us
    all_to_all x1, blocking collectives, local(): lax.all_to_all(slot_values.reshape(4, experts, capacity).transpose(1, 0,...  13.1 us
    dot_general x3, matrix products, contract_rows(): lax.dot_general(left, right, (((0,), (0,)), ((), ())), preferred_element_...  9.71 us
    all_to_all x1, starting transfers between devices, local(): lax.all_to_all(packed.reshape(experts, capacity, 2 * shard_width), 'ctx',...  8.68 us
    all_to_all x1, starting transfers between devices, ctx_sum(): lax.all_to_all(spread, 'ctx', split_axis=0, concat_axis=0, tiled=True)  8.09 us
    all_to_all x1, starting transfers between devices, ctx_sum(): lax.all_to_all(pieces, 'ctx', split_axis=0, concat_axis=0, tiled=True)  7.27 us
  transfers between devices with their start and end apart: 8, of which 7 were waited for; matrix products, arithmetic and copies ran while one was open for 8% of the time, Pallas kernels for 0%

profile of v12, /device:TPU:64, one launch (start us, length us, event | category | flops | bytes accessed | tf_op | source)
XLA Modules:
  0.0 297.8 jit_solution(11469457756111174418)
XLA Ops:
  7.2 0.9 copy.83
  8.4 1.2 reduce-window.6
  9.6 0.2 slice_reduce_fusion
  10.2 0.7 multiply_add_fusion.1
  10.9 0.3 fusion.49
  11.2 2.8 convolution_convert_fusion.6
  13.9 8.7 %all-to-all-start = ((bf16[32,24,1024]{2,1,0:T(8,128)(2,1)}), bf16[32,24,1024]{2,1,0:T(8,128)(2,1)S(1)}, u32[]{:S(2)}, u32[]{:S(2)}) async-start(bf16[32,24,1024]{2,1,0:T(8,128)(2,1)} %bitcast.158), calls=%async_computation | async-start | bytes 3145728 | tf_op jit(solution)/shard_map/all_to_all | solution.py:75
  22.7 22.9 %all-to-all-done = bf16[32,24,1024]{2,1,0:T(8,128)(2,1)S(1)} async-done(((bf16[32,24,1024]{2,1,0:T(8,128)(2,1)}), bf16[32,24,1024]{2,1,0:T(8,128)(2,1)S(1)}, u32[]{:S(2)}, u32[]{:S(2)}) %all-to-all-start) | async-done | bytes 1572896 | tf_op jit(solution)/shard_map/all_to_all | solution.py:75
  45.7 0.8 maximum_select_fusion.1
  46.6 0.5 copy-done.12
  47.1 1.4 fusion.28
  48.5 1.4 fusion.29
  50.0 1.4 fusion.30
  51.4 0.9 pad_maximum_fusion
  52.4 0.2 slice.173
  52.7 0.6 copy-done.7
  53.3 0.2 fusion.118
  53.5 5.0 %collective-permute-done = bf16[3,384,1408]{2,1,0:T(8,128)(2,1)S(1)} collective-permute-done((bf16[3,384,1408]{2,1,0:T(8,128)(2,1)S(1)}, bf16[3,384,1408]{2,1,0:T(8,128)(2,1)S(1)}, u32[]{:S(2)}, u32[]{:S(2)}) %collective-permute-start) | collective-permute-done | bytes 3244064 | tf_op jit(solution)/shard_map/ppermute | solution.py:105
  58.5 2.6 add_convert_fusion
  61.1 0.6 broadcast_in_dim.34
  61.7 7.2 %all-to-all-start.1 = ((f32[8,256,2]{1,2,0:T(2,128)}), f32[8,256,2]{1,2,0:T(2,128)S(1)}, u32[]{:S(2)}, u32[]{:S(2)}) async-start(f32[8,256,2]{1,2,0:T(2,128)} %broadcast_in_dim.34), calls=%async_computation.1 | async-start | bytes 32768 | tf_op jit(solution)/shard_map/all_to_all | solution.py:39
  69.0 0.3 iota_compare_fusion
  69.5 0.1 convert_element_type.220
  69.6 4.8 %all-to-all-done.1 = f32[8,256,2]{1,2,0:T(2,128)S(1)} async-done(((f32[8,256,2]{1,2,0:T(2,128)}), f32[8,256,2]{1,2,0:T(2,128)S(1)}, u32[]{:S(2)}, u32[]{:S(2)}) %all-to-all-start.1) | async-done | bytes 16416 | tf_op jit(solution)/shard_map/all_to_all | solution.py:39
  74.7 0.1 stack_reshape.9
  74.9 0.1 stack_reshape.10
  75.2 0.1 stack_reshape.11
  75.3 1.0 select_reduce_fusion
  76.4 13.1 %all_to_all.30 = bf16[32,4,24]{2,1,0:T(4,128)(2,1)S(1)} all-to-all(bf16[32,4,24]{2,1,0:T(4,128)(2,1)S(1)} %copy.89), channel_id=1, replica_groups=mesh['ctx'=32,'head'=8] {'ctx'}, dimensions={0} | all-to-all | bytes 12288 | tf_op jit(solution)/shard_map/all_to_all | solution.py:129
  89.9 106.6 %all-reduce.3.cloned.1.call-done = bf16[3,384,1408]{2,1,0:T(8,128)(2,1)} async-done(((bf16[3,384,1408]{2,1,0:T(8,128)(2,1)}), bf16[3,384,1408]{2,1,0:T(8,128)(2,1)}) %all-reduce.3.cloned.1.call-update) | async-done | bytes 3244048 | tf_op jit(solution)/shard_map/psum | solution.py:108
  196.5 0.6 compare_reduce_fusion
  197.2 0.6 compare_reduce_fusion.1
  197.8 2.2 constant_dynamic-update-slice_fusion.1
  200.0 2.6 collective-permute-done.1
  202.7 2.4 constant_dynamic-update-slice_fusion
  205.1 2.3 fusion.11
  207.4 0.2 copy-done.6
  207.6 3.2 %fusion.32 = bf16[1,1408,512]{2,1,0:T(8,128)(2,1)} fusion(f32[768]{0:T(1024)S(1)} %get-tuple-element.77, bf16[3,768,1408]{2,1,0:T(8,128)(2,1)S(1)} %constant_dynamic-update-slice_fusion, bf16[768,1024]{1,0:T(8,128)(2,1)S(1)} %copy-done.6), kind=kOutput, calls=%fused_computation.51 | convolution fusion | flops 1117749248 | bytes 6557696 | tf_op jit(solution)/shard_map/dot_general | solution.py:8
  210.9 3.9 %fusion.31 = bf16[1,1408,512]{2,1,0:T(8,128)(2,1)} fusion(f32[768]{0:T(1024)S(1)} %get-tuple-element.77, bf16[3,768,1408]{2,1,0:T(8,128)(2,1)S(1)} %constant_dynamic-update-slice_fusion, bf16[768,1024]{1,0:T(8,128)(2,1)S(1)} %copy-done.6), kind=kOutput, calls=%fused_computation.50 | convolution fusion | flops 1123155968 | bytes 8720384 | tf_op jit(solution)/shard_map/dot_general | solution.py:8
  214.8 3.0 %fusion.39 = f32[768,512]{1,0:T(8,128)} fusion(f32[768]{0:T(1024)S(1)} %get-tuple-element.77, bf16[1,1408,512]{2,1,0:T(8,128)(2,1)S(1)} %copy-done, bf16[3,768,1408]{2,1,0:T(8,128)(2,1)S(1)} %constant_dynamic-update-slice_fusion), kind=kOutput, calls=%fused_computation.56 | convolution fusion | flops 1117028352 | bytes 7344128 | tf_op jit(solution)/shard_map/dot_general | solution.py:153
  217.8 1.5 fusion.60
  219.3 2.5 fusion.33
  221.9 0.8 fusion.85
  222.8 0.8 reshape.294
  223.6 7.3 %all-to-all-start.4 = ((f32[32,1,512]{2,1,0:T(1,128)}), f32[32,1,512]{2,1,0:T(1,128)S(1)}, u32[]{:S(2)}, u32[]{:S(2)}) async-start(f32[32,1,512]{2,1,0:T(1,128)} %reshape.294), calls=%async_computation.4 | async-start | bytes 131072 | tf_op jit(solution)/shard_map/all_to_all | solution.py:47
  230.8 6.2 %add_convert_fusion.1 = bf16[768,512]{1,0:T(8,128)(2,1)S(1)} fusion(f32[768,512]{1,0:T(8,128)} %fusion.39, f32[768]{0:T(1024)S(1)} %get-tuple-element.77, bf16[1,1408,512]{2,1,0:T(8,128)(2,1)} %param.15, bf16[3,768,1408]{2,1,0:T(8,128)(2,1)} %copy-done.2), kind=kOutput, calls=%fused_computation.67 | convolution fusion | flops 1123221504 | bytes 10292224 | tf_op jit(solution)/shard_map/dot_general | solution.py:152
  237.1 1.6 fusion.95
  238.7 1.4 scatter.9
  240.6 0.5 broadcast.240
  241.1 0.8 reduce.26
  242.1 0.8 reshape.296
  242.9 8.1 %all-to-all-start.5 = ((f32[32,1,512]{2,1,0:T(1,128)}), f32[32,1,512]{2,1,0:T(1,128)S(1)}, u32[]{:S(2)}, u32[]{:S(2)}) async-start(f32[32,1,512]{2,1,0:T(1,128)} %reshape.296), calls=%async_computation.5 | async-start | bytes 131072 | tf_op jit(solution)/shard_map/all_to_all | solution.py:49
  251.0 3.0 %maximum_select_fusion = bf16[32,24,1152]{2,1,0:T(8,128)(2,1)} fusion(bf16[32,24,1152]{2,1,0:T(8,128)(2,1)S(1)} %bitcast.157, bf16[32,24,128]{2,1,0:T(8,128)(2,1)S(1)} %bitcast.163, bf16[32,24,512]{2,1,0:T(8,128)(2,1)} %bitcast.162, bf16[32,24,512]{2,1,0:T(8,128)(2,1)} %bitcast.161, pred[]{:T(512)S(6)} %eq.106), kind=kLoop, calls=%fused_computation.64 | loop fusion | flops 6193152 | bytes 5308417 | tf_op jit(solution)/shard_map/jit(_where)/select_n | solution.py:88
  254.0 5.4 %all-to-all-done.5 = f32[32,1,512]{2,1,0:T(1,128)S(1)} async-done(((f32[32,1,512]{2,1,0:T(1,128)}), f32[32,1,512]{2,1,0:T(1,128)S(1)}, u32[]{:S(2)}, u32[]{:S(2)}) %all-to-all-start.5) | async-done | bytes 65568 | tf_op jit(solution)/shard_map/all_to_all | solution.py:49
  259.5 4.0 %all-to-all-start.3 = ((bf16[32,24,1152]{2,1,0:T(8,128)(2,1)}), bf16[32,24,1152]{2,1,0:T(8,128)(2,1)S(1)}, u32[]{:S(2)}, u32[]{:S(2)}) async-start(bf16[32,24,1152]{2,1,0:T(8,128)(2,1)} %maximum_select_fusion), calls=%async_computation.3 | async-start | bytes 3538944 | tf_op jit(solution)/shard_map/all_to_all | solution.py:173
  263.5 0.3 iota_compare_fusion.1
  263.8 1.2 eq.124
  265.0 0.8 reduce.27
  265.9 0.7 copy.97
  266.7 19.6 %all-to-all-done.3 = bf16[32,24,1152]{2,1,0:T(8,128)(2,1)S(1)} async-done(((bf16[32,24,1152]{2,1,0:T(8,128)(2,1)}), bf16[32,24,1152]{2,1,0:T(8,128)(2,1)S(1)}, u32[]{:S(2)}, u32[]{:S(2)}) %all-to-all-start.3) | async-done | bytes 1769504 | tf_op jit(solution)/shard_map/all_to_all | solution.py:173
  286.2 2.4 fusion.117
  288.7 0.2 fusion.93
  289.0 0.9 multiply_reduce_fusion
  289.8 1.1 fusion.68
  (76 shorter events, 3.1 us)
Async XLA Ops:
  7.2 41.4 %copy-start = (bf16[1,1408,512]{2,1,0:T(8,128)(2,1)S(1)}, bf16[1,1408,512]{2,1,0:T(8,128)(2,1)}, u32[]{:S(2)}) copy-start(bf16[1,1408,512]{2,1,0:T(8,128)(2,1)} %param.16) | copy-start | bytes 4325380
  13.9 31.7 %all-to-all-start = ((bf16[32,24,1024]{2,1,0:T(8,128)(2,1)}), bf16[32,24,1024]{2,1,0:T(8,128)(2,1)S(1)}, u32[]{:S(2)}, u32[]{:S(2)}) async-start(bf16[32,24,1024]{2,1,0:T(8,128)(2,1)} %bitcast.158), calls=%async_computation | async-start | bytes 3145728 | tf_op jit(solution)/shard_map/all_to_all | solution.py:75
  22.6 173.9 %all-reduce.3.cloned.1.call-start = ((), (), s32[]{:S(2)}) async-start(), calls=%async_computation.6 | async-start | bytes 6488064 | tf_op jit(solution)/shard_map/psum | solution.py:108
  45.7 1.4 copy-start.12
  47.1 2.9 copy-start.5
  48.5 1.5 copy-start.10
  52.3 1.0 copy-start.7
  52.4 0.9 copy-start.9
  52.4 1.1 copy-start.8
  52.6 5.9 %collective-permute-start = (bf16[3,384,1408]{2,1,0:T(8,128)(2,1)S(1)}, bf16[3,384,1408]{2,1,0:T(8,128)(2,1)S(1)}, u32[]{:S(2)}, u32[]{:S(2)}) collective-permute-start(bf16[3,384,1408]{2,1,0:T(8,128)(2,1)S(1)} %slice.173), channel_id=1, source_target_pairs={{0,1},{1,0},{2,3},{3,2},{4,5},{5,4},{6,7},{7,6},{8,9},{9,8},{10,11... | collective-permute-start | bytes 9732104 | tf_op jit(solution)/shard_map/ppermute | solution.py:105
  61.7 12.7 %all-to-all-start.1 = ((f32[8,256,2]{1,2,0:T(2,128)}), f32[8,256,2]{1,2,0:T(2,128)S(1)}, u32[]{:S(2)}, u32[]{:S(2)}) async-start(f32[8,256,2]{1,2,0:T(2,128)} %broadcast_in_dim.34), calls=%async_computation.1 | async-start | bytes 32768 | tf_op jit(solution)/shard_map/all_to_all | solution.py:39
  196.5 6.1 %collective-permute-start.1 = (bf16[3,384,1408]{2,1,0:T(8,128)(2,1)}, bf16[3,384,1408]{2,1,0:T(8,128)(2,1)}, u32[]{:S(2)}, u32[]{:S(2)}) collective-permute-start(bf16[3,384,1408]{2,1,0:T(8,128)(2,1)} %all-reduce.3.cloned.1.call-done), channel_id=1, source_target_pairs={{0,1},{1,0},{2,3},{3,2},{4,5},{5,4},{6,7},{7,6},{8,9},{9,8},{10,11... | collective-permute-start | bytes 9732104 | tf_op jit(solution)/shard_map/ppermute | solution.py:140
  205.1 12.7 %copy-start.2 = (bf16[3,768,1408]{2,1,0:T(8,128)(2,1)}, bf16[3,768,1408]{2,1,0:T(8,128)(2,1)S(1)}, u32[]{:S(2)}) copy-start(bf16[3,768,1408]{2,1,0:T(8,128)(2,1)S(1)} %constant_dynamic-update-slice_fusion) | copy-start | bytes 19464196
  205.1 2.6 copy-start.6
  214.8 3.0 %copy-start.11 = (bf16[1,1408,512]{2,1,0:T(8,128)(2,1)S(1)}, bf16[1,1408,512]{2,1,0:T(8,128)(2,1)}, u32[]{:S(2)}) copy-start(bf16[1,1408,512]{2,1,0:T(8,128)(2,1)} %param.17) | copy-start | bytes 4325380
  219.3 20.8 %copy-start.3 = (bf16[768,512]{1,0:T(8,128)(2,1)}, bf16[768,512]{1,0:T(8,128)(2,1)S(1)}, u32[]{:S(2)}) copy-start(bf16[768,512]{1,0:T(8,128)(2,1)S(1)} %fusion.60) | copy-start | bytes 2359300
  223.6 17.0 %all-to-all-start.4 = ((f32[32,1,512]{2,1,0:T(1,128)}), f32[32,1,512]{2,1,0:T(1,128)S(1)}, u32[]{:S(2)}, u32[]{:S(2)}) async-start(f32[32,1,512]{2,1,0:T(1,128)} %reshape.294), calls=%async_computation.4 | async-start | bytes 131072 | tf_op jit(solution)/shard_map/all_to_all | solution.py:47
  237.1 3.4 %copy-start.4 = (bf16[768,512]{1,0:T(8,128)(2,1)}, bf16[768,512]{1,0:T(8,128)(2,1)S(1)}, u32[]{:S(2)}) copy-start(bf16[768,512]{1,0:T(8,128)(2,1)S(1)} %add_convert_fusion.1) | copy-start | bytes 2359300
  242.9 16.6 %all-to-all-start.5 = ((f32[32,1,512]{2,1,0:T(1,128)}), f32[32,1,512]{2,1,0:T(1,128)S(1)}, u32[]{:S(2)}, u32[]{:S(2)}) async-start(f32[32,1,512]{2,1,0:T(1,128)} %reshape.296), calls=%async_computation.5 | async-start | bytes 131072 | tf_op jit(solution)/shard_map/all_to_all | solution.py:49
  259.5 26.8 %all-to-all-start.3 = ((bf16[32,24,1152]{2,1,0:T(8,128)(2,1)}), bf16[32,24,1152]{2,1,0:T(8,128)(2,1)S(1)}, u32[]{:S(2)}, u32[]{:S(2)}) async-start(bf16[32,24,1152]{2,1,0:T(8,128)(2,1)} %maximum_select_fusion), calls=%async_computation.3 | async-start | bytes 3538944 | tf_op jit(solution)/shard_map/all_to_all | solution.py:173
  286.2 4.7 %copy-start.1 = (bf16[1,1408,512]{2,1,0:T(8,128)(2,1)S(1)}, bf16[1,1408,512]{2,1,0:T(8,128)(2,1)}, u32[]{:S(2)}) copy-start(bf16[1,1408,512]{2,1,0:T(8,128)(2,1)} %param.16) | copy-start | bytes 4325380
Sparse Core Ops, SparseCore 0:
  61.2 135.2 all-reduce.2

commit v13 on v8

--- a/solution.py
+++ b/solution.py
@@ -137,16 +137,16 @@
         recv_p.transpose(0, 2, 1).reshape(slot_count, 4)
     ).T.astype(jnp.float32)
     mine, row_values = lax.optimization_barrier((mine, row_values))
-    sums = jnp.concatenate([mine, lax.ppermute(mine, "head", partner)], axis=1)
-    gate_sum, up_sum, back_sum = sums[0], sums[1], sums[2]
+    halves = (mine.astype(jnp.float32), lax.ppermute(mine, "head", partner).astype(jnp.float32))
     prob_rows = row_values[0]
     pair_rows = row_values[1] + row_values[2]
     other_rows = row_values[3].astype(jnp.int32)
-    gate_pre = gate_sum.astype(jnp.float32)
-    up_pre = up_sum.astype(jnp.float32)
-    hidden = forward_act(gate_pre, up_pre)
-    back_proj = back_sum.astype(jnp.float32)
-    gate_grad, up_grad = backward_act(gate_pre, up_pre, back_proj, prob_rows)
+    prob_halves = (prob_rows[:half], prob_rows[half:])
+    hidden = jnp.concatenate([forward_act(h[0], h[1]) for h in halves], axis=0)
+    grads = [backward_act(h[0], h[1], h[2], p) for h, p in zip(halves, prob_halves)]
+    gate_grad = jnp.concatenate([g[0] for g in grads], axis=0)
+    up_grad = jnp.concatenate([g[1] for g in grads], axis=0)
+    back_proj = jnp.concatenate([h[2] for h in halves], axis=0)
     out_rows = jnp.dot(hidden, down_w, preferred_element_type=jnp.float32).astype(jnp.bfloat16)
     dx_rows = (
         jnp.dot(gate_grad, gate_w, preferred_element_type=jnp.float32)

time: 294 us -> 292 us (level)
  matrix products: 37 us -> 25.9 us
  other arithmetic: 20.6 us -> 28 us
  waiting for transfers between devices: 153 us -> 157 us
    convert_element_type x0 -> x4, other arithmetic: none -> 10.3 us  [the longest x2 5.58 us: backward_act(): (hidden_grad * up_pre * sigma * (1.0 + gate_pre * (1.0 - sigma))).astype(...]
    dot_general x3, matrix products: 13.9 us -> 7.39 us  [contract_rows(): lax.dot_general(left, right, (((0,), (0,)), ((), ())), preferred_element_...]
    all_to_all x1, waiting for transfers between devices: 5.61 us -> 10.5 us  [local(): lax.all_to_all(local_order(jnp.concatenate([out_rows, dx_rows, extra], ax...]
    dot_general x1, matrix products: 5.4 us -> 1.37 us  [local(): jnp.dot(gate_grad, gate_w, preferred_element_type=jnp.float32)]
    unnamed x39 -> x46, local copies, waits for them, and re-layouts: 7.32 us -> 7.36 us
  transfers between devices with their start and end apart: 8 -> 8, of which waited for: 7 -> 6; matrix products, arithmetic and copies ran while one was open for 14% -> 11% of each run, Pallas kernels for 0% -> 0%
where the time goes in v13:
time: 292 us; the launch traced here: 289 us
  waiting for transfers between devices  157 us (54%)
  starting transfers between devices  36.3 us (12%)
  other arithmetic  28 us (10%)
  matrix products  25.9 us (9%)
  between operations  14.7 us (5%)
  local copies, waits for them, and re-layouts  14.3 us (5%)
  blocking collectives  13.1 us (4%)
    psum x1, waiting for transfers between devices, local(): mine = lax.psum(pair_sum, 'head', axis_index_groups=same_core)  106 us
    all_to_all x1, waiting for transfers between devices, local(): lax.all_to_all(packed.reshape(experts, capacity, 2 * shard_width), 'ctx',...  22.9 us
    all_to_all x1, blocking collectives, local(): lax.all_to_all(slot_values.reshape(4, experts, capacity).transpose(1, 0,...  13.1 us
    all_to_all x1, waiting for transfers between devices, local(): lax.all_to_all(local_order(jnp.concatenate([out_rows, dx_rows, extra], ax...  10.5 us
    all_to_all x1, starting transfers between devices, local(): lax.all_to_all(packed.reshape(experts, capacity, 2 * shard_width), 'ctx',...  8.68 us
    all_to_all x1, starting transfers between devices, ctx_sum(): lax.all_to_all(spread, 'ctx', split_axis=0, concat_axis=0, tiled=True)  8.3 us
    dot_general x3, matrix products, contract_rows(): lax.dot_general(left, right, (((0,), (0,)), ((), ())), preferred_element_...  7.39 us
    unnamed x46, local copies, waits for them, and re-layouts  7.36 us
  transfers between devices with their start and end apart: 8, of which 6 were waited for; matrix products, arithmetic and copies ran while one was open for 11% of the time, Pallas kernels for 0%

profile of v13, /device:TPU:64, one launch (start us, length us, event | category | flops | bytes accessed | tf_op | source)
XLA Modules:
  0.0 288.9 jit_solution(11942465486380344931)
XLA Ops:
  7.2 0.9 copy.83
  8.4 1.2 reduce-window.6
  9.6 0.2 slice_reduce_fusion
  10.2 0.7 multiply_add_fusion.1
  10.9 0.3 fusion.10
  11.2 2.8 convolution_convert_fusion.6
  13.9 8.7 %all-to-all-start = ((bf16[32,24,1024]{2,1,0:T(8,128)(2,1)}), bf16[32,24,1024]{2,1,0:T(8,128)(2,1)S(1)}, u32[]{:S(2)}, u32[]{:S(2)}) async-start(bf16[32,24,1024]{2,1,0:T(8,128)(2,1)} %bitcast.124), calls=%async_computation | async-start | bytes 3145728 | tf_op jit(solution)/shard_map/all_to_all | solution.py:75
  22.7 22.9 %all-to-all-done = bf16[32,24,1024]{2,1,0:T(8,128)(2,1)S(1)} async-done(((bf16[32,24,1024]{2,1,0:T(8,128)(2,1)}), bf16[32,24,1024]{2,1,0:T(8,128)(2,1)S(1)}, u32[]{:S(2)}, u32[]{:S(2)}) %all-to-all-start) | async-done | bytes 1572896 | tf_op jit(solution)/shard_map/all_to_all | solution.py:75
  45.7 0.8 maximum_select_fusion.1
  46.6 0.5 copy-done.17
  47.1 1.4 fusion.2
  48.5 1.4 fusion.3
  50.0 1.4 fusion.1
  51.4 0.9 pad_maximum_fusion
  52.4 0.2 slice.200
  52.7 0.6 copy-done.13
  53.5 5.0 %collective-permute-done = bf16[3,384,1408]{2,1,0:T(8,128)(2,1)S(1)} collective-permute-done((bf16[3,384,1408]{2,1,0:T(8,128)(2,1)S(1)}, bf16[3,384,1408]{2,1,0:T(8,128)(2,1)S(1)}, u32[]{:S(2)}, u32[]{:S(2)}) %collective-permute-start) | collective-permute-done | bytes 3244064 | tf_op jit(solution)/shard_map/ppermute | solution.py:105
  58.5 2.6 add_convert_fusion
  61.1 0.6 broadcast_in_dim.34
  61.7 7.2 %all-to-all-start.1 = ((f32[8,256,2]{1,2,0:T(2,128)}), f32[8,256,2]{1,2,0:T(2,128)S(1)}, u32[]{:S(2)}, u32[]{:S(2)}) async-start(f32[8,256,2]{1,2,0:T(2,128)} %broadcast_in_dim.34), calls=%async_computation.1 | async-start | bytes 32768 | tf_op jit(solution)/shard_map/all_to_all | solution.py:39
  69.0 0.3 iota_compare_fusion
  69.6 4.8 %all-to-all-done.1 = f32[8,256,2]{1,2,0:T(2,128)S(1)} async-done(((f32[8,256,2]{1,2,0:T(2,128)}), f32[8,256,2]{1,2,0:T(2,128)S(1)}, u32[]{:S(2)}, u32[]{:S(2)}) %all-to-all-start.1) | async-done | bytes 16416 | tf_op jit(solution)/shard_map/all_to_all | solution.py:39
  75.3 1.0 select_reduce_fusion
  76.4 13.1 %all_to_all.30 = bf16[32,4,24]{2,1,0:T(4,128)(2,1)S(1)} all-to-all(bf16[32,4,24]{2,1,0:T(4,128)(2,1)S(1)} %copy.89), channel_id=1, replica_groups=mesh['ctx'=32,'head'=8] {'ctx'}, dimensions={0} | all-to-all | bytes 12288 | tf_op jit(solution)/shard_map/all_to_all | solution.py:129
  89.9 106.4 %all-reduce.3.cloned.1.call-done = bf16[3,384,1408]{2,1,0:T(8,128)(2,1)} async-done(((bf16[3,384,1408]{2,1,0:T(8,128)(2,1)}), bf16[3,384,1408]{2,1,0:T(8,128)(2,1)}) %all-reduce.3.cloned.1.call-update) | async-done | bytes 3244048 | tf_op jit(solution)/shard_map/psum | solution.py:108
  196.3 0.6 compare_reduce_fusion.1
  197.0 0.6 compare_reduce_fusion
  197.6 2.3 convert_element_type.194
  200.2 2.8 multiply_convert_fusion.5
  203.0 2.3 convert_element_type.196
  205.5 2.8 multiply_convert_fusion.4
  208.3 1.4 fusion.22
  209.7 0.5 fusion
  210.2 0.8 copy-done.5
  211.1 1.2 fusion.35
  212.2 0.8 reshape.278
  213.0 7.1 %all-to-all-start.4 = ((f32[32,1,512]{2,1,0:T(1,128)}), f32[32,1,512]{2,1,0:T(1,128)S(1)}, u32[]{:S(2)}, u32[]{:S(2)}) async-start(f32[32,1,512]{2,1,0:T(1,128)} %reshape.278), calls=%async_computation.4 | async-start | bytes 131072 | tf_op jit(solution)/shard_map/all_to_all | solution.py:47
  220.1 1.6 fusion.45
  221.7 1.4 scatter.9
  223.1 3.5 %fusion.16 = f32[768,512]{1,0:T(8,128)S(1)} fusion(bf16[1,1408,512]{2,1,0:T(8,128)(2,1)} %param.16, bf16[384,1408]{1,0:T(8,128)(2,1)} %get-tuple-element.80, bf16[384,1408]{1,0:T(8,128)(2,1)} %get-tuple-element.78), kind=kOutput, calls=%fused_computation.53 | convolution fusion | flops 1111621632 | bytes 5177344 | tf_op jit(solution)/shard_map/dot_general | solution.py:153
  226.7 1.4 add_convert_fusion.1
  228.4 1.4 pad_maximum_fusion.5
  229.7 0.5 broadcast.211
  230.3 0.8 reduce.30
  231.2 0.8 reshape.280
  232.0 8.3 %all-to-all-start.5 = ((f32[32,1,512]{2,1,0:T(1,128)}), f32[32,1,512]{2,1,0:T(1,128)S(1)}, u32[]{:S(2)}, u32[]{:S(2)}) async-start(f32[32,1,512]{2,1,0:T(1,128)} %reshape.280), calls=%async_computation.5 | async-start | bytes 131072 | tf_op jit(solution)/shard_map/all_to_all | solution.py:49
  240.3 1.6 maximum_select_fusion
  242.0 6.8 %all-to-all-done.5 = f32[32,1,512]{2,1,0:T(1,128)S(1)} async-done(((f32[32,1,512]{2,1,0:T(1,128)}), f32[32,1,512]{2,1,0:T(1,128)S(1)}, u32[]{:S(2)}, u32[]{:S(2)}) %all-to-all-start.5) | async-done | bytes 65568 | tf_op jit(solution)/shard_map/all_to_all | solution.py:49
  248.8 4.9 %all-to-all-start.3 = ((bf16[32,24,1152]{2,1,0:T(8,128)(2,1)}), bf16[32,24,1152]{2,1,0:T(8,128)(2,1)}, u32[]{:S(2)}, u32[]{:S(2)}) async-start(bf16[32,24,1152]{2,1,0:T(8,128)(2,1)} %maximum_select_fusion), calls=%async_computation.3 | async-start | bytes 3538944 | tf_op jit(solution)/shard_map/all_to_all | solution.py:173
  253.8 0.3 iota_compare_fusion.1
  254.1 1.2 eq.124
  255.5 1.2 copy-done.6
  256.7 0.3 copy-done.9
  257.0 0.3 copy-done.12
  257.4 2.4 fusion.4
  259.8 2.4 fusion.5
  262.2 2.5 fusion.6
  264.8 0.8 reduce.31
  265.7 0.7 copy.97
  266.4 10.5 %all-to-all-done.3 = bf16[32,24,1152]{2,1,0:T(8,128)(2,1)} async-done(((bf16[32,24,1152]{2,1,0:T(8,128)(2,1)}), bf16[32,24,1152]{2,1,0:T(8,128)(2,1)}, u32[]{:S(2)}, u32[]{:S(2)}) %all-to-all-start.3) | async-done | bytes 1769504 | tf_op jit(solution)/shard_map/all_to_all | solution.py:173
  276.9 2.8 fusion.65
  279.7 0.2 fusion.43
  280.0 0.9 multiply_reduce_fusion
  280.9 1.1 fusion.27
  (95 shorter events, 4.1 us)
Async XLA Ops:
  7.2 41.4 %copy-start = (bf16[1,1408,512]{2,1,0:T(8,128)(2,1)S(1)}, bf16[1,1408,512]{2,1,0:T(8,128)(2,1)}, u32[]{:S(2)}) copy-start(bf16[1,1408,512]{2,1,0:T(8,128)(2,1)} %param.17) | copy-start | bytes 4325380
  13.9 31.7 %all-to-all-start = ((bf16[32,24,1024]{2,1,0:T(8,128)(2,1)}), bf16[32,24,1024]{2,1,0:T(8,128)(2,1)S(1)}, u32[]{:S(2)}, u32[]{:S(2)}) async-start(bf16[32,24,1024]{2,1,0:T(8,128)(2,1)} %bitcast.124), calls=%async_computation | async-start | bytes 3145728 | tf_op jit(solution)/shard_map/all_to_all | solution.py:75
  22.6 173.7 %all-reduce.3.cloned.1.call-start = ((), (), s32[]{:S(2)}) async-start(), calls=%async_computation.6 | async-start | bytes 6488064 | tf_op jit(solution)/shard_map/psum | solution.py:108
  45.7 1.4 copy-start.17
  47.1 2.9 copy-start.4
  48.5 1.5 copy-start.18
  52.3 1.0 copy-start.13
  52.4 0.9 copy-start.16
  52.4 1.1 copy-start.15
  52.6 5.9 %collective-permute-start = (bf16[3,384,1408]{2,1,0:T(8,128)(2,1)S(1)}, bf16[3,384,1408]{2,1,0:T(8,128)(2,1)S(1)}, u32[]{:S(2)}, u32[]{:S(2)}) collective-permute-start(bf16[3,384,1408]{2,1,0:T(8,128)(2,1)S(1)} %slice.200), channel_id=1, source_target_pairs={{0,1},{1,0},{2,3},{3,2},{4,5},{5,4},{6,7},{7,6},{8,9},{9,8},{10,11... | collective-permute-start | bytes 9732104 | tf_op jit(solution)/shard_map/ppermute | solution.py:105
  61.7 12.7 %all-to-all-start.1 = ((f32[8,256,2]{1,2,0:T(2,128)}), f32[8,256,2]{1,2,0:T(2,128)S(1)}, u32[]{:S(2)}, u32[]{:S(2)}) async-start(f32[8,256,2]{1,2,0:T(2,128)} %broadcast_in_dim.34), calls=%async_computation.1 | async-start | bytes 32768 | tf_op jit(solution)/shard_map/all_to_all | solution.py:39
  196.3 6.7 %collective-permute-start.1 = (bf16[3,384,1408]{2,1,0:T(8,128)(2,1)}, bf16[3,384,1408]{2,1,0:T(8,128)(2,1)}, u32[]{:S(2)}, u32[]{:S(2)}) collective-permute-start(bf16[3,384,1408]{2,1,0:T(8,128)(2,1)} %all-reduce.3.cloned.1.call-done), channel_id=1, source_target_pairs={{0,1},{1,0},{2,3},{3,2},{4,5},{5,4},{6,7},{7,6},{8,9},{9,8},{10,11... | collective-permute-start | bytes 9732104 | tf_op jit(solution)/shard_map/ppermute | solution.py:140
  208.3 1.4 copy-start.2
  209.6 1.4 copy-start.5
  213.0 16.7 %all-to-all-start.4 = ((f32[32,1,512]{2,1,0:T(1,128)}), f32[32,1,512]{2,1,0:T(1,128)S(1)}, u32[]{:S(2)}, u32[]{:S(2)}) async-start(f32[32,1,512]{2,1,0:T(1,128)} %reshape.278), calls=%async_computation.4 | async-start | bytes 131072 | tf_op jit(solution)/shard_map/all_to_all | solution.py:47
  223.1 3.6 %copy-start.8 = (bf16[384,1408]{1,0:T(8,128)(2,1)S(1)}, bf16[384,1408]{1,0:T(8,128)(2,1)}, u32[]{:S(2)}) copy-start(bf16[384,1408]{1,0:T(8,128)(2,1)} %get-tuple-element.77) | copy-start | bytes 3244036
  223.1 3.6 %copy-start.11 = (bf16[384,1408]{1,0:T(8,128)(2,1)S(1)}, bf16[384,1408]{1,0:T(8,128)(2,1)}, u32[]{:S(2)}) copy-start(bf16[384,1408]{1,0:T(8,128)(2,1)} %get-tuple-element.79) | copy-start | bytes 3244036
  223.1 3.6 %copy-start.19 = (bf16[1,1408,512]{2,1,0:T(8,128)(2,1)S(1)}, bf16[1,1408,512]{2,1,0:T(8,128)(2,1)}, u32[]{:S(2)}) copy-start(bf16[1,1408,512]{2,1,0:T(8,128)(2,1)} %param.15) | copy-start | bytes 4325380
  232.0 16.8 %all-to-all-start.5 = ((f32[32,1,512]{2,1,0:T(1,128)}), f32[32,1,512]{2,1,0:T(1,128)S(1)}, u32[]{:S(2)}, u32[]{:S(2)}) async-start(f32[32,1,512]{2,1,0:T(1,128)} %reshape.280), calls=%async_computation.5 | async-start | bytes 131072 | tf_op jit(solution)/shard_map/all_to_all | solution.py:49
  242.0 13.3 %copy-start.3 = (bf16[384,1408]{1,0:T(8,128)(2,1)S(1)}, bf16[384,1408]{1,0:T(8,128)(2,1)}, u32[]{:S(2)}) copy-start(bf16[384,1408]{1,0:T(8,128)(2,1)} %copy-done.2) | copy-start | bytes 3244036
  248.8 28.1 %all-to-all-start.3 = ((bf16[32,24,1152]{2,1,0:T(8,128)(2,1)}), bf16[32,24,1152]{2,1,0:T(8,128)(2,1)}, u32[]{:S(2)}, u32[]{:S(2)}) async-start(bf16[32,24,1152]{2,1,0:T(8,128)(2,1)} %maximum_select_fusion), calls=%async_computation.3 | async-start | bytes 3538944 | tf_op jit(solution)/shard_map/all_to_all | solution.py:173
  255.3 1.4 copy-start.6
  255.3 1.7 copy-start.9
  255.3 2.0 copy-start.12
  257.3 2.4 copy-start.7
  257.4 2.4 copy-start.10
  262.2 14.7 %copy-start.14 = (pred[256,2,768]{2,1,0:T(4,128)(4,1)S(1)}, pred[256,2,768]{2,1,0:T(4,128)(4,1)}, u32[]{:S(2)}) copy-start(pred[256,2,768]{2,1,0:T(4,128)(4,1)} %eq.124) | copy-start | bytes 1179652
  276.9 5.1 %copy-start.1 = (bf16[1,1408,512]{2,1,0:T(8,128)(2,1)S(1)}, bf16[1,1408,512]{2,1,0:T(8,128)(2,1)}, u32[]{:S(2)}) copy-start(bf16[1,1408,512]{2,1,0:T(8,128)(2,1)} %param.17) | copy-start | bytes 4325380
Sparse Core Ops, SparseCore 0:
  61.2 135.0 all-reduce.2

commit v14 on v13

--- a/solution.py
+++ b/solution.py
@@ -123,8 +123,11 @@
         ],
         axis=0,
     )
-    slot_values = jnp.sum(
-        jnp.where(pick_hit[None], pick_values[:, None, :], 0.0), axis=2
+    slot_values = lax.dot_general(
+        pick_values.astype(jnp.bfloat16),
+        pick_hit.astype(jnp.bfloat16),
+        (((1,), (1,)), ((), ())),
+        preferred_element_type=jnp.float32,
     ).astype(jnp.bfloat16)
     recv_p = lax.all_to_all(
         slot_values.reshape(4, experts, capacity).transpose(1, 0, 2),

time: 292 us -> 293 us (level)
    unnamed x46 -> x48, local copies, waits for them, and re-layouts: 7.36 us -> 8.21 us
where the time goes in v14:
time: 293 us; the launch traced here: 290 us
  waiting for transfers between devices  156 us (53%)
  starting transfers between devices  36.3 us (12%)
  other arithmetic  28 us (10%)
  matrix products  26.3 us (9%)
  local copies, waits for them, and re-layouts  15.2 us (5%)
  between operations  14.6 us (5%)
  blocking collectives  13 us (4%)
    psum x1, waiting for transfers between devices, local(): mine = lax.psum(pair_sum, 'head', axis_index_groups=same_core)  107 us
    all_to_all x1, waiting for transfers between devices, local(): lax.all_to_all(packed.reshape(experts, capacity, 2 * shard_width), 'ctx',...  22.9 us
    all_to_all x1, blocking collectives, local(): lax.all_to_all(slot_values.reshape(4, experts, capacity).transpose(1, 0,...  13 us
    all_to_all x1, waiting for transfers between devices, local(): lax.all_to_all(local_order(jnp.concatenate([out_rows, dx_rows, extra], ax...  10.5 us
    all_to_all x1, starting transfers between devices, local(): lax.all_to_all(packed.reshape(experts, capacity, 2 * shard_width), 'ctx',...  8.68 us
    all_to_all x1, starting transfers between devices, ctx_sum(): lax.all_to_all(spread, 'ctx', split_axis=0, concat_axis=0, tiled=True)  8.3 us
    unnamed x48, local copies, waits for them, and re-layouts  8.21 us
    dot_general x3, matrix products, contract_rows(): lax.dot_general(left, right, (((0,), (0,)), ((), ())), preferred_element_...  7.39 us
  transfers between devices with their start and end apart: 8, of which 6 were waited for; matrix products, arithmetic and copies ran while one was open for 11% of the time, Pallas kernels for 0%

profile of v14, /device:TPU:64, one launch (start us, length us, event | category | flops | bytes accessed | tf_op | source)
XLA Modules:
  0.0 289.8 jit_solution(5819853652630432198)
XLA Ops:
  7.2 0.9 copy.68
  8.4 1.2 reduce-window.6
  9.6 0.2 slice_reduce_fusion
  10.2 0.7 multiply_add_fusion.1
  10.9 0.3 fusion.10
  11.2 2.8 convolution_convert_fusion.6
  13.9 8.7 %all-to-all-start = ((bf16[32,24,1024]{2,1,0:T(8,128)(2,1)}), bf16[32,24,1024]{2,1,0:T(8,128)(2,1)S(1)}, u32[]{:S(2)}, u32[]{:S(2)}) async-start(bf16[32,24,1024]{2,1,0:T(8,128)(2,1)} %bitcast.124), calls=%async_computation | async-start | bytes 3145728 | tf_op jit(solution)/shard_map/all_to_all | solution.py:75
  22.7 22.9 %all-to-all-done = bf16[32,24,1024]{2,1,0:T(8,128)(2,1)S(1)} async-done(((bf16[32,24,1024]{2,1,0:T(8,128)(2,1)}), bf16[32,24,1024]{2,1,0:T(8,128)(2,1)S(1)}, u32[]{:S(2)}, u32[]{:S(2)}) %all-to-all-start) | async-done | bytes 1572896 | tf_op jit(solution)/shard_map/all_to_all | solution.py:75
  45.7 0.8 maximum_select_fusion.1
  46.6 0.5 copy-done.18
  47.1 1.4 fusion.2
  48.5 1.4 fusion.3
  50.0 1.4 fusion.1
  51.4 0.9 pad_maximum_fusion
  52.4 0.2 slice.200
  52.7 0.6 copy-done.14
  53.5 5.0 %collective-permute-done = bf16[3,384,1408]{2,1,0:T(8,128)(2,1)S(1)} collective-permute-done((bf16[3,384,1408]{2,1,0:T(8,128)(2,1)S(1)}, bf16[3,384,1408]{2,1,0:T(8,128)(2,1)S(1)}, u32[]{:S(2)}, u32[]{:S(2)}) %collective-permute-start) | collective-permute-done | bytes 3244064 | tf_op jit(solution)/shard_map/ppermute | solution.py:105
  58.5 2.6 add_convert_fusion
  61.2 0.6 broadcast_in_dim.14
  61.8 7.2 %all-to-all-start.1 = ((f32[8,256,2]{1,2,0:T(2,128)}), f32[8,256,2]{1,2,0:T(2,128)S(1)}, u32[]{:S(2)}, u32[]{:S(2)}) async-start(f32[8,256,2]{1,2,0:T(2,128)} %broadcast_in_dim.14), calls=%async_computation.1 | async-start | bytes 32768 | tf_op jit(solution)/shard_map/all_to_all | solution.py:39
  69.4 5.2 %all-to-all-done.1 = f32[8,256,2]{1,2,0:T(2,128)S(1)} async-done(((f32[8,256,2]{1,2,0:T(2,128)}), f32[8,256,2]{1,2,0:T(2,128)S(1)}, u32[]{:S(2)}, u32[]{:S(2)}) %all-to-all-start.1) | async-done | bytes 16416 | tf_op jit(solution)/shard_map/all_to_all | solution.py:39
  75.4 0.4 fusion.29
  76.0 13.0 %all_to_all.30 = bf16[32,4,24]{2,1,0:T(4,128)(2,1)S(1)} all-to-all(bf16[32,4,24]{2,1,0:T(4,128)(2,1)S(1)} %copy.74), channel_id=1, replica_groups=mesh['ctx'=32,'head'=8] {'ctx'}, dimensions={0} | all-to-all | bytes 12288 | tf_op jit(solution)/shard_map/all_to_all | solution.py:132
  89.4 106.9 %all-reduce.3.cloned.1.call-done = bf16[3,384,1408]{2,1,0:T(8,128)(2,1)} async-done(((bf16[3,384,1408]{2,1,0:T(8,128)(2,1)}), bf16[3,384,1408]{2,1,0:T(8,128)(2,1)}) %all-reduce.3.cloned.1.call-update) | async-done | bytes 3244048 | tf_op jit(solution)/shard_map/psum | solution.py:108
  196.3 0.6 compare_reduce_fusion.1
  196.9 0.6 compare_reduce_fusion
  197.6 2.3 convert_element_type.191
  200.2 2.8 multiply_convert_fusion.5
  203.0 2.3 convert_element_type.193
  205.5 2.8 multiply_convert_fusion.4
  208.3 1.4 fusion.23
  209.7 0.6 fusion
  210.3 0.8 copy-done.6
  211.1 1.2 fusion.38
  212.3 0.8 reshape.259
  213.1 7.1 %all-to-all-start.4 = ((f32[32,1,512]{2,1,0:T(1,128)}), f32[32,1,512]{2,1,0:T(1,128)S(1)}, u32[]{:S(2)}, u32[]{:S(2)}) async-start(f32[32,1,512]{2,1,0:T(1,128)} %reshape.259), calls=%async_computation.4 | async-start | bytes 131072 | tf_op jit(solution)/shard_map/all_to_all | solution.py:47
  220.1 1.6 fusion.48
  221.7 1.4 scatter.9
  223.2 3.5 %fusion.17 = f32[768,512]{1,0:T(8,128)S(1)} fusion(bf16[1,1408,512]{2,1,0:T(8,128)(2,1)} %param.16, bf16[384,1408]{1,0:T(8,128)(2,1)} %get-tuple-element.76, bf16[384,1408]{1,0:T(8,128)(2,1)} %get-tuple-element.74), kind=kOutput, calls=%fused_computation.53 | convolution fusion | flops 1111621632 | bytes 5177344 | tf_op jit(solution)/shard_map/dot_general | solution.py:156
  226.8 1.4 add_convert_fusion.1
  228.1 0.9 copy-done.4
  229.3 1.3 pad_maximum_fusion.5
  230.6 0.5 broadcast.199
  231.2 0.8 reduce.30
  232.1 0.8 reshape.261
  232.9 8.3 %all-to-all-start.5 = ((f32[32,1,512]{2,1,0:T(1,128)}), f32[32,1,512]{2,1,0:T(1,128)S(1)}, u32[]{:S(2)}, u32[]{:S(2)}) async-start(f32[32,1,512]{2,1,0:T(1,128)} %reshape.261), calls=%async_computation.5 | async-start | bytes 131072 | tf_op jit(solution)/shard_map/all_to_all | solution.py:49
  241.3 2.8 maximum_select_fusion
  244.1 5.7 %all-to-all-done.5 = f32[32,1,512]{2,1,0:T(1,128)S(1)} async-done(((f32[32,1,512]{2,1,0:T(1,128)}), f32[32,1,512]{2,1,0:T(1,128)S(1)}, u32[]{:S(2)}, u32[]{:S(2)}) %all-to-all-start.5) | async-done | bytes 65568 | tf_op jit(solution)/shard_map/all_to_all | solution.py:49
  249.7 4.9 %all-to-all-start.3 = ((bf16[32,24,1152]{2,1,0:T(8,128)(2,1)}), bf16[32,24,1152]{2,1,0:T(8,128)(2,1)}, u32[]{:S(2)}, u32[]{:S(2)}) async-start(bf16[32,24,1152]{2,1,0:T(8,128)(2,1)} %maximum_select_fusion), calls=%async_computation.3 | async-start | bytes 3538944 | tf_op jit(solution)/shard_map/all_to_all | solution.py:176
  254.7 0.3 iota_compare_fusion.1
  255.0 1.2 eq.120
  256.4 1.2 copy-done.7
  257.6 0.3 copy-done.10
  257.9 0.3 copy-done.13
  258.3 2.4 fusion.4
  260.7 2.4 fusion.5
  263.1 2.5 fusion.6
  265.7 0.8 reduce.31
  266.6 0.7 copy.82
  267.3 10.5 %all-to-all-done.3 = bf16[32,24,1152]{2,1,0:T(8,128)(2,1)} async-done(((bf16[32,24,1152]{2,1,0:T(8,128)(2,1)}), bf16[32,24,1152]{2,1,0:T(8,128)(2,1)}, u32[]{:S(2)}, u32[]{:S(2)}) %all-to-all-start.3) | async-done | bytes 1769504 | tf_op jit(solution)/shard_map/all_to_all | solution.py:176
  277.8 2.8 fusion.76
  280.6 0.2 fusion.46
  280.9 1.1 fusion.28
  282.1 0.9 multiply_reduce_fusion
  (96 shorter events, 4.1 us)
Async XLA Ops:
  7.2 41.4 %copy-start = (bf16[1,1408,512]{2,1,0:T(8,128)(2,1)S(1)}, bf16[1,1408,512]{2,1,0:T(8,128)(2,1)}, u32[]{:S(2)}) copy-start(bf16[1,1408,512]{2,1,0:T(8,128)(2,1)} %param.17) | copy-start | bytes 4325380
  13.9 31.7 %all-to-all-start = ((bf16[32,24,1024]{2,1,0:T(8,128)(2,1)}), bf16[32,24,1024]{2,1,0:T(8,128)(2,1)S(1)}, u32[]{:S(2)}, u32[]{:S(2)}) async-start(bf16[32,24,1024]{2,1,0:T(8,128)(2,1)} %bitcast.124), calls=%async_computation | async-start | bytes 3145728 | tf_op jit(solution)/shard_map/all_to_all | solution.py:75
  22.6 173.7 %all-reduce.3.cloned.1.call-start = ((), (), s32[]{:S(2)}) async-start(), calls=%async_computation.6 | async-start | bytes 6488064 | tf_op jit(solution)/shard_map/psum | solution.py:108
  45.7 1.4 copy-start.18
  47.1 2.9 copy-start.5
  48.5 1.5 copy-start.19
  52.3 1.0 copy-start.14
  52.4 0.9 copy-start.17
  52.4 1.1 copy-start.16
  52.6 5.9 %collective-permute-start = (bf16[3,384,1408]{2,1,0:T(8,128)(2,1)S(1)}, bf16[3,384,1408]{2,1,0:T(8,128)(2,1)S(1)}, u32[]{:S(2)}, u32[]{:S(2)}) collective-permute-start(bf16[3,384,1408]{2,1,0:T(8,128)(2,1)S(1)} %slice.200), channel_id=1, source_target_pairs={{0,1},{1,0},{2,3},{3,2},{4,5},{5,4},{6,7},{7,6},{8,9},{9,8},{10,11... | collective-permute-start | bytes 9732104 | tf_op jit(solution)/shard_map/ppermute | solution.py:105
  61.8 12.7 %all-to-all-start.1 = ((f32[8,256,2]{1,2,0:T(2,128)}), f32[8,256,2]{1,2,0:T(2,128)S(1)}, u32[]{:S(2)}, u32[]{:S(2)}) async-start(f32[8,256,2]{1,2,0:T(2,128)} %broadcast_in_dim.14), calls=%async_computation.1 | async-start | bytes 32768 | tf_op jit(solution)/shard_map/all_to_all | solution.py:39
  196.3 6.7 %collective-permute-start.1 = (bf16[3,384,1408]{2,1,0:T(8,128)(2,1)}, bf16[3,384,1408]{2,1,0:T(8,128)(2,1)}, u32[]{:S(2)}, u32[]{:S(2)}) collective-permute-start(bf16[3,384,1408]{2,1,0:T(8,128)(2,1)} %all-reduce.3.cloned.1.call-done), channel_id=1, source_target_pairs={{0,1},{1,0},{2,3},{3,2},{4,5},{5,4},{6,7},{7,6},{8,9},{9,8},{10,11... | collective-permute-start | bytes 9732104 | tf_op jit(solution)/shard_map/ppermute | solution.py:143
  208.3 1.4 copy-start.2
  209.7 1.4 copy-start.6
  213.1 17.6 %all-to-all-start.4 = ((f32[32,1,512]{2,1,0:T(1,128)}), f32[32,1,512]{2,1,0:T(1,128)S(1)}, u32[]{:S(2)}, u32[]{:S(2)}) async-start(f32[32,1,512]{2,1,0:T(1,128)} %reshape.259), calls=%async_computation.4 | async-start | bytes 131072 | tf_op jit(solution)/shard_map/all_to_all | solution.py:47
  223.2 3.6 %copy-start.9 = (bf16[384,1408]{1,0:T(8,128)(2,1)S(1)}, bf16[384,1408]{1,0:T(8,128)(2,1)}, u32[]{:S(2)}) copy-start(bf16[384,1408]{1,0:T(8,128)(2,1)} %get-tuple-element.73) | copy-start | bytes 3244036
  223.2 3.6 %copy-start.12 = (bf16[384,1408]{1,0:T(8,128)(2,1)S(1)}, bf16[384,1408]{1,0:T(8,128)(2,1)}, u32[]{:S(2)}) copy-start(bf16[384,1408]{1,0:T(8,128)(2,1)} %get-tuple-element.75) | copy-start | bytes 3244036
  223.2 3.6 %copy-start.20 = (bf16[1,1408,512]{2,1,0:T(8,128)(2,1)S(1)}, bf16[1,1408,512]{2,1,0:T(8,128)(2,1)}, u32[]{:S(2)}) copy-start(bf16[1,1408,512]{2,1,0:T(8,128)(2,1)} %param.15) | copy-start | bytes 4325380
  228.1 0.9 copy-start.4
  232.9 16.8 %all-to-all-start.5 = ((f32[32,1,512]{2,1,0:T(1,128)}), f32[32,1,512]{2,1,0:T(1,128)S(1)}, u32[]{:S(2)}, u32[]{:S(2)}) async-start(f32[32,1,512]{2,1,0:T(1,128)} %reshape.261), calls=%async_computation.5 | async-start | bytes 131072 | tf_op jit(solution)/shard_map/all_to_all | solution.py:49
  244.1 12.2 %copy-start.3 = (bf16[384,1408]{1,0:T(8,128)(2,1)S(1)}, bf16[384,1408]{1,0:T(8,128)(2,1)}, u32[]{:S(2)}) copy-start(bf16[384,1408]{1,0:T(8,128)(2,1)} %copy-done.2) | copy-start | bytes 3244036
  249.7 28.1 %all-to-all-start.3 = ((bf16[32,24,1152]{2,1,0:T(8,128)(2,1)}), bf16[32,24,1152]{2,1,0:T(8,128)(2,1)}, u32[]{:S(2)}, u32[]{:S(2)}) async-start(bf16[32,24,1152]{2,1,0:T(8,128)(2,1)} %maximum_select_fusion), calls=%async_computation.3 | async-start | bytes 3538944 | tf_op jit(solution)/shard_map/all_to_all | solution.py:176
  256.2 1.4 copy-start.7
  256.2 1.7 copy-start.10
  256.2 2.0 copy-start.13
  258.3 2.4 copy-start.8
  258.3 2.4 copy-start.11
  263.1 14.7 %copy-start.15 = (pred[256,2,768]{2,1,0:T(4,128)(4,1)S(1)}, pred[256,2,768]{2,1,0:T(4,128)(4,1)}, u32[]{:S(2)}) copy-start(pred[256,2,768]{2,1,0:T(4,128)(4,1)} %eq.120) | copy-start | bytes 1179652
  277.8 5.1 %copy-start.1 = (bf16[1,1408,512]{2,1,0:T(8,128)(2,1)S(1)}, bf16[1,1408,512]{2,1,0:T(8,128)(2,1)}, u32[]{:S(2)}) copy-start(bf16[1,1408,512]{2,1,0:T(8,128)(2,1)} %param.17) | copy-start | bytes 4325380
Sparse Core Ops, SparseCore 0:
  61.2 135.0 all-reduce.2

commit v15 on v13

--- a/solution.py
+++ b/solution.py
@@ -152,8 +152,7 @@
         jnp.dot(gate_grad, gate_w, preferred_element_type=jnp.float32)
         + jnp.dot(up_grad, up_w, preferred_element_type=jnp.float32)
     ).astype(jnp.bfloat16)
-    hidden_kept = lax.optimization_barrier(hidden)
-    scaled = (prob_rows[:, None] * hidden_kept.astype(jnp.float32)).astype(jnp.bfloat16)
+    scaled = (prob_rows[:, None] * hidden.astype(jnp.float32)).astype(jnp.bfloat16)
     grad_down = contract_rows(scaled, cot_rows).astype(jnp.bfloat16)[None]
     grad_gate = contract_rows(gate_grad, x_rows).astype(jnp.bfloat16)[None]
     grad_up = contract_rows(up_grad, x_rows).astype(jnp.bfloat16)[None]

time: 292 us -> 291 us (level)
    unnamed x46 -> x50, local copies, waits for them, and re-layouts: 7.36 us -> 6.73 us
  transfers between devices with their start and end apart: 8 -> 8, of which waited for: 6 -> 6; matrix products, arithmetic and copies ran while one was open for 11% -> 12% of each run, Pallas kernels for 0% -> 0%
where the time goes in v15:
time: 291 us; the launch traced here: 288 us
  waiting for transfers between devices  155 us (53%)
  starting transfers between devices  35.6 us (12%)
  other arithmetic  28.4 us (10%)
  matrix products  27.2 us (9%)
  between operations  14.7 us (5%)
  local copies, waits for them, and re-layouts  13.7 us (5%)
  blocking collectives  13.1 us (5%)
    psum x1, waiting for transfers between devices, local(): mine = lax.psum(pair_sum, 'head', axis_index_groups=same_core)  106 us
    all_to_all x1, waiting for transfers between devices, local(): lax.all_to_all(packed.reshape(experts, capacity, 2 * shard_width), 'ctx',...  22.9 us
    all_to_all x1, blocking collectives, local(): lax.all_to_all(slot_values.reshape(4, experts, capacity).transpose(1, 0,...  13.1 us
    all_to_all x1, waiting for transfers between devices, local(): lax.all_to_all(local_order(jnp.concatenate([out_rows, dx_rows, extra], ax...  10.6 us
    dot_general x3, matrix products, contract_rows(): lax.dot_general(left, right, (((0,), (0,)), ((), ())), preferred_element_...  9.31 us
    all_to_all x1, starting transfers between devices, local(): lax.all_to_all(packed.reshape(experts, capacity, 2 * shard_width), 'ctx',...  8.68 us
    all_to_all x1, starting transfers between devices, ctx_sum(): lax.all_to_all(spread, 'ctx', split_axis=0, concat_axis=0, tiled=True)  8.3 us
    all_to_all x1, starting transfers between devices, head_sum(): lax.all_to_all(spread, 'head', split_axis=0, concat_axis=0, tiled=True)  7.22 us
  transfers between devices with their start and end apart: 8, of which 6 were waited for; matrix products, arithmetic and copies ran while one was open for 12% of the time, Pallas kernels for 0%

profile of v15, /device:TPU:64, one launch (start us, length us, event | category | flops | bytes accessed | tf_op | source)
XLA Modules:
  0.0 288.0 jit_solution(16676614235848047045)
XLA Ops:
  7.2 0.9 copy.83
  8.4 1.2 reduce-window.6
  9.6 0.2 slice_reduce_fusion
  10.2 0.7 multiply_add_fusion.1
  10.9 0.3 fusion.12
  11.2 2.8 convolution_convert_fusion.6
  13.9 8.7 %all-to-all-start = ((bf16[32,24,1024]{2,1,0:T(8,128)(2,1)}), bf16[32,24,1024]{2,1,0:T(8,128)(2,1)S(1)}, u32[]{:S(2)}, u32[]{:S(2)}) async-start(bf16[32,24,1024]{2,1,0:T(8,128)(2,1)} %bitcast.124), calls=%async_computation | async-start | bytes 3145728 | tf_op jit(solution)/shard_map/all_to_all | solution.py:75
  22.7 22.9 %all-to-all-done = bf16[32,24,1024]{2,1,0:T(8,128)(2,1)S(1)} async-done(((bf16[32,24,1024]{2,1,0:T(8,128)(2,1)}), bf16[32,24,1024]{2,1,0:T(8,128)(2,1)S(1)}, u32[]{:S(2)}, u32[]{:S(2)}) %all-to-all-start) | async-done | bytes 1572896 | tf_op jit(solution)/shard_map/all_to_all | solution.py:75
  45.7 0.8 maximum_select_fusion.1
  46.6 0.5 copy-done.19
  47.1 1.4 fusion.3
  48.5 1.4 fusion.4
  50.0 1.4 fusion.2
  51.4 0.9 pad_maximum_fusion
  52.4 0.2 slice.200
  52.7 0.6 copy-done.16
  53.3 0.2 fusion.70
  53.5 5.0 %collective-permute-done = bf16[3,384,1408]{2,1,0:T(8,128)(2,1)S(1)} collective-permute-done((bf16[3,384,1408]{2,1,0:T(8,128)(2,1)S(1)}, bf16[3,384,1408]{2,1,0:T(8,128)(2,1)S(1)}, u32[]{:S(2)}, u32[]{:S(2)}) %collective-permute-start) | collective-permute-done | bytes 3244064 | tf_op jit(solution)/shard_map/ppermute | solution.py:105
  58.5 2.6 add_convert_fusion
  61.1 0.6 broadcast_in_dim.34
  61.7 7.2 %all-to-all-start.1 = ((f32[8,256,2]{1,2,0:T(2,128)}), f32[8,256,2]{1,2,0:T(2,128)S(1)}, u32[]{:S(2)}, u32[]{:S(2)}) async-start(f32[8,256,2]{1,2,0:T(2,128)} %broadcast_in_dim.34), calls=%async_computation.1 | async-start | bytes 32768 | tf_op jit(solution)/shard_map/all_to_all | solution.py:39
  69.0 0.3 iota_compare_fusion
  69.6 4.8 %all-to-all-done.1 = f32[8,256,2]{1,2,0:T(2,128)S(1)} async-done(((f32[8,256,2]{1,2,0:T(2,128)}), f32[8,256,2]{1,2,0:T(2,128)S(1)}, u32[]{:S(2)}, u32[]{:S(2)}) %all-to-all-start.1) | async-done | bytes 16416 | tf_op jit(solution)/shard_map/all_to_all | solution.py:39
  74.6 0.1 stack_reshape.10
  74.9 0.1 stack_reshape.11
  75.3 1.0 select_reduce_fusion
  76.4 13.1 %all_to_all.30 = bf16[32,4,24]{2,1,0:T(4,128)(2,1)S(1)} all-to-all(bf16[32,4,24]{2,1,0:T(4,128)(2,1)S(1)} %copy.89), channel_id=1, replica_groups=mesh['ctx'=32,'head'=8] {'ctx'}, dimensions={0} | all-to-all | bytes 12288 | tf_op jit(solution)/shard_map/all_to_all | solution.py:129
  89.9 106.4 %all-reduce.3.cloned.1.call-done = bf16[3,384,1408]{2,1,0:T(8,128)(2,1)} async-done(((bf16[3,384,1408]{2,1,0:T(8,128)(2,1)}), bf16[3,384,1408]{2,1,0:T(8,128)(2,1)}) %all-reduce.3.cloned.1.call-update) | async-done | bytes 3244048 | tf_op jit(solution)/shard_map/psum | solution.py:108
  196.3 0.6 compare_reduce_fusion.1
  197.0 0.6 compare_reduce_fusion
  197.6 2.3 convert_element_type.192
  200.2 2.5 multiply_convert_fusion.3
  202.6 3.1 %convert_element_type.194 = f32[3,384,1408]{2,1,0:T(8,128)S(1)} convert(bf16[3,384,1408]{2,1,0:T(8,128)(2,1)} %collective-permute-done.1) | non-fusion elementwise | flops 1622016 | bytes 9732096 | tf_op jit(solution)/shard_map/convert_element_type | solution.py:140
  205.9 2.8 multiply_convert_fusion.2
  208.7 1.4 fusion.24
  210.2 0.5 fusion
  210.7 1.2 copy-done.9
  211.8 1.2 fusion.37
  213.0 0.8 reshape.278
  213.8 7.0 %all-to-all-start.4 = ((f32[32,1,512]{2,1,0:T(1,128)}), f32[32,1,512]{2,1,0:T(1,128)S(1)}, u32[]{:S(2)}, u32[]{:S(2)}) async-start(f32[32,1,512]{2,1,0:T(1,128)} %reshape.278), calls=%async_computation.4 | async-start | bytes 131072 | tf_op jit(solution)/shard_map/all_to_all | solution.py:47
  220.9 1.6 fusion.47
  222.5 1.4 scatter.9
  223.9 3.2 %fusion.18 = f32[768,512]{1,0:T(8,128)S(1)} fusion(bf16[1,1408,512]{2,1,0:T(8,128)(2,1)} %param.16, bf16[384,1408]{1,0:T(8,128)(2,1)} %get-tuple-element.80, bf16[384,1408]{1,0:T(8,128)(2,1)S(1)} %get-tuple-element.78), kind=kOutput, calls=%fused_computation.54 | convolution fusion | flops 1111621632 | bytes 5177344 | tf_op jit(solution)/shard_map/dot_general | solution.py:153
  227.2 1.4 add_convert_fusion.1
  228.6 0.9 copy-done.7
  229.9 0.5 broadcast.211
  230.4 0.8 reduce.30
  231.4 0.8 reshape.280
  232.2 8.3 %all-to-all-start.5 = ((f32[32,1,512]{2,1,0:T(1,128)}), f32[32,1,512]{2,1,0:T(1,128)S(1)}, u32[]{:S(2)}, u32[]{:S(2)}) async-start(f32[32,1,512]{2,1,0:T(1,128)} %reshape.280), calls=%async_computation.5 | async-start | bytes 131072 | tf_op jit(solution)/shard_map/all_to_all | solution.py:49
  240.5 3.0 %maximum_select_fusion = bf16[32,24,1152]{2,1,0:T(8,128)(2,1)} fusion(bf16[32,24,1152]{2,1,0:T(8,128)(2,1)S(1)} %bitcast.123, bf16[32,24,128]{2,1,0:T(8,128)(2,1)S(1)} %bitcast.129, bf16[32,24,512]{2,1,0:T(8,128)(2,1)} %bitcast.128, bf16[32,24,512]{2,1,0:T(8,128)(2,1)} %bitcast.127, pred[]{:T(512)S(6)} %eq.106), kind=kLoop, calls=%fused_computation.41 | loop fusion | flops 6193152 | bytes 5308417 | tf_op jit(solution)/shard_map/jit(_where)/select_n | solution.py:88
  243.5 5.4 %all-to-all-done.5 = f32[32,1,512]{2,1,0:T(1,128)S(1)} async-done(((f32[32,1,512]{2,1,0:T(1,128)}), f32[32,1,512]{2,1,0:T(1,128)S(1)}, u32[]{:S(2)}, u32[]{:S(2)}) %all-to-all-start.5) | async-done | bytes 65568 | tf_op jit(solution)/shard_map/all_to_all | solution.py:49
  249.0 4.2 %all-to-all-start.3 = ((bf16[32,24,1152]{2,1,0:T(8,128)(2,1)}), bf16[32,24,1152]{2,1,0:T(8,128)(2,1)S(1)}, u32[]{:S(2)}, u32[]{:S(2)}) async-start(bf16[32,24,1152]{2,1,0:T(8,128)(2,1)} %maximum_select_fusion), calls=%async_computation.3 | async-start | bytes 3538944 | tf_op jit(solution)/shard_map/all_to_all | solution.py:172
  253.2 0.3 iota_compare_fusion.1
  253.5 1.2 eq.124
  254.7 4.4 %fusion.5 = bf16[1,1408,512]{2,1,0:T(8,128)(2,1)} fusion(bf16[384,1408]{1,0:T(8,128)(2,1)} %get-tuple-element.79, bf16[384,1408]{1,0:T(8,128)(2,1)} %get-tuple-element.77, bf16[768,1024]{1,0:T(8,128)(2,1)} %copy-done.8), kind=kOutput, calls=%fused_computation.16 | convolution fusion | flops 1112342528 | bytes 4390912 | tf_op jit(solution)/shard_map/dot_general | solution.py:8
  259.1 2.4 fusion.6
  261.5 2.5 fusion.7
  264.1 0.8 reduce.31
  265.0 0.7 copy.97
  265.7 10.6 %all-to-all-done.3 = bf16[32,24,1152]{2,1,0:T(8,128)(2,1)S(1)} async-done(((bf16[32,24,1152]{2,1,0:T(8,128)(2,1)}), bf16[32,24,1152]{2,1,0:T(8,128)(2,1)S(1)}, u32[]{:S(2)}, u32[]{:S(2)}) %all-to-all-start.3) | async-done | bytes 1769504 | tf_op jit(solution)/shard_map/all_to_all | solution.py:172
  276.4 2.4 fusion.69
  278.8 0.2 fusion.45
  279.1 0.9 multiply_reduce_fusion
  280.0 1.1 fusion.29
  (98 shorter events, 3.6 us)
Async XLA Ops:
  7.2 41.4 %copy-start = (bf16[1,1408,512]{2,1,0:T(8,128)(2,1)S(1)}, bf16[1,1408,512]{2,1,0:T(8,128)(2,1)}, u32[]{:S(2)}) copy-start(bf16[1,1408,512]{2,1,0:T(8,128)(2,1)} %param.17) | copy-start | bytes 4325380
  13.9 31.7 %all-to-all-start = ((bf16[32,24,1024]{2,1,0:T(8,128)(2,1)}), bf16[32,24,1024]{2,1,0:T(8,128)(2,1)S(1)}, u32[]{:S(2)}, u32[]{:S(2)}) async-start(bf16[32,24,1024]{2,1,0:T(8,128)(2,1)} %bitcast.124), calls=%async_computation | async-start | bytes 3145728 | tf_op jit(solution)/shard_map/all_to_all | solution.py:75
  22.6 173.7 %all-reduce.3.cloned.1.call-start = ((), (), s32[]{:S(2)}) async-start(), calls=%async_computation.6 | async-start | bytes 6488064 | tf_op jit(solution)/shard_map/psum | solution.py:108
  45.7 1.4 copy-start.19
  47.1 2.9 %copy-start.8 = (bf16[768,1024]{1,0:T(8,128)(2,1)}, bf16[768,1024]{1,0:T(8,128)(2,1)S(1)}, u32[]{:S(2)}) copy-start(bf16[768,1024]{1,0:T(8,128)(2,1)S(1)} %maximum_select_fusion.1) | copy-start | bytes 4718596
  48.5 1.5 copy-start.20
  52.3 1.0 copy-start.16
  52.4 0.9 copy-start.18
  52.4 1.1 copy-start.17
  52.6 5.9 %collective-permute-start = (bf16[3,384,1408]{2,1,0:T(8,128)(2,1)S(1)}, bf16[3,384,1408]{2,1,0:T(8,128)(2,1)S(1)}, u32[]{:S(2)}, u32[]{:S(2)}) collective-permute-start(bf16[3,384,1408]{2,1,0:T(8,128)(2,1)S(1)} %slice.200), channel_id=1, source_target_pairs={{0,1},{1,0},{2,3},{3,2},{4,5},{5,4},{6,7},{7,6},{8,9},{9,8},{10,11... | collective-permute-start | bytes 9732104 | tf_op jit(solution)/shard_map/ppermute | solution.py:105
  61.7 12.7 %all-to-all-start.1 = ((f32[8,256,2]{1,2,0:T(2,128)}), f32[8,256,2]{1,2,0:T(2,128)S(1)}, u32[]{:S(2)}, u32[]{:S(2)}) async-start(f32[8,256,2]{1,2,0:T(2,128)} %broadcast_in_dim.34), calls=%async_computation.1 | async-start | bytes 32768 | tf_op jit(solution)/shard_map/all_to_all | solution.py:39
  196.3 6.3 %collective-permute-start.1 = (bf16[3,384,1408]{2,1,0:T(8,128)(2,1)}, bf16[3,384,1408]{2,1,0:T(8,128)(2,1)}, u32[]{:S(2)}, u32[]{:S(2)}) collective-permute-start(bf16[3,384,1408]{2,1,0:T(8,128)(2,1)} %all-reduce.3.cloned.1.call-done), channel_id=1, source_target_pairs={{0,1},{1,0},{2,3},{3,2},{4,5},{5,4},{6,7},{7,6},{8,9},{9,8},{10,11... | collective-permute-start | bytes 9732104 | tf_op jit(solution)/shard_map/ppermute | solution.py:140
  202.6 7.5 %copy-start.2 = (bf16[384,1408]{1,0:T(8,128)(2,1)}, bf16[384,1408]{1,0:T(8,128)(2,1)S(1)}, u32[]{:S(2)}) copy-start(bf16[384,1408]{1,0:T(8,128)(2,1)S(1)} %get-tuple-element.81) | copy-start | bytes 3244036
  202.6 21.3 %copy-start.11 = (bf16[384,1408]{1,0:T(8,128)(2,1)}, bf16[384,1408]{1,0:T(8,128)(2,1)S(1)}, u32[]{:S(2)}) copy-start(bf16[384,1408]{1,0:T(8,128)(2,1)S(1)} %get-tuple-element.78) | copy-start | bytes 3244036
  208.7 1.4 copy-start.4
  210.1 18.4 %copy-start.6 = (bf16[768,512]{1,0:T(8,128)(2,1)}, bf16[768,512]{1,0:T(8,128)(2,1)S(1)}, u32[]{:S(2)}) copy-start(bf16[768,512]{1,0:T(8,128)(2,1)S(1)} %fusion.24) | copy-start | bytes 2359300
  210.1 1.7 copy-start.9
  213.8 16.1 %all-to-all-start.4 = ((f32[32,1,512]{2,1,0:T(1,128)}), f32[32,1,512]{2,1,0:T(1,128)S(1)}, u32[]{:S(2)}, u32[]{:S(2)}) async-start(f32[32,1,512]{2,1,0:T(1,128)} %reshape.278), calls=%async_computation.4 | async-start | bytes 131072 | tf_op jit(solution)/shard_map/all_to_all | solution.py:47
  223.9 3.2 %copy-start.13 = (bf16[384,1408]{1,0:T(8,128)(2,1)S(1)}, bf16[384,1408]{1,0:T(8,128)(2,1)}, u32[]{:S(2)}) copy-start(bf16[384,1408]{1,0:T(8,128)(2,1)} %get-tuple-element.77) | copy-start | bytes 3244036
  223.9 3.2 %copy-start.15 = (bf16[384,1408]{1,0:T(8,128)(2,1)S(1)}, bf16[384,1408]{1,0:T(8,128)(2,1)}, u32[]{:S(2)}) copy-start(bf16[384,1408]{1,0:T(8,128)(2,1)} %get-tuple-element.79) | copy-start | bytes 3244036
  223.9 3.2 %copy-start.21 = (bf16[1,1408,512]{2,1,0:T(8,128)(2,1)S(1)}, bf16[1,1408,512]{2,1,0:T(8,128)(2,1)}, u32[]{:S(2)}) copy-start(bf16[1,1408,512]{2,1,0:T(8,128)(2,1)} %param.15) | copy-start | bytes 4325380
  228.6 0.9 copy-start.7
  232.2 16.8 %all-to-all-start.5 = ((f32[32,1,512]{2,1,0:T(1,128)}), f32[32,1,512]{2,1,0:T(1,128)S(1)}, u32[]{:S(2)}, u32[]{:S(2)}) async-start(f32[32,1,512]{2,1,0:T(1,128)} %reshape.280), calls=%async_computation.5 | async-start | bytes 131072 | tf_op jit(solution)/shard_map/all_to_all | solution.py:49
  249.0 27.4 %all-to-all-start.3 = ((bf16[32,24,1152]{2,1,0:T(8,128)(2,1)}), bf16[32,24,1152]{2,1,0:T(8,128)(2,1)S(1)}, u32[]{:S(2)}, u32[]{:S(2)}) async-start(bf16[32,24,1152]{2,1,0:T(8,128)(2,1)} %maximum_select_fusion), calls=%async_computation.3 | async-start | bytes 3538944 | tf_op jit(solution)/shard_map/all_to_all | solution.py:172
  254.7 4.4 %copy-start.10 = (bf16[768,1024]{1,0:T(8,128)(2,1)S(1)}, bf16[768,1024]{1,0:T(8,128)(2,1)}, u32[]{:S(2)}) copy-start(bf16[768,1024]{1,0:T(8,128)(2,1)} %copy-done.8) | copy-start | bytes 4718596
  254.7 4.4 %copy-start.12 = (bf16[384,1408]{1,0:T(8,128)(2,1)S(1)}, bf16[384,1408]{1,0:T(8,128)(2,1)}, u32[]{:S(2)}) copy-start(bf16[384,1408]{1,0:T(8,128)(2,1)} %copy-done.11) | copy-start | bytes 3244036
  254.7 4.4 %copy-start.14 = (bf16[384,1408]{1,0:T(8,128)(2,1)S(1)}, bf16[384,1408]{1,0:T(8,128)(2,1)}, u32[]{:S(2)}) copy-start(bf16[384,1408]{1,0:T(8,128)(2,1)} %get-tuple-element.80) | copy-start | bytes 3244036
  259.1 2.4 copy-start.3
  259.1 2.4 copy-start.5
  276.4 4.8 %copy-start.1 = (bf16[1,1408,512]{2,1,0:T(8,128)(2,1)S(1)}, bf16[1,1408,512]{2,1,0:T(8,128)(2,1)}, u32[]{:S(2)}) copy-start(bf16[1,1408,512]{2,1,0:T(8,128)(2,1)} %param.17) | copy-start | bytes 4325380
Sparse Core Ops, SparseCore 0:
  61.2 135.0 all-reduce.2
